TPU v7x, 256 devices: a whole 4x4x8 slice. The times are simulated.
256 devices in a mesh: sample: 32 (over z, y_hi, core), tensor: 8 (over y_lo, x).
Axes of the slice: x: 4, y: 4 (y_hi: 2, y_lo: 2; y = y_hi * 2 + y_lo), z: 8, core: 2. Of those that a mesh axis runs over, the one named last changes fastest.
Arguments:
- hidden: bfloat16 [8192, 14336], P('sample', 'tensor'), may hold values from -6 to 6
- down_weight: bfloat16 [4096, 14336], P('sample', 'tensor'), may hold values from -0.046875 to 0.046875
- cotangent: bfloat16 [8192, 4096], P('sample'), may hold values from -6 to 6
- scores: int32 [128], P('sample'), may hold values from 0 to 38654
- prompt_ids: int32 [128], P('sample'), may hold values from 0 to 3, as said below
Outputs:
- layer_out: bfloat16 [8192, 4096], P('sample', 'tensor')
- hidden_grad: bfloat16 [8192, 14336], P('sample', 'tensor')
- weight_grad: bfloat16 [4096, 14336], P('sample', 'tensor')
Inputs may be any that keep to these rules, and one draw needn't show every extreme that they name: `prompt_ids`: each prompt id names exactly 32 responses.
All inputs are finite; a program needn't handle non-finite values.
Results may differ from a plain program's by a relative error of at most 0.015.
Values may be sent and summed in bfloat16 or wider, within the bound.
No kernel may reach another device: no remote copies, remote signals or barrier semaphores. Data moves between devices by JAX's collectives and lax.ppermute only.
A program may use at most 128 MiB of HBM per device.

v0:
```python
import math

import jax
import jax.numpy as jnp
from jax import lax
from jax.sharding import PartitionSpec as P

GROUP = 32


def shards(hidden, down_weight, cotangent, scores, prompt_ids):
    samples_here = scores.shape[0]
    prompts = samples_here * lax.axis_size("sample") // GROUP
    rewards = scores.astype(jnp.float32) / 64.0
    onehot = prompt_ids[:, None] == jnp.arange(prompts, dtype=jnp.int32)[None, :]
    local_peak = jnp.max(jnp.where(onehot, rewards[:, None], jnp.float32(-1e30)), axis=0)
    peak = lax.pmax(local_peak, "sample")
    shifted = jnp.where(onehot, jnp.exp(rewards[:, None] - peak[None, :]), 0.0)
    total = lax.psum(jnp.sum(shifted, axis=0), "sample")
    log_norm = peak + jnp.log(total)
    sample_norm = jnp.sum(jnp.where(onehot, log_norm[None, :], 0.0), axis=1)
    tokens_here = hidden.shape[0]
    token_weight = jnp.repeat(GROUP * jnp.exp(rewards - sample_norm), tokens_here // samples_here)
    weighted = (cotangent.astype(jnp.float32) * token_weight[:, None]).astype(jnp.bfloat16)
    gathered = lax.all_gather(down_weight, "sample", axis=0, tiled=True)
    partial_value = lax.dot_general(
        hidden, gathered, (((1,), (1,)), ((), ())), preferred_element_type=jnp.float32
    )
    hidden_grad = jnp.dot(weighted, gathered, preferred_element_type=jnp.float32).astype(
        jnp.bfloat16
    )
    layer_out = lax.psum_scatter(
        partial_value.astype(jnp.bfloat16), "tensor", scatter_dimension=1, tiled=True
    )
    scale = 1.0 / math.sqrt(tokens_here * lax.axis_size("sample"))
    weight_grad = lax.psum_scatter(
        (
            lax.dot_general(
                weighted, hidden, (((0,), (0,)), ((), ())), preferred_element_type=jnp.float32
            )
            * scale
        ).astype(jnp.bfloat16),
        "sample",
        scatter_dimension=0,
        tiled=True,
    )
    return (layer_out, hidden_grad, weight_grad)


def solution(mesh):
    return jax.shard_map(
        shards,
        mesh=mesh,
        in_specs=(
            P("sample", "tensor"),
            P("sample", "tensor"),
            P("sample", None),
            P("sample"),
            P("sample"),
        ),
        out_specs=(P("sample", "tensor"), P("sample", "tensor"), P("sample", "tensor")),
        check_vma=False,
    )
```

profile of v0, /device:TPU:32, one launch (start us, length us, event | category | flops | bytes accessed | tf_op | source)
XLA Modules:
  0.0 393.9 jit_solution(11148836205205911618)
XLA Ops:
  7.2 0.0 copy-start
  7.2 0.0 all-gather.2.cloned.1.call-start
  7.2 0.7 all-gather.2.cloned.1.call-update
  7.9 0.0 reduce-scatter.5.cloned.1.call-start
  8.0 0.7 convert_multiply_fusion
  8.6 0.7 select_reduce_fusion.2
  9.4 64.6 %pmax.7 = f32[4]{0:T(128)S(1)} all-reduce(f32[4]{0:T(128)S(1)} %select_reduce_fusion.2), channel_id=1, replica_groups=mesh['sample'=32,'tensor'=8] {'sample'}, use_global_device_ids=true, to_apply=%region_2.3 | all-reduce | flops 4 | bytes 32 | tf_op jit(solution)/shard_map/pmax | solution.py:17
  74.0 0.7 select_reduce_fusion.1
  74.7 66.5 %psum.7 = f32[4]{0:T(128)S(1)} all-reduce(f32[4]{0:T(128)S(1)} %select_reduce_fusion.1), channel_id=1, replica_groups=mesh['sample'=32,'tensor'=8] {'sample'}, use_global_device_ids=true, to_apply=%region_4.5 | all-reduce | flops 4 | bytes 32 | tf_op jit(solution)/shard_map/psum | solution.py:19
  141.2 0.8 select_reduce_fusion
  142.1 0.7 exponential_multiply_fusion
  142.7 0.1 broadcast_in_dim.39
  142.8 0.1 mul.20
  142.9 0.0 copy-done
  142.9 9.7 %multiply_convert_fusion = bf16[4096,1792]{1,0:T(8,128)(2,1)} fusion(bf16[256,1792]{1,0:T(8,128)(2,1)S(1)} %copy-done, bf16[256,4096]{1,0:T(8,128)(2,1)} %param.7, f32[256]{0:T(256)S(1)} %mul.20), kind=kOutput, calls=%fused_computation | convolution fusion | flops 3775922176 | bytes 17695744 | tf_op jit(solution)/shard_map/dot_general | solution.py:38
  152.5 0.0 reduce-scatter.5.cloned.1.call-update
  152.6 0.0 copy-start.1
  152.6 0.0 reduce-scatter.3.cloned.1.call-start
  152.6 0.0 all-gather.2.cloned.1.call-done
  152.6 16.0 %convolution_convert_fusion = bf16[256,4096]{1,0:T(8,128)(2,1)} fusion(bf16[256,1792]{1,0:T(8,128)(2,1)S(1)} %copy-done, bf16[4096,1792]{1,0:T(8,128)(2,1)} %all-gather.2.cloned.1.call-done), kind=kOutput, calls=%fused_computation.1 | convolution fusion | flops 3759144960 | bytes 17694720 | tf_op jit(solution)/shard_map/dot_general | solution.py:26
  168.6 0.0 reduce-scatter.3.cloned.1.call-update
  168.6 0.0 copy-done.1
  168.6 9.5 %convolution_convert_fusion.1 = bf16[256,1792]{1,0:T(8,128)(2,1)} fusion(bf16[4096,1792]{1,0:T(8,128)(2,1)} %all-gather.2.cloned.1.call-done, bf16[256,4096]{1,0:T(8,128)(2,1)S(1)} %copy-done.1, f32[256]{0:T(256)S(1)} %mul.20), kind=kOutput, calls=%fused_computation.3 | convolution fusion | flops 3761700864 | bytes 17695744 | tf_op jit(solution)/shard_map/dot_general | solution.py:29
  178.2 161.3 %reduce-scatter.5.cloned.1.call-done = bf16[128,1792]{1,0:T(8,128)(2,1)} async-done(((bf16[4096,1792]{1,0:T(8,128)(2,1)}), bf16[128,1792]{1,0:T(8,128)(2,1)}) %reduce-scatter.5.cloned.1.call-update) | async-done | bytes 458768 | tf_op jit(solution)/shard_map/reduce_scatter | solution.py:36
  339.5 47.9 %reduce-scatter.3.cloned.1.call-done = bf16[256,512]{1,0:T(8,128)(2,1)} async-done(((bf16[256,4096]{1,0:T(8,128)(2,1)}), bf16[256,512]{1,0:T(8,128)(2,1)}) %reduce-scatter.3.cloned.1.call-update) | async-done | bytes 262160 | tf_op jit(solution)/shard_map/reduce_scatter | solution.py:32
  (1 shorter events, 0.0 us)
Async XLA Ops:
  7.2 135.7 %copy-start = (bf16[256,1792]{1,0:T(8,128)(2,1)S(1)}, bf16[256,1792]{1,0:T(8,128)(2,1)}, u32[]{:S(2)}) copy-start(bf16[256,1792]{1,0:T(8,128)(2,1)} %param.5) | copy-start | bytes 2752516
  7.2 145.5 %all-gather.2.cloned.1.call-start = ((), (), s32[]{:S(2)}) async-start(), calls=%async_computation.2 | async-start | bytes 15138816 | tf_op jit(solution)/shard_map/all_gather | solution.py:25
  7.9 331.6 %reduce-scatter.5.cloned.1.call-start = ((), (), s32[]{:S(2)}) async-start(), calls=%async_computation.4 | async-start | bytes 15138816 | tf_op jit(solution)/shard_map/reduce_scatter | solution.py:36
  152.6 16.1 %copy-start.1 = (bf16[256,4096]{1,0:T(8,128)(2,1)S(1)}, bf16[256,4096]{1,0:T(8,128)(2,1)}, u32[]{:S(2)}) copy-start(bf16[256,4096]{1,0:T(8,128)(2,1)} %param.7) | copy-start | bytes 6291460
  152.6 234.8 %reduce-scatter.3.cloned.1.call-start = ((), (), s32[]{:S(2)}) async-start(), calls=%async_computation.3 | async-start | bytes 2359296 | tf_op jit(solution)/shard_map/reduce_scatter | solution.py:32
Sparse Core Ops, SparseCore 0:
  10.8 129.2 all-gather.1
  152.7 186.7 reduce-scatter.4
  342.6 44.7 reduce-scatter.2
where the time goes:
time: 394 us
  waiting for transfers between devices  210 us (53%)
  blocking collectives  131 us (33%)
  matrix products  35.1 us (9%)
  between operations  13.8 us (4%)
    reduce_scatter x1, waiting for transfers between devices, shards(): lax.psum_scatter((lax.dot_general(weighted, hidden, (((0,), (0,)), ((), (...  161 us
    psum x1, blocking collectives, shards(): total = lax.psum(jnp.sum(shifted, axis=0), 'sample')  66.5 us
    pmax x1, blocking collectives, shards(): peak = lax.pmax(local_peak, 'sample')  64.6 us
    reduce_scatter x1, waiting for transfers between devices, shards(): lax.psum_scatter(partial_value.astype(jnp.bfloat16), 'tensor', scatter_di...  47.9 us
    dot_general x1, matrix products, shards(): lax.dot_general(hidden, gathered, (((1,), (1,)), ((), ())), preferred_ele...  16 us
    dot_general x1, matrix products, shards(): lax.dot_general(weighted, hidden, (((0,), (0,)), ((), ())), preferred_ele...  9.65 us
    dot_general x1, matrix products, shards(): jnp.dot(weighted, gathered, preferred_element_type=jnp.float32)  9.54 us
  transfers between devices with their start and end apart: 3, of which 2 were waited for; matrix products, arithmetic and copies ran while one was open for 10% of the time, Pallas kernels for 0%

commit v1 on v0

v1 whole, which is shorter than its diff:
```python
import math

import jax
import jax.numpy as jnp
from jax import lax
from jax.sharding import Mesh
from jax.sharding import PartitionSpec as P

GROUP = 32
SAMPLE = ("z", "yhi", "core")
CHIPS = ("z", "yhi")


def shards(hidden, down_weight, cotangent, scores, prompt_ids):
    samples_here = scores.shape[0]
    n_sample = lax.axis_size(SAMPLE)
    n_core = lax.axis_size("core")
    n_chip = n_sample // n_core
    prompts = samples_here * n_sample // GROUP

    packed = jnp.concatenate([scores, prompt_ids])[None, :]
    everything = lax.all_gather(packed, SAMPLE, axis=0, tiled=True)
    all_scores = everything[:, :samples_here].reshape(-1)
    all_ids = everything[:, samples_here:].reshape(-1)
    all_rewards = all_scores.astype(jnp.float32) / 64.0
    all_onehot = all_ids[:, None] == jnp.arange(prompts, dtype=jnp.int32)[None, :]
    peak = jnp.max(jnp.where(all_onehot, all_rewards[:, None], jnp.float32(-1e30)), axis=0)
    shifted = jnp.where(all_onehot, jnp.exp(all_rewards[:, None] - peak[None, :]), 0.0)
    total = jnp.sum(shifted, axis=0)
    log_norm = peak + jnp.log(total)

    rewards = scores.astype(jnp.float32) / 64.0
    onehot = prompt_ids[:, None] == jnp.arange(prompts, dtype=jnp.int32)[None, :]
    sample_norm = jnp.sum(jnp.where(onehot, log_norm[None, :], 0.0), axis=1)
    tokens_here = hidden.shape[0]
    token_weight = jnp.repeat(GROUP * jnp.exp(rewards - sample_norm), tokens_here // samples_here)
    weighted = (cotangent.astype(jnp.float32) * token_weight[:, None]).astype(jnp.bfloat16)

    rows_w = down_weight.shape[0]
    d_all = weighted.shape[1]
    weighted_p = (
        weighted.reshape(tokens_here, n_chip, n_core, rows_w)
        .transpose(0, 2, 1, 3)
        .reshape(tokens_here, d_all)
    )
    gathered = lax.all_gather(down_weight, CHIPS, axis=0, tiled=True)
    gathered = lax.all_gather(gathered, "core", axis=0, tiled=True)

    partial_value = lax.dot_general(
        hidden, gathered, (((1,), (1,)), ((), ())), preferred_element_type=jnp.float32
    ).astype(jnp.bfloat16)
    partial_value = (
        partial_value.reshape(tokens_here, n_core, n_chip, rows_w)
        .transpose(0, 2, 1, 3)
        .reshape(tokens_here, d_all)
    )
    hidden_grad = jnp.dot(weighted_p, gathered, preferred_element_type=jnp.float32).astype(
        jnp.bfloat16
    )
    layer_out = lax.psum_scatter(partial_value, "tensor", scatter_dimension=1, tiled=True)
    scale = 1.0 / math.sqrt(tokens_here * n_sample)
    grad_part = (
        lax.dot_general(
            weighted_p, hidden, (((0,), (0,)), ((), ())), preferred_element_type=jnp.float32
        )
        * scale
    ).astype(jnp.bfloat16)
    grad_part = lax.psum_scatter(grad_part, "core", scatter_dimension=0, tiled=True)
    weight_grad = lax.psum_scatter(grad_part, CHIPS, scatter_dimension=0, tiled=True)
    return (layer_out, hidden_grad, weight_grad)


def solution(mesh):
    n_tensor = mesh.shape["tensor"]
    fine = Mesh(mesh.devices.reshape(-1, 2, 2, n_tensor), ("z", "yhi", "core", "tensor"))
    return jax.shard_map(
        shards,
        mesh=fine,
        in_specs=(
            P(SAMPLE, "tensor"),
            P(SAMPLE, "tensor"),
            P(SAMPLE, None),
            P(SAMPLE),
            P(SAMPLE),
        ),
        out_specs=(P(SAMPLE, "tensor"), P(SAMPLE, "tensor"), P(SAMPLE, "tensor")),
        check_vma=False,
    )
```

time: 394 us -> 489 us (1.24)
  waiting for transfers between devices: 210 us -> 409 us
  blocking collectives: 131 us -> 16.5 us
  local copies, waits for them, and re-layouts: 0.17 us -> 15.2 us
    all_gather x1 -> x2, waiting for transfers between devices: 0.02 us -> 131 us  [the longest x1 129 us: shards(): gathered = lax.all_gather(down_weight, CHIPS, axis=0, tiled=True)]
    reduce_scatter x2 -> x3, waiting for transfers between devices: 209 us -> 278 us  [the longest x1 228 us: shards(): lax.psum_scatter(grad_part, CHIPS, scatter_dimension=0, tiled=True)]
    psum x1 -> x0, blocking collectives: 66.5 us -> none  [shards(): total = lax.psum(jnp.sum(shifted, axis=0), 'sample')]
    pmax x1 -> x0, blocking collectives: 64.6 us -> none  [shards(): peak = lax.pmax(local_peak, 'sample')]
    unnamed x0 -> x1, blocking collectives: none -> 16.5 us
    unnamed x4 -> x12, local copies, waits for them, and re-layouts: 0.02 us -> 6.39 us
  transfers between devices with their start and end apart: 3 -> 5, of which waited for: 2 -> 5; matrix products, arithmetic and copies ran while one was open for 10% -> 10% of each run, Pallas kernels for 0% -> 0%
where the time goes in v1:
time: 489 us; the launch traced here: 488 us
  waiting for transfers between devices  409 us (84%)
  matrix products  31.4 us (6%)
  blocking collectives  16.5 us (3%)
  local copies, waits for them, and re-layouts  15.2 us (3%)
  between operations  14.6 us (3%)
    reduce_scatter x1, waiting for transfers between devices, shards(): lax.psum_scatter(grad_part, CHIPS, scatter_dimension=0, tiled=True)  228 us
    all_gather x1, waiting for transfers between devices, shards(): gathered = lax.all_gather(down_weight, CHIPS, axis=0, tiled=True)  129 us
    reduce_scatter x1, waiting for transfers between devices, shards(): lax.psum_scatter(partial_value, 'tensor', scatter_dimension=1, tiled=True)  41.4 us
    unnamed x1, blocking collectives  16.5 us
    dot_general x1, matrix products, shards(): lax.dot_general(hidden, gathered, (((1,), (1,)), ((), ())), preferred_ele...  15.8 us
  transfers between devices with their start and end apart: 5, of which 5 were waited for; matrix products, arithmetic and copies ran while one was open for 10% of the time, Pallas kernels for 0%

profile of v1, /device:TPU:32, one launch (start us, length us, event | category | flops | bytes accessed | tf_op | source)
XLA Modules:
  0.0 487.9 jit_solution(408446374786911396)
XLA Ops:
  7.2 0.0 all-gather.4.cloned.1.call-start
  7.3 0.7 all-gather.4.cloned.1.call-update
  7.9 0.0 all-gather.6.cloned.1.call-start
  8.0 129.5 %all-gather.4.cloned.1.call-done = bf16[2048,1792]{1,0:T(8,128)(2,1)} async-done(((bf16[128,1792]{1,0:T(8,128)(2,1)}), bf16[2048,1792]{1,0:T(8,128)(2,1)}) %all-gather.4.cloned.1.call-update) | async-done | bytes 7340048 | tf_op jit(solution)/shard_map/all_gather | solution.py:46
  137.5 0.0 reduce-scatter.6.cloned.1.call-start
  137.5 0.6 dynamic-slice
  138.8 0.2 add_dynamic-update-slice_fusion
  139.0 16.5 %all-reduce = s32[256]{0:T(256)S(1)} all-reduce(s32[256]{0:T(256)S(1)} %add_dynamic-update-slice_fusion), channel_id=2, replica_groups=mesh['z'=8,'yhi'=2,'core'=2,'tensor'=8] {'z','yhi','core'}, use_global_device_ids=true, to_apply=%add | all-reduce | flops 256 | bytes 2048
  155.5 0.1 reshape.42
  155.5 0.1 slice.8
  155.6 0.1 div.14
  155.7 0.1 eq.31
  155.8 0.1 select_reduce_fusion.2
  156.0 0.2 select_reduce_fusion.1
  156.2 0.2 select_reduce_fusion
  156.4 0.1 broadcast_in_dim.47
  156.4 0.1 mul.20
  156.5 3.6 copy.14
  160.1 0.4 multiply_convert_fusion.1
  160.6 0.1 copy.15
  160.7 7.3 %multiply_convert_fusion = bf16[4096,1792]{1,0:T(8,128)(2,1)} fusion(bf16[256,4096]{0,1:T(8,128)(2,1)S(1)} %bitcast.17, bf16[256,1792]{1,0:T(8,128)(2,1)S(1)} %copy-done), kind=kOutput, calls=%fused_computation | convolution fusion | flops 3772776448 | bytes 17694720 | tf_op jit(solution)/shard_map/dot_general | solution.py:63
  168.0 0.0 reduce-scatter.4.cloned.1.call-start
  168.1 1.2 all-gather.6.cloned.1.call-done
  169.3 15.8 %fusion = bf16[32,8,32,128]{3,1,2,0:T(8,128)(2,1)} fusion(bf16[256,1792]{1,0:T(8,128)(2,1)S(1)} %copy-done, bf16[4096,1792]{1,0:T(8,128)(2,1)} %all-gather.6.cloned.1.call-done), kind=kOutput, calls=%fused_computation.4 | convolution fusion | flops 3759144960 | bytes 17694720 | tf_op jit(solution)/shard_map/dot_general | solution.py:49
  185.1 2.2 copy.16
  187.3 3.5 copy.13
  190.8 4.6 reshape.39
  195.4 0.0 reduce-scatter.8.cloned.1.call-start
  195.5 8.0 %reduce-scatter.6.cloned.1.call-done = bf16[2048,1792]{1,0:T(8,128)(2,1)} async-done(((bf16[4096,1792]{1,0:T(8,128)(2,1)}), bf16[2048,1792]{1,0:T(8,128)(2,1)}) %reduce-scatter.6.cloned.1.call-update) | async-done | bytes 7340048 | tf_op jit(solution)/shard_map/reduce_scatter | solution.py:68
  203.5 8.3 %convolution_convert_fusion.1 = bf16[256,1792]{1,0:T(8,128)(2,1)} fusion(bf16[256,4096]{0,1:T(8,128)(2,1)S(1)} %bitcast.18, bf16[4096,1792]{1,0:T(8,128)(2,1)} %all-gather.6.cloned.1.call-done), kind=kOutput, calls=%fused_computation.3 | convolution fusion | flops 3758555136 | bytes 17694720 | tf_op jit(solution)/shard_map/dot_general | solution.py:57
  211.8 41.4 %reduce-scatter.4.cloned.1.call-done = bf16[256,512]{1,0:T(8,128)(2,1)} async-done(((bf16[256,4096]{1,0:T(8,128)(2,1)}), bf16[256,512]{1,0:T(8,128)(2,1)}) %reduce-scatter.4.cloned.1.call-update) | async-done | bytes 262160 | tf_op jit(solution)/shard_map/reduce_scatter | solution.py:60
  253.3 228.0 %reduce-scatter.8.cloned.1.call-done = bf16[128,1792]{1,0:T(8,128)(2,1)} async-done(((bf16[2048,1792]{1,0:T(8,128)(2,1)}), bf16[128,1792]{1,0:T(8,128)(2,1)}) %reduce-scatter.8.cloned.1.call-update) | async-done | bytes 458768 | tf_op jit(solution)/shard_map/reduce_scatter | solution.py:69
  (16 shorter events, 0.1 us)
Async XLA Ops:
  7.2 153.6 %copy-start = (bf16[256,1792]{1,0:T(8,128)(2,1)S(1)}, bf16[256,1792]{1,0:T(8,128)(2,1)}, u32[]{:S(2)}) copy-start(bf16[256,1792]{1,0:T(8,128)(2,1)} %param.5) | copy-start | bytes 2752516
  7.2 130.4 %copy-start.3 = (u32[256]{0:T(256)S(1)}, u32[256]{0:T(256)}, u32[]{:S(2)}) copy-start(u32[256]{0:T(256)} %constant.19) | copy-start | bytes 3076
  7.2 131.6 %copy-start.1 = (s32[4]{0:T(128)S(1)}, s32[4]{0:T(128)}, u32[]{:S(2)}) copy-start(s32[4]{0:T(128)} %param.9) | copy-start | bytes 52
  7.2 131.6 %copy-start.2 = (s32[4]{0:T(128)S(1)}, s32[4]{0:T(128)}, u32[]{:S(2)}) copy-start(s32[4]{0:T(128)} %param.8) | copy-start | bytes 52
  7.2 130.2 %all-gather.4.cloned.1.call-start = ((), (), s32[]{:S(2)}) async-start(), calls=%async_computation.3 | async-start | bytes 7798784 | tf_op jit(solution)/shard_map/all_gather | solution.py:46
  7.9 161.4 %all-gather.6.cloned.1.call-start = ((), (), s32[]{:S(2)}) async-start(), calls=%async_computation.4 | async-start | bytes 22020096 | tf_op jit(solution)/shard_map/all_gather | solution.py:47
  137.5 66.0 %reduce-scatter.6.cloned.1.call-start = ((), (), s32[]{:S(2)}) async-start(), calls=%async_computation.6 | async-start | bytes 22020096 | tf_op jit(solution)/shard_map/reduce_scatter | solution.py:68
  168.0 85.3 %reduce-scatter.4.cloned.1.call-start = ((), (), s32[]{:S(2)}) async-start(), calls=%async_computation.5 | async-start | bytes 2359296 | tf_op jit(solution)/shard_map/reduce_scatter | solution.py:60
  195.4 285.9 %reduce-scatter.8.cloned.1.call-start = ((), (), s32[]{:S(2)}) async-start(), calls=%async_computation.7 | async-start | bytes 7798784 | tf_op jit(solution)/shard_map/reduce_scatter | solution.py:69
Sparse Core Ops, SparseCore 0:
  10.6 126.7 all-gather.3
  139.3 30.0 all-gather.5
  171.9 31.5 reduce-scatter.5
  206.5 46.7 reduce-scatter.3
  257.9 223.3 reduce-scatter.7

commit v2 on v0

v2 whole, which is shorter than its diff:
```python
import math

import jax
import jax.numpy as jnp
from jax import lax
from jax.sharding import PartitionSpec as P

GROUP = 32


def sum_to_bf16(received, axis):
    return jnp.sum(received.astype(jnp.float32), axis=axis).astype(jnp.bfloat16)


def shards(hidden, down_weight, cotangent, scores, prompt_ids):
    samples_here = scores.shape[0]
    n_sample = lax.axis_size("sample")
    n_tensor = lax.axis_size("tensor")
    prompts = samples_here * n_sample // GROUP

    packed = jnp.concatenate([scores, prompt_ids])[None, :]
    everything = lax.all_gather(packed, "sample", axis=0, tiled=True)
    all_scores = everything[:, :samples_here].reshape(-1)
    all_ids = everything[:, samples_here:].reshape(-1)
    all_rewards = all_scores.astype(jnp.float32) / 64.0
    all_onehot = all_ids[:, None] == jnp.arange(prompts, dtype=jnp.int32)[None, :]
    peak = jnp.max(jnp.where(all_onehot, all_rewards[:, None], jnp.float32(-1e30)), axis=0)
    shifted = jnp.where(all_onehot, jnp.exp(all_rewards[:, None] - peak[None, :]), 0.0)
    total = jnp.sum(shifted, axis=0)
    log_norm = peak + jnp.log(total)

    rewards = scores.astype(jnp.float32) / 64.0
    onehot = prompt_ids[:, None] == jnp.arange(prompts, dtype=jnp.int32)[None, :]
    sample_norm = jnp.sum(jnp.where(onehot, log_norm[None, :], 0.0), axis=1)
    tokens_here = hidden.shape[0]
    token_weight = jnp.repeat(GROUP * jnp.exp(rewards - sample_norm), tokens_here // samples_here)
    weighted = (cotangent.astype(jnp.float32) * token_weight[:, None]).astype(jnp.bfloat16)

    ff_here = hidden.shape[1]
    cut = ff_here // 2
    scale = 1.0 / math.sqrt(tokens_here * n_sample)

    def grad_term(cols):
        return (
            lax.dot_general(
                weighted, cols, (((0,), (0,)), ((), ())), preferred_element_type=jnp.float32
            )
            * scale
        ).astype(jnp.bfloat16)

    grad_a = lax.psum_scatter(grad_term(hidden[:, :cut]), "sample", scatter_dimension=0, tiled=True)
    term_b = grad_term(hidden[:, cut:])
    rows_here = down_weight.shape[0]
    term_b = term_b.reshape(n_sample, rows_here, ff_here - cut)
    grad_b = sum_to_bf16(lax.all_to_all(term_b, "sample", 0, 0, tiled=True), 0)
    weight_grad = jnp.concatenate([grad_a, grad_b], axis=1)

    gathered = lax.all_gather(down_weight, "sample", axis=0, tiled=True)
    partial_value = lax.dot_general(
        hidden, gathered, (((1,), (1,)), ((), ())), preferred_element_type=jnp.float32
    ).astype(jnp.bfloat16)
    d_all = partial_value.shape[1]
    partial_value = partial_value.reshape(tokens_here, n_tensor, d_all // n_tensor)
    layer_out = sum_to_bf16(lax.all_to_all(partial_value, "tensor", 1, 1, tiled=True), 1)
    hidden_grad = jnp.dot(weighted, gathered, preferred_element_type=jnp.float32).astype(
        jnp.bfloat16
    )
    return (layer_out, hidden_grad, weight_grad)


def solution(mesh):
    return jax.shard_map(
        shards,
        mesh=mesh,
        in_specs=(
            P("sample", "tensor"),
            P("sample", "tensor"),
            P("sample", None),
            P("sample"),
            P("sample"),
        ),
        out_specs=(P("sample", "tensor"), P("sample", "tensor"), P("sample", "tensor")),
        check_vma=False,
    )
```

time: 394 us -> 403 us (1.023)
  blocking collectives: 131 us -> 20.3 us
  waiting for transfers between devices: 210 us -> 304 us
  starting transfers between devices: 0.12 us -> 11.1 us
  other arithmetic: 3.66 us -> 9.96 us
    all_gather x1, waiting for transfers between devices: 0.02 us -> 187 us  [shards(): gathered = lax.all_gather(down_weight, 'sample', axis=0, tiled=True)]
    reduce_scatter x2 -> x1, waiting for transfers between devices: 209 us -> 116 us  [shards(): lax.psum_scatter(grad_term(hidden[:, :cut]), 'sample', scatter_dimension=...]
    psum x1 -> x0, blocking collectives: 66.5 us -> none  [shards(): total = lax.psum(jnp.sum(shifted, axis=0), 'sample')]
    pmax x1 -> x0, blocking collectives: 64.6 us -> none  [shards(): peak = lax.pmax(local_peak, 'sample')]
    unnamed x0 -> x1, blocking collectives: none -> 20.3 us
    all_to_all x0 -> x2, starting transfers between devices: none -> 11 us  [the longest x1 6.35 us: shards(): grad_b = sum_to_bf16(lax.all_to_all(term_b, 'sample', 0, 0, tiled=True), 0)]
    reduce_sum x1 -> x3, other arithmetic: 0.74 us -> 5.74 us  [the longest x2 5.55 us: sum_to_bf16(): return jnp.sum(received.astype(jnp.float32), axis=axis).astype(jnp.bfloat16)]
    dot_general x1 -> x2, matrix products: 9.65 us -> 12.7 us  [grad_term(): lax.dot_general(weighted, cols, (((0,), (0,)), ((), ())), preferred_eleme...]
  transfers between devices with their start and end apart: 3 -> 4, of which waited for: 2 -> 2; matrix products, arithmetic and copies ran while one was open for 10% -> 13% of each run, Pallas kernels for 0% -> 0%
where the time goes in v2:
time: 403 us; the launch traced here: 402 us
  waiting for transfers between devices  304 us (75%)
  matrix products  38.3 us (10%)
  blocking collectives  20.3 us (5%)
  between operations  14.8 us (4%)
  starting transfers between devices  11.1 us (3%)
  other arithmetic  9.96 us (2%)
    all_gather x1, waiting for transfers between devices, shards(): gathered = lax.all_gather(down_weight, 'sample', axis=0, tiled=True)  187 us
    reduce_scatter x1, waiting for transfers between devices, shards(): lax.psum_scatter(grad_term(hidden[:, :cut]), 'sample', scatter_dimension=...  116 us
    unnamed x1, blocking collectives  20.3 us
    dot_general x1, matrix products, shards(): lax.dot_general(hidden, gathered, (((1,), (1,)), ((), ())), preferred_ele...  14.8 us
    dot_general x2, matrix products, grad_term(): lax.dot_general(weighted, cols, (((0,), (0,)), ((), ())), preferred_eleme...  12.7 us
    dot_general x1, matrix products, shards(): jnp.dot(weighted, gathered, preferred_element_type=jnp.float32)  10.7 us
  transfers between devices with their start and end apart: 4, of which 2 were waited for; matrix products, arithmetic and copies ran while one was open for 13% of the time, Pallas kernels for 0%

profile of v2, /device:TPU:32, one launch (start us, length us, event | category | flops | bytes accessed | tf_op | source)
XLA Modules:
  0.0 401.6 jit_solution(7093868213546993436)
XLA Ops:
  7.2 0.0 all-gather.3.cloned.1.call-start
  7.2 0.7 all-gather.3.cloned.1.call-update
  7.9 1.3 dynamic-slice
  9.8 0.8 add_dynamic-update-slice_fusion
  10.7 20.3 %all-reduce = s32[256]{0:T(256)S(1)} all-reduce(s32[256]{0:T(256)S(1)} %add_dynamic-update-slice_fusion), channel_id=2, replica_groups=mesh['sample'=32,'tensor'=8] {'sample'}, use_global_device_ids=true, to_apply=%add | all-reduce | flops 256 | bytes 2048
  30.9 0.1 reshape.34
  31.0 0.1 slice.16
  31.1 0.1 div.14
  31.2 0.1 eq.31
  31.3 0.1 select_reduce_fusion.2
  31.5 0.2 select_reduce_fusion.1
  31.7 0.8 select_reduce_fusion
  32.5 0.7 exponential_multiply_fusion
  33.2 0.1 broadcast_in_dim.47
  33.2 0.1 mul.20
  33.3 7.2 %multiply_convert_fusion = bf16[4096,896]{1,0:T(8,128)(2,1)} fusion(bf16[256,1792]{1,0:T(8,128)(2,1)} %param.5, bf16[256,4096]{1,0:T(8,128)(2,1)} %param.7, f32[256]{0:T(256)S(1)} %mul.20), kind=kOutput, calls=%fused_computation | convolution fusion | flops 1889533952 | bytes 9896960 | tf_op jit(solution)/shard_map/dot_general | solution.py:45
  40.5 6.3 %all-to-all-start.1 = ((bf16[32,128,896]{2,1,0:T(8,128)(2,1)}), bf16[32,128,896]{2,1,0:T(8,128)(2,1)}, u32[]{:S(2)}, u32[]{:S(2)}) async-start(bf16[32,128,896]{2,1,0:T(8,128)(2,1)} %bitcast.10), calls=%async_computation.2 | async-start | bytes 14680064 | tf_op jit(solution)/shard_map/all_to_all | solution.py:55
  46.9 0.0 reduce-scatter.2.cloned.1.call-start
  46.9 0.0 copy-done
  46.9 5.6 %multiply_convert_fusion.1 = bf16[4096,896]{1,0:T(8,128)(2,1)} fusion(bf16[256,1792]{1,0:T(8,128)(2,1)S(1)} %copy-done.1, bf16[256,4096]{1,0:T(8,128)(2,1)S(1)} %copy-done, f32[256]{0:T(256)S(1)} %mul.20), kind=kOutput, calls=%fused_computation.1 | convolution fusion | flops 1889533952 | bytes 9896960 | tf_op jit(solution)/shard_map/dot_general | solution.py:45
  52.5 0.0 reduce-scatter.2.cloned.1.call-update
  52.5 186.6 %all-gather.3.cloned.1.call-done = bf16[4096,1792]{1,0:T(8,128)(2,1)} async-done(((bf16[128,1792]{1,0:T(8,128)(2,1)}), bf16[4096,1792]{1,0:T(8,128)(2,1)}) %all-gather.3.cloned.1.call-update) | async-done | bytes 14680080 | tf_op jit(solution)/shard_map/all_gather | solution.py:58
  239.1 14.8 %convolution_convert_fusion = bf16[256,4096]{1,0:T(8,128)(2,1)S(1)} fusion(bf16[256,1792]{1,0:T(8,128)(2,1)S(1)} %copy-done.1, bf16[4096,1792]{1,0:T(8,128)(2,1)} %all-gather.3.cloned.1.call-done), kind=kOutput, calls=%fused_computation.2 | convolution fusion | flops 3759144960 | bytes 17694720 | tf_op jit(solution)/shard_map/dot_general | solution.py:59
  254.0 1.5 copy.12
  255.5 0.0 all-to-all-done.1
  255.5 4.7 %all-to-all-start = ((bf16[256,8,512]{2,0,1:T(8,128)(2,1)}), bf16[256,8,512]{2,0,1:T(8,128)(2,1)S(1)}, u32[]{:S(2)}, u32[]{:S(2)}) async-start(bf16[256,8,512]{2,0,1:T(8,128)(2,1)} %bitcast.9), calls=%async_computation | async-start | bytes 4194304 | tf_op jit(solution)/shard_map/all_to_all | solution.py:64
  260.2 4.5 %reduce_sum.45 = bf16[128,896]{1,0:T(8,128)(2,1)S(1)} reduce(bf16[32,128,896]{2,1,0:T(8,128)(2,1)} %all-to-all-done.1, bf16[]{:T(256)} %constant.4.clone.1), dimensions={0}, to_apply=%region_5.6 | reduce | flops 3555328 | bytes 7569410 | tf_op jit(solution)/shard_map/reduce_sum | solution.py:12
  264.7 116.5 %reduce-scatter.2.cloned.1.call-done = bf16[128,896]{1,0:T(8,128)(2,1)} async-done(((bf16[4096,896]{1,0:T(8,128)(2,1)}), bf16[128,896]{1,0:T(8,128)(2,1)}) %reduce-scatter.2.cloned.1.call-update) | async-done | bytes 229392 | tf_op jit(solution)/shard_map/reduce_scatter | solution.py:51
  381.2 1.7 pad_maximum_fusion
  382.9 10.7 %convolution_convert_fusion.1 = bf16[256,1792]{1,0:T(8,128)(2,1)} fusion(bf16[4096,1792]{1,0:T(8,128)(2,1)} %all-gather.3.cloned.1.call-done, bf16[256,4096]{1,0:T(8,128)(2,1)} %param.7, f32[256]{0:T(256)S(1)} %mul.20), kind=kOutput, calls=%fused_computation.4 | convolution fusion | flops 3761700864 | bytes 17695744 | tf_op jit(solution)/shard_map/dot_general | solution.py:65
  393.7 0.0 all-to-all-done
  393.7 1.1 reduce_sum.42
  (6 shorter events, 0.0 us)
Async XLA Ops:
  7.2 232.0 %all-gather.3.cloned.1.call-start = ((), (), s32[]{:S(2)}) async-start(), calls=%async_computation.3 | async-start | bytes 15138816 | tf_op jit(solution)/shard_map/all_gather | solution.py:58
  40.5 6.4 %copy-start = (bf16[256,4096]{1,0:T(8,128)(2,1)S(1)}, bf16[256,4096]{1,0:T(8,128)(2,1)}, u32[]{:S(2)}) copy-start(bf16[256,4096]{1,0:T(8,128)(2,1)} %param.7) | copy-start | bytes 6291460
  40.5 6.4 %copy-start.1 = (bf16[256,1792]{1,0:T(8,128)(2,1)S(1)}, bf16[256,1792]{1,0:T(8,128)(2,1)}, u32[]{:S(2)}) copy-start(bf16[256,1792]{1,0:T(8,128)(2,1)} %param.5) | copy-start | bytes 2752516
  40.5 215.0 %all-to-all-start.1 = ((bf16[32,128,896]{2,1,0:T(8,128)(2,1)}), bf16[32,128,896]{2,1,0:T(8,128)(2,1)}, u32[]{:S(2)}, u32[]{:S(2)}) async-start(bf16[32,128,896]{2,1,0:T(8,128)(2,1)} %bitcast.10), calls=%async_computation.2 | async-start | bytes 14680064 | tf_op jit(solution)/shard_map/all_to_all | solution.py:55
  46.9 334.3 %reduce-scatter.2.cloned.1.call-start = ((), (), s32[]{:S(2)}) async-start(), calls=%async_computation.4 | async-start | bytes 7569408 | tf_op jit(solution)/shard_map/reduce_scatter | solution.py:51
  255.5 138.1 %all-to-all-start = ((bf16[256,8,512]{2,0,1:T(8,128)(2,1)}), bf16[256,8,512]{2,0,1:T(8,128)(2,1)S(1)}, u32[]{:S(2)}, u32[]{:S(2)}) async-start(bf16[256,8,512]{2,0,1:T(8,128)(2,1)} %bitcast.9), calls=%async_computation | async-start | bytes 4194304 | tf_op jit(solution)/shard_map/all_to_all | solution.py:64
Sparse Core Ops, SparseCore 0:
  10.7 228.3 all-gather.2
  243.5 137.6 reduce-scatter.1

commit v3 on v1

--- a/solution.py
+++ b/solution.py
@@ -8,14 +8,19 @@
 
 GROUP = 32
 SAMPLE = ("z", "yhi", "core")
-CHIPS = ("z", "yhi")
+
+
+def sum_to_bf16(received, axis):
+    return jnp.sum(received.astype(jnp.float32), axis=axis).astype(jnp.bfloat16)
 
 
 def shards(hidden, down_weight, cotangent, scores, prompt_ids):
     samples_here = scores.shape[0]
     n_sample = lax.axis_size(SAMPLE)
+    n_z = lax.axis_size("z")
+    n_yhi = lax.axis_size("yhi")
     n_core = lax.axis_size("core")
-    n_chip = n_sample // n_core
+    n_tensor = lax.axis_size("tensor")
     prompts = samples_here * n_sample // GROUP
 
     packed = jnp.concatenate([scores, prompt_ids])[None, :]
@@ -39,25 +44,14 @@
     rows_w = down_weight.shape[0]
     d_all = weighted.shape[1]
     weighted_p = (
-        weighted.reshape(tokens_here, n_chip, n_core, rows_w)
-        .transpose(0, 2, 1, 3)
+        weighted.reshape(tokens_here, n_z, n_yhi, n_core, rows_w)
+        .transpose(0, 3, 2, 1, 4)
         .reshape(tokens_here, d_all)
     )
-    gathered = lax.all_gather(down_weight, CHIPS, axis=0, tiled=True)
+    gathered = lax.all_gather(down_weight, "z", axis=0, tiled=True)
+    gathered = lax.all_gather(gathered, "yhi", axis=0, tiled=True)
     gathered = lax.all_gather(gathered, "core", axis=0, tiled=True)
 
-    partial_value = lax.dot_general(
-        hidden, gathered, (((1,), (1,)), ((), ())), preferred_element_type=jnp.float32
-    ).astype(jnp.bfloat16)
-    partial_value = (
-        partial_value.reshape(tokens_here, n_core, n_chip, rows_w)
-        .transpose(0, 2, 1, 3)
-        .reshape(tokens_here, d_all)
-    )
-    hidden_grad = jnp.dot(weighted_p, gathered, preferred_element_type=jnp.float32).astype(
-        jnp.bfloat16
-    )
-    layer_out = lax.psum_scatter(partial_value, "tensor", scatter_dimension=1, tiled=True)
     scale = 1.0 / math.sqrt(tokens_here * n_sample)
     grad_part = (
         lax.dot_general(
@@ -66,7 +60,21 @@
         * scale
     ).astype(jnp.bfloat16)
     grad_part = lax.psum_scatter(grad_part, "core", scatter_dimension=0, tiled=True)
-    weight_grad = lax.psum_scatter(grad_part, CHIPS, scatter_dimension=0, tiled=True)
+    grad_part = lax.psum_scatter(grad_part, "yhi", scatter_dimension=0, tiled=True)
+    weight_grad = lax.psum_scatter(grad_part, "z", scatter_dimension=0, tiled=True)
+
+    partial_value = lax.dot_general(
+        hidden, gathered, (((1,), (1,)), ((), ())), preferred_element_type=jnp.float32
+    ).astype(jnp.bfloat16)
+    partial_value = (
+        partial_value.reshape(tokens_here, n_core, n_yhi, n_z, rows_w)
+        .transpose(0, 3, 2, 1, 4)
+        .reshape(tokens_here, n_tensor, d_all // n_tensor)
+    )
+    layer_out = sum_to_bf16(lax.all_to_all(partial_value, "tensor", 1, 1, tiled=True), 1)
+    hidden_grad = jnp.dot(weighted_p, gathered, preferred_element_type=jnp.float32).astype(
+        jnp.bfloat16
+    )
     return (layer_out, hidden_grad, weight_grad)
 
 

time: 489 us -> 321 us (0.66)
  waiting for transfers between devices: 409 us -> 233 us
  local copies, waits for them, and re-layouts: 15.2 us -> 8.1 us
    reduce_scatter x2, waiting for transfers between devices: 269 us -> 97.1 us  [the longest x1 97.1 us: shards(): lax.psum_scatter(grad_part, 'yhi', scatter_dimension=0, tiled=True)]
    all_gather x1 -> x2, waiting for transfers between devices: 129 us -> 105 us  [the longest x1 89.1 us: shards(): gathered = lax.all_gather(gathered, 'yhi', axis=0, tiled=True)]
    all_to_all x0 -> x1, waiting for transfers between devices: none -> 18.5 us  [shards(): lax.all_to_all(partial_value, 'tensor', 1, 1, tiled=True)]
  transfers between devices with their start and end apart: 5 -> 7, of which waited for: 5 -> 5; matrix products, arithmetic and copies ran while one was open for 10% -> 14% of each run, Pallas kernels for 0% -> 0%
where the time goes in v3:
time: 321 us; the launch traced here: 319 us
  waiting for transfers between devices  233 us (73%)
  matrix products  30.8 us (10%)
  blocking collectives  20.4 us (6%)
  between operations  16 us (5%)
  local copies, waits for them, and re-layouts  8.1 us (3%)
  other arithmetic  5.77 us (2%)
  starting transfers between devices  4.59 us (1%)
    reduce_scatter x1, waiting for transfers between devices, shards(): lax.psum_scatter(grad_part, 'yhi', scatter_dimension=0, tiled=True)  97.1 us
    all_gather x1, waiting for transfers between devices, shards(): gathered = lax.all_gather(gathered, 'yhi', axis=0, tiled=True)  89.1 us
    unnamed x1, blocking collectives  20.4 us
    all_to_all x1, waiting for transfers between devices, shards(): lax.all_to_all(partial_value, 'tensor', 1, 1, tiled=True)  18.5 us
    all_gather x1, waiting for transfers between devices, shards(): gathered = lax.all_gather(down_weight, 'z', axis=0, tiled=True)  16 us
    dot_general x1, matrix products, shards(): lax.dot_general(hidden, gathered, (((1,), (1,)), ((), ())), preferred_ele...  14.9 us
    reduce_scatter x1, waiting for transfers between devices, shards(): lax.psum_scatter(grad_part, 'core', scatter_dimension=0, tiled=True)  11.5 us
    dot_general x1, matrix products, shards(): jnp.dot(weighted_p, gathered, preferred_element_type=jnp.float32)  8.5 us
  transfers between devices with their start and end apart: 7, of which 5 were waited for; matrix products, arithmetic and copies ran while one was open for 14% of the time, Pallas kernels for 0%

profile of v3, /device:TPU:32, one launch (start us, length us, event | category | flops | bytes accessed | tf_op | source)
XLA Modules:
  0.0 318.6 jit_solution(105216864615985112)
XLA Ops:
  8.1 0.7 all-gather.5.cloned.1.call-update
  8.7 0.0 reduce-scatter.4.cloned.1.call-start
  8.8 1.3 dynamic-slice
  10.7 0.8 add_dynamic-update-slice_fusion
  11.6 20.4 %all-reduce = s32[256]{0:T(256)S(1)} all-reduce(s32[256]{0:T(256)S(1)} %add_dynamic-update-slice_fusion), channel_id=2, replica_groups=mesh['z'=8,'yhi'=2,'core'=2,'tensor'=8] {'z','yhi','core'}, use_global_device_ids=true, to_apply=%add | all-reduce | flops 256 | bytes 2048
  32.0 0.1 reshape.42
  32.1 0.1 slice.8
  32.1 0.1 div.14
  32.2 0.1 eq.31
  32.4 0.1 select_reduce_fusion.2
  32.5 0.2 select_reduce_fusion.1
  32.7 0.8 select_reduce_fusion
  33.5 0.7 exponential_multiply_fusion
  34.2 0.1 broadcast_in_dim.47
  34.3 0.1 mul.20
  34.3 3.3 %copy.18 = bf16[256,4096]{0,1:T(8,128)(2,1)S(1)} copy(bf16[256,4096]{1,0:T(8,128)(2,1)} %param.7) | data formatting | bytes 4194304 | tf_op args[2]
  37.6 0.4 multiply_convert_fusion.1
  38.1 0.1 copy.19
  38.2 7.4 %multiply_convert_fusion = bf16[4096,1792]{1,0:T(8,128)(2,1)} fusion(bf16[256,4096]{0,1:T(8,128)(2,1)S(1)} %bitcast.18, bf16[256,1792]{1,0:T(8,128)(2,1)S(1)} %copy-done), kind=kOutput, calls=%fused_computation | convolution fusion | flops 3772776448 | bytes 17694720 | tf_op jit(solution)/shard_map/dot_general | solution.py:57
  45.6 0.0 all-gather.7.cloned.1.call-start
  45.7 16.0 %all-gather.5.cloned.1.call-done = bf16[1024,1792]{1,0:T(8,128)(2,1)} async-done(((bf16[128,1792]{1,0:T(8,128)(2,1)}), bf16[1024,1792]{1,0:T(8,128)(2,1)}) %all-gather.5.cloned.1.call-update) | async-done | bytes 3670032 | tf_op jit(solution)/shard_map/all_gather | solution.py:51
  61.8 11.5 %reduce-scatter.4.cloned.1.call-done = bf16[2048,1792]{1,0:T(8,128)(2,1)} async-done(((bf16[4096,1792]{1,0:T(8,128)(2,1)}), bf16[2048,1792]{1,0:T(8,128)(2,1)}) %reduce-scatter.4.cloned.1.call-update) | async-done | bytes 7340048 | tf_op jit(solution)/shard_map/reduce_scatter | solution.py:62
  73.4 89.1 %all-gather.7.cloned.1.call-done = bf16[2048,1792]{1,0:T(8,128)(2,1)} async-done(((bf16[1024,1792]{1,0:T(8,128)(2,1)}), bf16[2048,1792]{1,0:T(8,128)(2,1)}) %all-gather.7.cloned.1.call-update) | async-done | bytes 7340048 | tf_op jit(solution)/shard_map/all_gather | solution.py:52
  162.5 97.1 %reduce-scatter.6.cloned.1.call-done = bf16[1024,1792]{1,0:T(8,128)(2,1)} async-done(((bf16[2048,1792]{1,0:T(8,128)(2,1)}), bf16[1024,1792]{1,0:T(8,128)(2,1)}) %reduce-scatter.6.cloned.1.call-update) | async-done | bytes 3670032 | tf_op jit(solution)/shard_map/reduce_scatter | solution.py:63
  259.7 14.9 %fusion = bf16[32,8,32,128]{3,1,2,0:T(8,128)(2,1)S(1)} fusion(bf16[256,1792]{1,0:T(8,128)(2,1)S(1)} %copy-done, bf16[4096,1792]{1,0:T(8,128)(2,1)} %all-gather.9.cloned.1.call-done), kind=kOutput, calls=%fused_computation.4 | convolution fusion | flops 3759144960 | bytes 17694720 | tf_op jit(solution)/shard_map/dot_general | solution.py:66
  274.5 0.5 copy.20
  275.0 0.4 copy.16
  275.4 2.0 copy.17
  277.4 4.4 %all-to-all-start = ((bf16[256,8,512]{2,0,1:T(8,128)(2,1)}), bf16[256,8,512]{2,0,1:T(8,128)(2,1)}, u32[]{:S(2)}, u32[]{:S(2)}) async-start(bf16[256,8,512]{2,0,1:T(8,128)(2,1)} %copy.17), calls=%async_computation | async-start | bytes 4194304 | tf_op jit(solution)/shard_map/all_to_all | solution.py:74
  281.8 8.5 %convolution_convert_fusion.1 = bf16[256,1792]{1,0:T(8,128)(2,1)} fusion(bf16[256,4096]{0,1:T(8,128)(2,1)S(1)} %bitcast.19, bf16[4096,1792]{1,0:T(8,128)(2,1)} %all-gather.9.cloned.1.call-done), kind=kOutput, calls=%fused_computation.3 | convolution fusion | flops 3758555136 | bytes 17694720 | tf_op jit(solution)/shard_map/dot_general | solution.py:75
  290.3 18.5 %all-to-all-done = bf16[256,8,512]{2,0,1:T(8,128)(2,1)} async-done(((bf16[256,8,512]{2,0,1:T(8,128)(2,1)}), bf16[256,8,512]{2,0,1:T(8,128)(2,1)}, u32[]{:S(2)}, u32[]{:S(2)}) %all-to-all-start) | async-done | bytes 2097184 | tf_op jit(solution)/shard_map/all_to_all | solution.py:74
  308.8 2.7 reduce_sum.30
  (18 shorter events, 0.3 us)
Async XLA Ops:
  8.0 30.2 %copy-start = (bf16[256,1792]{1,0:T(8,128)(2,1)S(1)}, bf16[256,1792]{1,0:T(8,128)(2,1)}, u32[]{:S(2)}) copy-start(bf16[256,1792]{1,0:T(8,128)(2,1)} %param.5) | copy-start | bytes 2752516
  8.0 53.7 %all-gather.5.cloned.1.call-start = ((), (), s32[]{:S(2)}) async-start(), calls=%async_computation.4 | async-start | bytes 4128768 | tf_op jit(solution)/shard_map/all_gather | solution.py:51
  8.7 64.5 %reduce-scatter.4.cloned.1.call-start = ((), (), s32[]{:S(2)}) async-start(), calls=%async_computation.7 | async-start | bytes 22020096 | tf_op jit(solution)/shard_map/reduce_scatter | solution.py:62
  45.6 116.8 %all-gather.7.cloned.1.call-start = ((), (), s32[]{:S(2)}) async-start(), calls=%async_computation.5 | async-start | bytes 11010048 | tf_op jit(solution)/shard_map/all_gather | solution.py:52
  61.7 197.9 %reduce-scatter.6.cloned.1.call-start = ((), (), s32[]{:S(2)}) async-start(), calls=%async_computation.8 | async-start | bytes 11010048 | tf_op jit(solution)/shard_map/reduce_scatter | solution.py:63
  73.3 186.3 %all-gather.9.cloned.1.call-start = ((), (), s32[]{:S(2)}) async-start(), calls=%async_computation.6 | async-start | bytes 22020096 | tf_op jit(solution)/shard_map/all_gather | solution.py:53
  162.5 149.0 %reduce-scatter.8.cloned.1.call-start = ((), (), s32[]{:S(2)}) async-start(), calls=%async_computation.9 | async-start | bytes 4128768 | tf_op jit(solution)/shard_map/reduce_scatter | solution.py:64
  277.4 31.4 %all-to-all-start = ((bf16[256,8,512]{2,0,1:T(8,128)(2,1)}), bf16[256,8,512]{2,0,1:T(8,128)(2,1)}, u32[]{:S(2)}, u32[]{:S(2)}) async-start(bf16[256,8,512]{2,0,1:T(8,128)(2,1)} %copy.17), calls=%async_computation | async-start | bytes 4194304 | tf_op jit(solution)/shard_map/all_to_all | solution.py:74
  281.8 29.7 %copy-start.1 = (bf16[256,1792]{1,0:T(8,128)(2,1)S(1)}, bf16[256,1792]{1,0:T(8,128)(2,1)}, u32[]{:S(2)}) copy-start(bf16[256,1792]{1,0:T(8,128)(2,1)} %param.5) | copy-start | bytes 2752516
Sparse Core Ops, SparseCore 0:
  10.6 51.0 all-gather.4
  63.5 98.9 all-gather.6
  165.0 94.5 reduce-scatter.5
  262.6 48.3 reduce-scatter.7
Sparse Core Ops, SparseCore 1:
  45.7 27.5 reduce-scatter.3
  162.6 31.7 all-gather.8

commit v4 on v3

--- a/solution.py
+++ b/solution.py
@@ -43,13 +43,16 @@
 
     rows_w = down_weight.shape[0]
     d_all = weighted.shape[1]
+    own_first = lax.axis_index("yhi") == 0
+    weighted_5 = weighted.reshape(tokens_here, n_z, n_yhi, n_core, rows_w)
     weighted_p = (
-        weighted.reshape(tokens_here, n_z, n_yhi, n_core, rows_w)
+        jnp.where(own_first, weighted_5, jnp.flip(weighted_5, axis=2))
         .transpose(0, 3, 2, 1, 4)
         .reshape(tokens_here, d_all)
     )
+    swap = [(0, 1), (1, 0)]
     gathered = lax.all_gather(down_weight, "z", axis=0, tiled=True)
-    gathered = lax.all_gather(gathered, "yhi", axis=0, tiled=True)
+    gathered = jnp.concatenate([gathered, lax.ppermute(gathered, "yhi", swap)], axis=0)
     gathered = lax.all_gather(gathered, "core", axis=0, tiled=True)
 
     scale = 1.0 / math.sqrt(tokens_here * n_sample)
@@ -60,16 +63,21 @@
         * scale
     ).astype(jnp.bfloat16)
     grad_part = lax.psum_scatter(grad_part, "core", scatter_dimension=0, tiled=True)
-    grad_part = lax.psum_scatter(grad_part, "yhi", scatter_dimension=0, tiled=True)
+    half = grad_part.shape[0] // n_yhi
+    grad_part = (
+        grad_part[:half].astype(jnp.float32)
+        + lax.ppermute(grad_part[half:], "yhi", swap).astype(jnp.float32)
+    ).astype(jnp.bfloat16)
     weight_grad = lax.psum_scatter(grad_part, "z", scatter_dimension=0, tiled=True)
 
     partial_value = lax.dot_general(
         hidden, gathered, (((1,), (1,)), ((), ())), preferred_element_type=jnp.float32
     ).astype(jnp.bfloat16)
-    partial_value = (
-        partial_value.reshape(tokens_here, n_core, n_yhi, n_z, rows_w)
-        .transpose(0, 3, 2, 1, 4)
-        .reshape(tokens_here, n_tensor, d_all // n_tensor)
+    partial_value = partial_value.reshape(tokens_here, n_core, n_yhi, n_z, rows_w).transpose(
+        0, 3, 2, 1, 4
+    )
+    partial_value = jnp.where(own_first, partial_value, jnp.flip(partial_value, axis=2)).reshape(
+        tokens_here, n_tensor, d_all // n_tensor
     )
     layer_out = sum_to_bf16(lax.all_to_all(partial_value, "tensor", 1, 1, tiled=True), 1)
     hidden_grad = jnp.dot(weighted_p, gathered, preferred_element_type=jnp.float32).astype(

time: 321 us -> 302 us (0.941)
  waiting for transfers between devices: 233 us -> 183 us
  other arithmetic: 5.77 us -> 19.2 us
  local copies, waits for them, and re-layouts: 8.1 us -> 19.9 us
  starting transfers between devices: 4.59 us -> 11.6 us
  matrix products: 30.8 us -> 26.3 us
    ppermute x0 -> x2, waiting for transfers between devices: none -> 157 us  [the longest x1 79.3 us: shards(): lax.ppermute(gathered, 'yhi', swap)]
    reduce_scatter x1 -> x0, waiting for transfers between devices: 97.1 us -> none  [shards(): lax.psum_scatter(grad_part, 'yhi', scatter_dimension=0, tiled=True)]
    all_gather x1 -> x0, waiting for transfers between devices: 89.1 us -> none  [shards(): gathered = lax.all_gather(gathered, 'yhi', axis=0, tiled=True)]
    reduce_scatter x1, waiting for transfers between devices: 11.5 us -> 0.03 us  [shards(): lax.psum_scatter(grad_part, 'core', scatter_dimension=0, tiled=True)]
    all_gather x1, waiting for transfers between devices: 16 us -> 8.86 us  [shards(): gathered = lax.all_gather(down_weight, 'z', axis=0, tiled=True)]
    concatenate x0 -> x1, other arithmetic: none -> 6.64 us  [shards(): jnp.concatenate([gathered, lax.ppermute(gathered, 'yhi', swap)], axis=0)]
    ppermute x0 -> x2, starting transfers between devices: none -> 6.25 us  [the longest x1 3.28 us: shards(): lax.ppermute(grad_part[half:], 'yhi', swap).astype(jnp.float32)]
    dot_general x1, matrix products: 14.9 us -> 10.5 us  [shards(): lax.dot_general(hidden, gathered, (((1,), (1,)), ((), ())), preferred_ele...]
  transfers between devices with their start and end apart: 7 -> 7, of which waited for: 5 -> 4; matrix products, arithmetic and copies ran while one was open for 14% -> 22% of each run, Pallas kernels for 0% -> 0%
where the time goes in v4:
time: 302 us; the launch traced here: 297 us
  waiting for transfers between devices  183 us (61%)
  matrix products  26.3 us (9%)
  blocking collectives  20.6 us (7%)
  local copies, waits for them, and re-layouts  19.9 us (7%)
  other arithmetic  19.2 us (6%)
  between operations  16.3 us (5%)
  starting transfers between devices  11.6 us (4%)
    ppermute x1, waiting for transfers between devices, shards(): lax.ppermute(gathered, 'yhi', swap)  79.3 us
    ppermute x1, waiting for transfers between devices, shards(): lax.ppermute(grad_part[half:], 'yhi', swap).astype(jnp.float32)  78.1 us
    unnamed x1, blocking collectives  20.6 us
    all_to_all x1, waiting for transfers between devices, shards(): lax.all_to_all(partial_value, 'tensor', 1, 1, tiled=True)  16.3 us
    dot_general x1, matrix products, shards(): lax.dot_general(hidden, gathered, (((1,), (1,)), ((), ())), preferred_ele...  10.5 us
    all_gather x1, waiting for transfers between devices, shards(): gathered = lax.all_gather(down_weight, 'z', axis=0, tiled=True)  8.86 us
    dot_general x1, matrix products, shards(): jnp.dot(weighted_p, gathered, preferred_element_type=jnp.float32)  8.43 us
    dot_general x1, matrix products, shards(): lax.dot_general(weighted_p, hidden, (((0,), (0,)), ((), ())), preferred_e...  7.37 us
  transfers between devices with their start and end apart: 7, of which 4 were waited for; matrix products, arithmetic and copies ran while one was open for 22% of the time, Pallas kernels for 0%

profile of v4, /device:TPU:32, one launch (start us, length us, event | category | flops | bytes accessed | tf_op | source)
XLA Modules:
  0.0 297.3 jit_solution(13355716329540757321)
XLA Ops:
  8.1 0.7 all-gather.4.cloned.1.call-update
  8.8 3.3 %copy.24 = bf16[256,4096]{0,1:T(8,128)(2,1)S(1)} copy(bf16[256,4096]{1,0:T(8,128)(2,1)} %param.7) | data formatting | bytes 4194304 | tf_op args[2]
  12.1 0.6 dynamic-slice
  13.4 0.2 add_dynamic-update-slice_fusion
  13.6 20.6 %all-reduce = s32[256]{0:T(256)S(1)} all-reduce(s32[256]{0:T(256)S(1)} %add_dynamic-update-slice_fusion), channel_id=2, replica_groups=mesh['z'=8,'yhi'=2,'core'=2,'tensor'=8] {'z','yhi','core'}, use_global_device_ids=true, to_apply=%add | all-reduce | flops 256 | bytes 2048
  34.4 0.1 div.14
  34.5 0.1 eq.35
  34.6 0.1 select_reduce_fusion.2
  34.7 0.2 select_reduce_fusion.1
  34.9 0.2 select_reduce_fusion
  35.2 0.1 mul.20
  35.3 1.8 multiply_convert_fusion.1
  37.1 3.5 %copy.26 = bf16[256,8,2,2,128]{4,1,3,2,0:T(8,128)(2,1)S(1)} copy(bf16[256,8,2,2,128]{0,4,3,2,1:T(8,128)(2,1)} %bitcast.18) | data formatting | bytes 4194304 | tf_op jit(solution)/shard_map/reshape | solution.py:47
  40.6 1.9 fusion
  42.5 3.0 %copy.27 = bf16[256,2,2,8,128]{0,4,3,2,1:T(8,128)(2,1)S(1)} copy(bf16[256,2,2,8,128]{4,3,1,2,0:T(8,128)(2,1)} %fusion) | data formatting | bytes 4194304 | tf_op jit(solution)/shard_map/transpose | solution.py:50
  45.5 7.4 %multiply_convert_fusion = bf16[4096,1792]{1,0:T(8,128)(2,1)} fusion(bf16[256,4096]{0,1:T(8,128)(2,1)S(1)} %bitcast.16, bf16[256,1792]{1,0:T(8,128)(2,1)S(1)} %copy-done), kind=kOutput, calls=%fused_computation | convolution fusion | flops 3772776448 | bytes 17694720 | tf_op jit(solution)/shard_map/dot_general | solution.py:60
  53.0 8.9 %all-gather.4.cloned.1.call-done = bf16[1024,1792]{1,0:T(8,128)(2,1)} async-done(((bf16[128,1792]{1,0:T(8,128)(2,1)}), bf16[1024,1792]{1,0:T(8,128)(2,1)}) %all-gather.4.cloned.1.call-update) | async-done | bytes 3670032 | tf_op jit(solution)/shard_map/all_gather | solution.py:54
  61.8 3.0 collective-permute-start
  64.8 79.3 %collective-permute-done = bf16[1024,1792]{1,0:T(8,128)(2,1)} collective-permute-done((bf16[1024,1792]{1,0:T(8,128)(2,1)}, bf16[1024,1792]{1,0:T(8,128)(2,1)}, u32[]{:S(2)}, u32[]{:S(2)}) %collective-permute-start) | collective-permute-done | bytes 3670048 | tf_op jit(solution)/shard_map/ppermute | solution.py:55
  144.1 6.6 %pad_maximum_fusion = bf16[2048,1792]{1,0:T(8,128)(2,1)} fusion(bf16[1024,1792]{1,0:T(8,128)(2,1)} %collective-permute-done, bf16[1024,1792]{1,0:T(8,128)(2,1)} %all-gather.4.cloned.1.call-done), kind=kLoop, calls=%fused_computation.1 | loop fusion | flops 14680064 | bytes 14680064 | tf_op jit(solution)/shard_map/concatenate | solution.py:55
  150.8 2.4 slice.19
  153.3 3.3 %collective-permute-start.1 = (bf16[1024,1792]{1,0:T(8,128)(2,1)S(1)}, bf16[1024,1792]{1,0:T(8,128)(2,1)S(1)}, u32[]{:S(2)}, u32[]{:S(2)}) collective-permute-start(bf16[1024,1792]{1,0:T(8,128)(2,1)S(1)} %slice.19), channel_id=1, source_target_pairs={{0,16},{16,0},{1,17},{17,1},{2,18},{18,2},{3,19},{19,3},{4,20},{20... | collective-permute-start | bytes 11010056 | tf_op jit(solution)/shard_map/ppermute | solution.py:69
  156.5 78.1 %collective-permute-done.1 = bf16[1024,1792]{1,0:T(8,128)(2,1)S(1)} collective-permute-done((bf16[1024,1792]{1,0:T(8,128)(2,1)S(1)}, bf16[1024,1792]{1,0:T(8,128)(2,1)S(1)}, u32[]{:S(2)}, u32[]{:S(2)}) %collective-permute-start.1) | collective-permute-done | bytes 3670048 | tf_op jit(solution)/shard_map/ppermute | solution.py:69
  234.6 2.7 add_convert_fusion
  237.3 10.5 %convolution_convert_fusion = bf16[4096,256]{1,0:T(8,128)(2,1)} fusion(bf16[4096,1792]{1,0:T(8,128)(2,1)} %all-gather.6.cloned.1.call-done, bf16[256,1792]{1,0:T(8,128)(2,1)S(1)} %copy-done), kind=kOutput, calls=%fused_computation.3 | convolution fusion | flops 3759144960 | bytes 17694720 | tf_op jit(solution)/shard_map/dot_general | solution.py:73
  247.8 4.6 %copy.22 = bf16[256,2,2,8,128]{4,3,1,2,0:T(8,128)(2,1)} copy(bf16[256,2,2,8,128]{0,4,3,2,1:T(8,128)(2,1)} %bitcast.21) | data formatting | bytes 4194304 | tf_op jit(solution)/shard_map/reshape | solution.py:76
  252.4 2.8 reverse_select_fusion.1
  255.2 2.0 copy.23
  257.2 5.2 %all-to-all-start = ((bf16[256,8,512]{2,0,1:T(8,128)(2,1)}), bf16[256,8,512]{2,0,1:T(8,128)(2,1)}, u32[]{:S(2)}, u32[]{:S(2)}) async-start(bf16[256,8,512]{2,0,1:T(8,128)(2,1)} %copy.23), calls=%async_computation | async-start | bytes 4194304 | tf_op jit(solution)/shard_map/all_to_all | solution.py:82
  262.4 8.4 %convolution_convert_fusion.1 = bf16[256,1792]{1,0:T(8,128)(2,1)} fusion(bf16[256,4096]{0,1:T(8,128)(2,1)S(1)} %bitcast.17, bf16[4096,1792]{1,0:T(8,128)(2,1)} %all-gather.6.cloned.1.call-done), kind=kOutput, calls=%fused_computation.7 | convolution fusion | flops 3758555136 | bytes 17694720 | tf_op jit(solution)/shard_map/dot_general | solution.py:83
  270.9 16.3 %all-to-all-done = bf16[256,8,512]{2,0,1:T(8,128)(2,1)} async-done(((bf16[256,8,512]{2,0,1:T(8,128)(2,1)}), bf16[256,8,512]{2,0,1:T(8,128)(2,1)}, u32[]{:S(2)}, u32[]{:S(2)}) %all-to-all-start) | async-done | bytes 2097184 | tf_op jit(solution)/shard_map/all_to_all | solution.py:82
  287.2 2.7 reduce_sum.30
  (27 shorter events, 0.5 us)
Async XLA Ops:
  8.0 37.5 %copy-start = (bf16[256,1792]{1,0:T(8,128)(2,1)S(1)}, bf16[256,1792]{1,0:T(8,128)(2,1)}, u32[]{:S(2)}) copy-start(bf16[256,1792]{1,0:T(8,128)(2,1)} %param.5) | copy-start | bytes 2752516
  8.0 4.1 %copy-start.4 = (u32[256]{0:T(256)S(1)}, u32[256]{0:T(256)}, u32[]{:S(2)}) copy-start(u32[256]{0:T(256)} %constant.29) | copy-start | bytes 3076
  8.0 5.4 %copy-start.2 = (s32[4]{0:T(128)S(1)}, s32[4]{0:T(128)}, u32[]{:S(2)}) copy-start(s32[4]{0:T(128)} %param.9) | copy-start | bytes 52
  8.0 5.4 %copy-start.3 = (s32[4]{0:T(128)S(1)}, s32[4]{0:T(128)}, u32[]{:S(2)}) copy-start(s32[4]{0:T(128)} %param.8) | copy-start | bytes 52
  8.0 53.8 %all-gather.4.cloned.1.call-start = ((), (), s32[]{:S(2)}) async-start(), calls=%async_computation.3 | async-start | bytes 4128768 | tf_op jit(solution)/shard_map/all_gather | solution.py:54
  8.8 142.0 %reduce-scatter.3.cloned.1.call-start = ((), (), s32[]{:S(2)}) async-start(), calls=%async_computation.5 | async-start | bytes 22020096 | tf_op jit(solution)/shard_map/reduce_scatter | solution.py:65
  52.9 184.4 %all-gather.6.cloned.1.call-start = ((), (), s32[]{:S(2)}) async-start(), calls=%async_computation.4 | async-start | bytes 22020096 | tf_op jit(solution)/shard_map/all_gather | solution.py:56
  61.8 82.2 %collective-permute-start = (bf16[1024,1792]{1,0:T(8,128)(2,1)}, bf16[1024,1792]{1,0:T(8,128)(2,1)}, u32[]{:S(2)}, u32[]{:S(2)}) collective-permute-start(bf16[1024,1792]{1,0:T(8,128)(2,1)} %all-gather.4.cloned.1.call-done), channel_id=1, source_target_pairs={{0,16},{16,0},{1,17},{17,1},{2,18},{18,2},{3,19},{19,3},{4,20},{20... | collective-permute-start | bytes 11010056 | tf_op jit(solution)/shard_map/ppermute | solution.py:55
  150.7 139.1 %reduce-scatter.5.cloned.1.call-start = ((), (), s32[]{:S(2)}) async-start(), calls=%async_computation.6 | async-start | bytes 4128768 | tf_op jit(solution)/shard_map/reduce_scatter | solution.py:71
  150.8 83.8 %copy-start.1 = (bf16[2048,1792]{1,0:T(8,128)(2,1)S(1)}, bf16[2048,1792]{1,0:T(8,128)(2,1)}, u32[]{:S(2)}) copy-start(bf16[2048,1792]{1,0:T(8,128)(2,1)} %reduce-scatter.3.cloned.1.call-done) | copy-start | bytes 22020100
  153.3 81.3 %collective-permute-start.1 = (bf16[1024,1792]{1,0:T(8,128)(2,1)S(1)}, bf16[1024,1792]{1,0:T(8,128)(2,1)S(1)}, u32[]{:S(2)}, u32[]{:S(2)}) collective-permute-start(bf16[1024,1792]{1,0:T(8,128)(2,1)S(1)} %slice.19), channel_id=1, source_target_pairs={{0,16},{16,0},{1,17},{17,1},{2,18},{18,2},{3,19},{19,3},{4,20},{20... | collective-permute-start | bytes 11010056 | tf_op jit(solution)/shard_map/ppermute | solution.py:69
  257.2 29.9 %all-to-all-start = ((bf16[256,8,512]{2,0,1:T(8,128)(2,1)}), bf16[256,8,512]{2,0,1:T(8,128)(2,1)}, u32[]{:S(2)}, u32[]{:S(2)}) async-start(bf16[256,8,512]{2,0,1:T(8,128)(2,1)} %copy.23), calls=%async_computation | async-start | bytes 4194304 | tf_op jit(solution)/shard_map/all_to_all | solution.py:82
Sparse Core Ops, SparseCore 0:
  10.6 51.1 all-gather.3
  237.4 49.9 reduce-scatter.4
Sparse Core Ops, SparseCore 1:
  53.0 27.3 reduce-scatter.2
  150.8 32.8 all-gather.5

commit v5 on v4

--- a/solution.py
+++ b/solution.py
@@ -47,12 +47,12 @@
     weighted_5 = weighted.reshape(tokens_here, n_z, n_yhi, n_core, rows_w)
     weighted_p = (
         jnp.where(own_first, weighted_5, jnp.flip(weighted_5, axis=2))
-        .transpose(0, 3, 2, 1, 4)
+        .transpose(0, 3, 1, 2, 4)
         .reshape(tokens_here, d_all)
     )
     swap = [(0, 1), (1, 0)]
-    gathered = lax.all_gather(down_weight, "z", axis=0, tiled=True)
-    gathered = jnp.concatenate([gathered, lax.ppermute(gathered, "yhi", swap)], axis=0)
+    gathered = jnp.concatenate([down_weight, lax.ppermute(down_weight, "yhi", swap)], axis=0)
+    gathered = lax.all_gather(gathered, "z", axis=0, tiled=True)
     gathered = lax.all_gather(gathered, "core", axis=0, tiled=True)
 
     scale = 1.0 / math.sqrt(tokens_here * n_sample)
@@ -63,18 +63,17 @@
         * scale
     ).astype(jnp.bfloat16)
     grad_part = lax.psum_scatter(grad_part, "core", scatter_dimension=0, tiled=True)
-    half = grad_part.shape[0] // n_yhi
-    grad_part = (
-        grad_part[:half].astype(jnp.float32)
-        + lax.ppermute(grad_part[half:], "yhi", swap).astype(jnp.float32)
+    grad_part = lax.psum_scatter(grad_part, "z", scatter_dimension=0, tiled=True)
+    weight_grad = (
+        grad_part[:rows_w].astype(jnp.float32)
+        + lax.ppermute(grad_part[rows_w:], "yhi", swap).astype(jnp.float32)
     ).astype(jnp.bfloat16)
-    weight_grad = lax.psum_scatter(grad_part, "z", scatter_dimension=0, tiled=True)
 
     partial_value = lax.dot_general(
         hidden, gathered, (((1,), (1,)), ((), ())), preferred_element_type=jnp.float32
     ).astype(jnp.bfloat16)
-    partial_value = partial_value.reshape(tokens_here, n_core, n_yhi, n_z, rows_w).transpose(
-        0, 3, 2, 1, 4
+    partial_value = partial_value.reshape(tokens_here, n_core, n_z, n_yhi, rows_w).transpose(
+        0, 2, 3, 1, 4
     )
     partial_value = jnp.where(own_first, partial_value, jnp.flip(partial_value, axis=2)).reshape(
         tokens_here, n_tensor, d_all // n_tensor

time: 302 us -> 225 us (0.75)
  waiting for transfers between devices: 183 us -> 113 us
    ppermute x2, waiting for transfers between devices: 157 us -> 10.8 us  [the longest x1 10.8 us: shards(): lax.ppermute(down_weight, 'yhi', swap)]
    all_gather x1, waiting for transfers between devices: 0.03 us -> 32 us  [shards(): gathered = lax.all_gather(gathered, 'core', axis=0, tiled=True)]
    all_gather x1, waiting for transfers between devices: 8.86 us -> 40.2 us  [shards(): gathered = lax.all_gather(gathered, 'z', axis=0, tiled=True)]
    reduce_scatter x1, waiting for transfers between devices: 0.01 us -> 29 us  [shards(): lax.psum_scatter(grad_part, 'z', scatter_dimension=0, tiled=True)]
    all_to_all x1, waiting for transfers between devices: 16.3 us -> 0.01 us  [shards(): lax.all_to_all(partial_value, 'tensor', 1, 1, tiled=True)]
    concatenate x1, other arithmetic: 6.64 us -> 2 us  [shards(): jnp.concatenate([down_weight, lax.ppermute(down_weight, 'yhi', swap)], ax...]
  transfers between devices with their start and end apart: 7 -> 7, of which waited for: 4 -> 4; matrix products, arithmetic and copies ran while one was open for 22% -> 25% of each run, Pallas kernels for 0% -> 0%
where the time goes in v5:
time: 225 us; the launch traced here: 221 us
  waiting for transfers between devices  113 us (50%)
  matrix products  26.4 us (12%)
  blocking collectives  20.4 us (9%)
  local copies, waits for them, and re-layouts  17.4 us (8%)
  between operations  16.3 us (7%)
  other arithmetic  16.2 us (7%)
  starting transfers between devices  11.9 us (5%)
    all_gather x1, waiting for transfers between devices, shards(): gathered = lax.all_gather(gathered, 'z', axis=0, tiled=True)  40.2 us
    all_gather x1, waiting for transfers between devices, shards(): gathered = lax.all_gather(gathered, 'core', axis=0, tiled=True)  32 us
    reduce_scatter x1, waiting for transfers between devices, shards(): lax.psum_scatter(grad_part, 'z', scatter_dimension=0, tiled=True)  29 us
    unnamed x1, blocking collectives  20.4 us
    ppermute x1, waiting for transfers between devices, shards(): lax.ppermute(down_weight, 'yhi', swap)  10.8 us
    dot_general x1, matrix products, shards(): lax.dot_general(hidden, gathered, (((1,), (1,)), ((), ())), preferred_ele...  10.7 us
    dot_general x1, matrix products, shards(): jnp.dot(weighted_p, gathered, preferred_element_type=jnp.float32)  8.39 us
    dot_general x1, matrix products, shards(): lax.dot_general(weighted_p, hidden, (((0,), (0,)), ((), ())), preferred_e...  7.36 us
  transfers between devices with their start and end apart: 7, of which 4 were waited for; matrix products, arithmetic and copies ran while one was open for 25% of the time, Pallas kernels for 0%

profile of v5, /device:TPU:32, one launch (start us, length us, event | category | flops | bytes accessed | tf_op | source)
XLA Modules:
  0.0 221.4 jit_solution(7047300326295365313)
XLA Ops:
  8.1 3.3 %collective-permute-start = (bf16[128,1792]{1,0:T(8,128)(2,1)}, bf16[128,1792]{1,0:T(8,128)(2,1)S(1)}, u32[]{:S(2)}, u32[]{:S(2)}) collective-permute-start(bf16[128,1792]{1,0:T(8,128)(2,1)} %param.6), channel_id=1, source_target_pairs={{0,16},{16,0},{1,17},{17,1},{2,18},{18,2},{3,19},{19,3},{4,20},{20... | collective-permute-start | bytes 1376264 | tf_op jit(solution)/shard_map/ppermute | solution.py:54
  11.4 10.8 %collective-permute-done = bf16[128,1792]{1,0:T(8,128)(2,1)S(1)} collective-permute-done((bf16[128,1792]{1,0:T(8,128)(2,1)}, bf16[128,1792]{1,0:T(8,128)(2,1)S(1)}, u32[]{:S(2)}, u32[]{:S(2)}) %collective-permute-start) | collective-permute-done | bytes 458784 | tf_op jit(solution)/shard_map/ppermute | solution.py:54
  22.2 2.0 pad_maximum_fusion
  24.3 0.6 dynamic-slice
  25.5 0.2 add_dynamic-update-slice_fusion
  25.7 20.4 %all-reduce = s32[256]{0:T(256)S(1)} all-reduce(s32[256]{0:T(256)S(1)} %add_dynamic-update-slice_fusion), channel_id=2, replica_groups=mesh['z'=8,'yhi'=2,'core'=2,'tensor'=8] {'z','yhi','core'}, use_global_device_ids=true, to_apply=%add | all-reduce | flops 256 | bytes 2048
  46.3 0.1 div.14
  46.4 0.1 eq.35
  46.5 0.1 select_reduce_fusion.2
  46.6 0.2 select_reduce_fusion.1
  46.8 0.2 select_reduce_fusion
  47.1 0.1 mul.20
  47.2 2.5 %copy.24 = bf16[256,4096]{0,1:T(8,128)(2,1)} copy(bf16[256,4096]{1,0:T(8,128)(2,1)S(1)} %copy-done.2) | data formatting | bytes 4194304 | tf_op args[2]
  49.6 2.0 multiply_convert_fusion.1
  51.7 3.1 %copy.26 = bf16[256,8,2,2,128]{4,1,3,2,0:T(8,128)(2,1)} copy(bf16[256,8,2,2,128]{0,4,3,2,1:T(8,128)(2,1)S(1)} %bitcast.18) | data formatting | bytes 4194304 | tf_op jit(solution)/shard_map/reshape | solution.py:47
  54.8 4.1 %fusion = bf16[256,2,8,2,128]{4,2,1,3,0:T(8,128)(2,1)} fusion(bf16[256,8,2,2,128]{4,1,3,2,0:T(8,128)(2,1)} %copy.26, pred[]{:T(512)S(6)} %eq.31), kind=kLoop, calls=%fused_computation.6 | loop fusion | flops 1048576 | bytes 4194305 | tf_op jit(solution)/shard_map/transpose | solution.py:50
  58.9 3.0 %copy.27 = bf16[256,2,8,2,128]{0,4,3,2,1:T(8,128)(2,1)S(1)} copy(bf16[256,2,8,2,128]{4,2,1,3,0:T(8,128)(2,1)} %fusion) | data formatting | bytes 4194304 | tf_op jit(solution)/shard_map/transpose | solution.py:50
  61.9 7.4 %multiply_convert_fusion = bf16[4096,1792]{1,0:T(8,128)(2,1)} fusion(bf16[256,4096]{0,1:T(8,128)(2,1)S(1)} %bitcast.16, bf16[256,1792]{1,0:T(8,128)(2,1)S(1)} %copy-done), kind=kOutput, calls=%fused_computation | convolution fusion | flops 3772776448 | bytes 17694720 | tf_op jit(solution)/shard_map/dot_general | solution.py:60
  69.4 40.2 %all-gather.4.cloned.1.call-done = bf16[2048,1792]{1,0:T(8,128)(2,1)} async-done(((bf16[256,1792]{1,0:T(8,128)(2,1)}), bf16[2048,1792]{1,0:T(8,128)(2,1)}) %all-gather.4.cloned.1.call-update) | async-done | bytes 7340048 | tf_op jit(solution)/shard_map/all_gather | solution.py:55
  109.6 0.7 reduce-scatter.5.cloned.1.call-update
  110.3 32.0 %all-gather.6.cloned.1.call-done = bf16[4096,1792]{1,0:T(8,128)(2,1)} async-done(((bf16[2048,1792]{1,0:T(8,128)(2,1)}), bf16[4096,1792]{1,0:T(8,128)(2,1)}) %all-gather.6.cloned.1.call-update) | async-done | bytes 14680080 | tf_op jit(solution)/shard_map/all_gather | solution.py:56
  142.3 10.7 %convolution_convert_fusion = bf16[4096,256]{1,0:T(8,128)(2,1)} fusion(bf16[4096,1792]{1,0:T(8,128)(2,1)} %all-gather.6.cloned.1.call-done, bf16[256,1792]{1,0:T(8,128)(2,1)S(1)} %copy-done), kind=kOutput, calls=%fused_computation.1 | convolution fusion | flops 3759144960 | bytes 17694720 | tf_op jit(solution)/shard_map/dot_general | solution.py:72
  153.0 4.6 %copy.22 = bf16[256,2,8,2,128]{4,2,1,3,0:T(8,128)(2,1)} copy(bf16[256,2,8,2,128]{0,4,3,2,1:T(8,128)(2,1)} %bitcast.21) | data formatting | bytes 4194304 | tf_op jit(solution)/shard_map/reshape | solution.py:75
  157.5 2.8 %reverse_select_fusion.1 = bf16[256,8,2,2,128]{4,1,3,2,0:T(8,128)(2,1)S(1)} fusion(bf16[256,8,2,2,128]{4,1,3,2,0:T(8,128)(2,1)} %bitcast.19, pred[]{:T(512)S(6)} %eq.31), kind=kLoop, calls=%fused_computation.4 | loop fusion | flops 1048576 | bytes 4194305 | tf_op jit(solution)/shard_map/jit(_where)/select_n | solution.py:78
  160.3 2.0 copy.23
  162.3 5.2 %all-to-all-start = ((bf16[256,8,512]{2,0,1:T(8,128)(2,1)}), bf16[256,8,512]{2,0,1:T(8,128)(2,1)}, u32[]{:S(2)}, u32[]{:S(2)}) async-start(bf16[256,8,512]{2,0,1:T(8,128)(2,1)} %copy.23), calls=%async_computation | async-start | bytes 4194304 | tf_op jit(solution)/shard_map/all_to_all | solution.py:81
  167.5 29.0 %reduce-scatter.5.cloned.1.call-done = bf16[256,1792]{1,0:T(8,128)(2,1)} async-done(((bf16[2048,1792]{1,0:T(8,128)(2,1)}), bf16[256,1792]{1,0:T(8,128)(2,1)}) %reduce-scatter.5.cloned.1.call-update) | async-done | bytes 917520 | tf_op jit(solution)/shard_map/reduce_scatter | solution.py:66
  196.6 1.0 slice.19
  197.6 3.3 %collective-permute-start.1 = (bf16[128,1792]{1,0:T(8,128)(2,1)S(1)}, bf16[128,1792]{1,0:T(8,128)(2,1)}, u32[]{:S(2)}, u32[]{:S(2)}) collective-permute-start(bf16[128,1792]{1,0:T(8,128)(2,1)S(1)} %slice.19), channel_id=1, source_target_pairs={{0,16},{16,0},{1,17},{17,1},{2,18},{18,2},{3,19},{19,3},{4,20},{20... | collective-permute-start | bytes 1376264 | tf_op jit(solution)/shard_map/ppermute | solution.py:69
  200.9 8.4 %convolution_convert_fusion.1 = bf16[256,1792]{1,0:T(8,128)(2,1)} fusion(bf16[256,4096]{0,1:T(8,128)(2,1)S(1)} %bitcast.17, bf16[4096,1792]{1,0:T(8,128)(2,1)} %all-gather.6.cloned.1.call-done), kind=kOutput, calls=%fused_computation.5 | convolution fusion | flops 3758555136 | bytes 17694720 | tf_op jit(solution)/shard_map/dot_general | solution.py:82
  209.3 2.7 %reduce_sum.30 = bf16[256,512]{1,0:T(8,128)(2,1)} reduce(bf16[256,8,512]{2,0,1:T(8,128)(2,1)} %all-to-all-done, bf16[]{:T(256)} %constant.8.clone.1), dimensions={1}, to_apply=%region_0.1 | reduce | flops 917504 | bytes 2359298 | tf_op jit(solution)/shard_map/reduce_sum | solution.py:14
  212.1 1.9 add_convert_fusion
  (31 shorter events, 0.5 us)
Async XLA Ops:
  8.0 53.9 %copy-start = (bf16[256,1792]{1,0:T(8,128)(2,1)S(1)}, bf16[256,1792]{1,0:T(8,128)(2,1)}, u32[]{:S(2)}) copy-start(bf16[256,1792]{1,0:T(8,128)(2,1)} %param.5) | copy-start | bytes 2752516
  8.0 16.2 %copy-start.6 = (u32[256]{0:T(256)S(1)}, u32[256]{0:T(256)}, u32[]{:S(2)}) copy-start(u32[256]{0:T(256)} %constant.29) | copy-start | bytes 3076
  8.0 17.5 %copy-start.4 = (s32[4]{0:T(128)S(1)}, s32[4]{0:T(128)}, u32[]{:S(2)}) copy-start(s32[4]{0:T(128)} %param.9) | copy-start | bytes 52
  8.0 17.5 %copy-start.5 = (s32[4]{0:T(128)S(1)}, s32[4]{0:T(128)}, u32[]{:S(2)}) copy-start(s32[4]{0:T(128)} %param.8) | copy-start | bytes 52
  8.0 39.1 %copy-start.2 = (bf16[256,4096]{1,0:T(8,128)(2,1)S(1)}, bf16[256,4096]{1,0:T(8,128)(2,1)}, u32[]{:S(2)}) copy-start(bf16[256,4096]{1,0:T(8,128)(2,1)} %param.7) | copy-start | bytes 6291460
  8.1 101.5 %all-gather.4.cloned.1.call-start = ((), (), s32[]{:S(2)}) async-start(), calls=%async_computation.3 | async-start | bytes 8257536 | tf_op jit(solution)/shard_map/all_gather | solution.py:55
  8.1 14.1 %collective-permute-start = (bf16[128,1792]{1,0:T(8,128)(2,1)}, bf16[128,1792]{1,0:T(8,128)(2,1)S(1)}, u32[]{:S(2)}, u32[]{:S(2)}) collective-permute-start(bf16[128,1792]{1,0:T(8,128)(2,1)} %param.6), channel_id=1, source_target_pairs={{0,16},{16,0},{1,17},{17,1},{2,18},{18,2},{3,19},{19,3},{4,20},{20... | collective-permute-start | bytes 1376264 | tf_op jit(solution)/shard_map/ppermute | solution.py:54
  24.2 85.4 %reduce-scatter.3.cloned.1.call-start = ((), (), s32[]{:S(2)}) async-start(), calls=%async_computation.5 | async-start | bytes 22020096 | tf_op jit(solution)/shard_map/reduce_scatter | solution.py:65
  69.3 73.0 %all-gather.6.cloned.1.call-start = ((), (), s32[]{:S(2)}) async-start(), calls=%async_computation.4 | async-start | bytes 22020096 | tf_op jit(solution)/shard_map/all_gather | solution.py:56
  109.6 87.0 %reduce-scatter.5.cloned.1.call-start = ((), (), s32[]{:S(2)}) async-start(), calls=%async_computation.6 | async-start | bytes 8257536 | tf_op jit(solution)/shard_map/reduce_scatter | solution.py:66
  162.3 47.0 %all-to-all-start = ((bf16[256,8,512]{2,0,1:T(8,128)(2,1)}), bf16[256,8,512]{2,0,1:T(8,128)(2,1)}, u32[]{:S(2)}, u32[]{:S(2)}) async-start(bf16[256,8,512]{2,0,1:T(8,128)(2,1)} %copy.23), calls=%async_computation | async-start | bytes 4194304 | tf_op jit(solution)/shard_map/all_to_all | solution.py:81
  197.6 14.4 %collective-permute-start.1 = (bf16[128,1792]{1,0:T(8,128)(2,1)S(1)}, bf16[128,1792]{1,0:T(8,128)(2,1)}, u32[]{:S(2)}, u32[]{:S(2)}) collective-permute-start(bf16[128,1792]{1,0:T(8,128)(2,1)S(1)} %slice.19), channel_id=1, source_target_pairs={{0,16},{16,0},{1,17},{17,1},{2,18},{18,2},{3,19},{19,3},{4,20},{20... | collective-permute-start | bytes 1376264 | tf_op jit(solution)/shard_map/ppermute | solution.py:69
  200.9 13.0 %copy-start.1 = (bf16[256,1792]{1,0:T(8,128)(2,1)S(1)}, bf16[256,1792]{1,0:T(8,128)(2,1)}, u32[]{:S(2)}) copy-start(bf16[256,1792]{1,0:T(8,128)(2,1)} %param.5) | copy-start | bytes 2752516
  209.3 2.7 %copy-start.3 = (bf16[256,1792]{1,0:T(8,128)(2,1)S(1)}, bf16[256,1792]{1,0:T(8,128)(2,1)}, u32[]{:S(2)}) copy-start(bf16[256,1792]{1,0:T(8,128)(2,1)} %reduce-scatter.5.cloned.1.call-done) | copy-start | bytes 2752516
Sparse Core Ops, SparseCore 0:
  24.3 85.1 all-gather.3
  112.9 83.5 reduce-scatter.4
Sparse Core Ops, SparseCore 1:
  69.4 27.5 reduce-scatter.2
  109.6 32.6 all-gather.5

commit v6 on v5

--- a/solution.py
+++ b/solution.py
@@ -43,45 +43,67 @@
 
     rows_w = down_weight.shape[0]
     d_all = weighted.shape[1]
+    ff_here = hidden.shape[1]
+    cut = ff_here // 2
+    swap = [(0, 1), (1, 0)]
     own_first = lax.axis_index("yhi") == 0
     weighted_5 = weighted.reshape(tokens_here, n_z, n_yhi, n_core, rows_w)
-    weighted_p = (
-        jnp.where(own_first, weighted_5, jnp.flip(weighted_5, axis=2))
-        .transpose(0, 3, 1, 2, 4)
-        .reshape(tokens_here, d_all)
-    )
-    swap = [(0, 1), (1, 0)]
-    gathered = jnp.concatenate([down_weight, lax.ppermute(down_weight, "yhi", swap)], axis=0)
-    gathered = lax.all_gather(gathered, "z", axis=0, tiled=True)
-    gathered = lax.all_gather(gathered, "core", axis=0, tiled=True)
+    weighted_rel = jnp.where(own_first, weighted_5, jnp.flip(weighted_5, axis=2))
+    weighted_a = weighted_rel.transpose(0, 3, 2, 1, 4).reshape(tokens_here, d_all)
+    weighted_b = weighted_rel.transpose(0, 3, 1, 2, 4).reshape(tokens_here, d_all)
+
+    gathered_a = lax.all_gather(down_weight[:, :cut], "z", axis=0, tiled=True)
+    gathered_a = jnp.concatenate([gathered_a, lax.ppermute(gathered_a, "yhi", swap)], axis=0)
+    gathered_a = lax.all_gather(gathered_a, "core", axis=0, tiled=True)
+    weight_b = down_weight[:, cut:]
+    gathered_b = jnp.concatenate([weight_b, lax.ppermute(weight_b, "yhi", swap)], axis=0)
+    gathered_b = lax.all_gather(gathered_b, "z", axis=0, tiled=True)
+    gathered_b = lax.all_gather(gathered_b, "core", axis=0, tiled=True)
 
     scale = 1.0 / math.sqrt(tokens_here * n_sample)
-    grad_part = (
-        lax.dot_general(
-            weighted_p, hidden, (((0,), (0,)), ((), ())), preferred_element_type=jnp.float32
-        )
-        * scale
-    ).astype(jnp.bfloat16)
-    grad_part = lax.psum_scatter(grad_part, "core", scatter_dimension=0, tiled=True)
-    grad_part = lax.psum_scatter(grad_part, "z", scatter_dimension=0, tiled=True)
-    weight_grad = (
-        grad_part[:rows_w].astype(jnp.float32)
-        + lax.ppermute(grad_part[rows_w:], "yhi", swap).astype(jnp.float32)
-    ).astype(jnp.bfloat16)
 
-    partial_value = lax.dot_general(
-        hidden, gathered, (((1,), (1,)), ((), ())), preferred_element_type=jnp.float32
-    ).astype(jnp.bfloat16)
-    partial_value = partial_value.reshape(tokens_here, n_core, n_z, n_yhi, rows_w).transpose(
-        0, 2, 3, 1, 4
+    def grad_term(rows, cols):
+        return (
+            lax.dot_general(rows, cols, (((0,), (0,)), ((), ())), preferred_element_type=jnp.float32)
+            * scale
+        ).astype(jnp.bfloat16)
+
+    def add_swapped(mine, theirs):
+        got = lax.ppermute(theirs, "yhi", swap)
+        return (mine.astype(jnp.float32) + got.astype(jnp.float32)).astype(jnp.bfloat16)
+
+    grad_a = grad_term(weighted_a, hidden[:, :cut])
+    grad_a = lax.psum_scatter(grad_a, "core", scatter_dimension=0, tiled=True)
+    half = grad_a.shape[0] // n_yhi
+    grad_a = add_swapped(grad_a[:half], grad_a[half:])
+    grad_a = lax.psum_scatter(grad_a, "z", scatter_dimension=0, tiled=True)
+    grad_b = grad_term(weighted_b, hidden[:, cut:])
+    grad_b = lax.psum_scatter(grad_b, "core", scatter_dimension=0, tiled=True)
+    grad_b = lax.psum_scatter(grad_b, "z", scatter_dimension=0, tiled=True)
+    grad_b = add_swapped(grad_b[:rows_w], grad_b[rows_w:])
+    weight_grad = jnp.concatenate([grad_a, grad_b], axis=1)
+
+    value_a = lax.dot_general(
+        hidden[:, :cut], gathered_a, (((1,), (1,)), ((), ())), preferred_element_type=jnp.float32
     )
-    partial_value = jnp.where(own_first, partial_value, jnp.flip(partial_value, axis=2)).reshape(
+    value_b = lax.dot_general(
+        hidden[:, cut:], gathered_b, (((1,), (1,)), ((), ())), preferred_element_type=jnp.float32
+    )
+    partial_value = value_a.reshape(tokens_here, n_core, n_yhi, n_z, rows_w).transpose(
+        0, 3, 2, 1, 4
+    ) + value_b.reshape(tokens_here, n_core, n_z, n_yhi, rows_w).transpose(0, 2, 3, 1, 4)
+    partial_value = jnp.where(own_first, partial_value, jnp.flip(partial_value, axis=2))
+    partial_value = partial_value.astype(jnp.bfloat16).reshape(
         tokens_here, n_tensor, d_all // n_tensor
     )
     layer_out = sum_to_bf16(lax.all_to_all(partial_value, "tensor", 1, 1, tiled=True), 1)
-    hidden_grad = jnp.dot(weighted_p, gathered, preferred_element_type=jnp.float32).astype(
-        jnp.bfloat16
-    )
+    hidden_grad = jnp.concatenate(
+        [
+            jnp.dot(weighted_a, gathered_a, preferred_element_type=jnp.float32),
+            jnp.dot(weighted_b, gathered_b, preferred_element_type=jnp.float32),
+        ],
+        axis=1,
+    ).astype(jnp.bfloat16)
     return (layer_out, hidden_grad, weight_grad)
 
 

time: 225 us -> 240 us (1.067)
  waiting for transfers between devices: 113 us -> 93.7 us
  local copies, waits for them, and re-layouts: 17.4 us -> 32.5 us
  matrix products: 26.4 us -> 35.9 us
  other arithmetic: 16.2 us -> 24.8 us
    ppermute x2 -> x4, waiting for transfers between devices: 10.8 us -> 83.4 us  [the longest x2 39.4 us: add_swapped(): got = lax.ppermute(theirs, 'yhi', swap)]
    all_gather x2 -> x4, waiting for transfers between devices: 72.2 us -> 0.06 us  [the longest x1 0.02 us: shards(): gathered_a = lax.all_gather(gathered_a, 'core', axis=0, tiled=True)]
    reduce_scatter x2 -> x4, waiting for transfers between devices: 29.1 us -> 0.07 us  [the longest x1 0.03 us: shards(): grad_a = lax.psum_scatter(grad_a, 'z', scatter_dimension=0, tiled=True)]
    dot_general x3 -> x6, matrix products: 26.4 us -> 35.9 us  [the longest x2 10.6 us: grad_term(): lax.dot_general(rows, cols, (((0,), (0,)), ((), ())), preferred_element_t...]
    all_to_all x1, waiting for transfers between devices: 0.01 us -> 9.13 us  [shards(): lax.all_to_all(partial_value, 'tensor', 1, 1, tiled=True)]
    reshape x2 -> x3, local copies, waits for them, and re-layouts: 6.58 us -> 13.2 us  [the longest x1 5.62 us: shards(): value_a.reshape(tokens_here, n_core, n_yhi, n_z, rows_w)]
    concatenate x1 -> x4, other arithmetic: 2 us -> 8.28 us  [the longest x1 3.59 us: shards(): jnp.concatenate([gathered_a, lax.ppermute(gathered_a, 'yhi', swap)], axis=0)]
    add x0 -> x1, other arithmetic: none -> 4.58 us  [shards(): value_a.reshape(tokens_here, n_core, n_yhi, n_z, rows_w)]
  transfers between devices with their start and end apart: 7 -> 13, of which waited for: 4 -> 5; matrix products, arithmetic and copies ran while one was open for 25% -> 38% of each run, Pallas kernels for 0% -> 0%
where the time goes in v6:
time: 240 us; the launch traced here: 237 us
  waiting for transfers between devices  93.7 us (39%)
  matrix products  35.9 us (15%)
  local copies, waits for them, and re-layouts  32.5 us (14%)
  other arithmetic  24.8 us (10%)
  blocking collectives  20.4 us (8%)
  between operations  16.4 us (7%)
  starting transfers between devices  13.2 us (6%)
    ppermute x2, waiting for transfers between devices, add_swapped(): got = lax.ppermute(theirs, 'yhi', swap)  39.4 us
    ppermute x1, waiting for transfers between devices, shards(): lax.ppermute(gathered_a, 'yhi', swap)  38.4 us
    unnamed x1, blocking collectives  20.4 us
    dot_general x2, matrix products, grad_term(): lax.dot_general(rows, cols, (((0,), (0,)), ((), ())), preferred_element_t...  10.6 us
    all_to_all x1, waiting for transfers between devices, shards(): lax.all_to_all(partial_value, 'tensor', 1, 1, tiled=True)  9.13 us
    dot_general x1, matrix products, shards(): lax.dot_general(hidden[:, :cut], gathered_a, (((1,), (1,)), ((), ())), pr...  7.54 us
    dot_general x1, matrix products, shards(): lax.dot_general(hidden[:, cut:], gathered_b, (((1,), (1,)), ((), ())), pr...  7.49 us
    dot_general x1, matrix products, shards(): jnp.dot(weighted_a, gathered_a, preferred_element_type=jnp.float32)  7.08 us
  transfers between devices with their start and end apart: 13, of which 5 were waited for; matrix products, arithmetic and copies ran while one was open for 38% of the time, Pallas kernels for 0%

profile of v6, /device:TPU:32, one launch (start us, length us, event | category | flops | bytes accessed | tf_op | source)
XLA Modules:
  0.0 236.9 jit_solution(684611387117791789)
XLA Ops:
  8.0 1.8 fusion.10
  9.9 3.3 %collective-permute-start.1 = (bf16[128,896]{1,0:T(8,128)(2,1)S(1)}, bf16[128,896]{1,0:T(8,128)(2,1)S(1)}, u32[]{:S(2)}, u32[]{:S(2)}) collective-permute-start(bf16[128,896]{1,0:T(8,128)(2,1)S(1)} %get-tuple-element.6), channel_id=1, source_target_pairs={{0,16},{16,0},{1,17},{17,1},{2,18},{18,2},{3,19},{19,3},{4,20},{20... | collective-permute-start | bytes 688136 | tf_op jit(solution)/shard_map/ppermute | solution.py:59
  13.2 5.7 %collective-permute-done.1 = bf16[128,896]{1,0:T(8,128)(2,1)S(1)} collective-permute-done((bf16[128,896]{1,0:T(8,128)(2,1)S(1)}, bf16[128,896]{1,0:T(8,128)(2,1)S(1)}, u32[]{:S(2)}, u32[]{:S(2)}) %collective-permute-start.1) | collective-permute-done | bytes 229408 | tf_op jit(solution)/shard_map/ppermute | solution.py:59
  22.5 20.4 %all-reduce = s32[256]{0:T(256)S(1)} all-reduce(s32[256]{0:T(256)S(1)} %add_dynamic-update-slice_fusion), channel_id=2, replica_groups=mesh['z'=8,'yhi'=2,'core'=2,'tensor'=8] {'z','yhi','core'}, use_global_device_ids=true, to_apply=%add | all-reduce | flops 256 | bytes 2048
  45.3 3.3 %copy.32 = bf16[256,4096]{0,1:T(8,128)(2,1)S(1)} copy(bf16[256,4096]{1,0:T(8,128)(2,1)} %param.7) | data formatting | bytes 4194304 | tf_op args[2]
  48.6 1.8 multiply_convert_fusion.2
  50.4 3.5 %copy.34 = bf16[256,8,2,2,128]{4,1,3,2,0:T(8,128)(2,1)S(1)} copy(bf16[256,8,2,2,128]{0,4,3,2,1:T(8,128)(2,1)} %bitcast.33) | data formatting | bytes 4194304 | tf_op jit(solution)/shard_map/reshape | solution.py:50
  53.8 2.6 %fusion.2 = (bf16[256,2,2,8,128]{4,3,1,2,0:T(8,128)(2,1)}, bf16[256,2,8,2,128]{4,2,1,3,0:T(8,128)(2,1)}) fusion(bf16[256,8,2,2,128]{4,1,3,2,0:T(8,128)(2,1)S(1)} %copy.34, pred[]{:T(512)S(6)} %eq.31), kind=kLoop, calls=%fused_computation.10 | loop fusion | flops 1048576 | bytes 6291457 | tf_op jit(solution)/shard_map/transpose | solution.py:52
  56.4 3.1 %copy.36 = bf16[256,2,8,2,128]{0,4,3,2,1:T(8,128)(2,1)S(1)} copy(bf16[256,2,8,2,128]{4,2,1,3,0:T(8,128)(2,1)} %get-tuple-element.4) | data formatting | bytes 4194304 | tf_op jit(solution)/shard_map/transpose | solution.py:53
  59.5 5.3 %multiply_convert_fusion = bf16[4096,896]{1,0:T(8,128)(2,1)} fusion(bf16[256,4096]{0,1:T(8,128)(2,1)S(1)} %bitcast.29, bf16[256,1792]{1,0:T(8,128)(2,1)S(1)} %copy-done.5), kind=kOutput, calls=%fused_computation | convolution fusion | flops 1886388224 | bytes 9895936 | tf_op jit(solution)/shard_map/dot_general | solution.py:67
  64.9 3.0 %copy.35 = bf16[256,2,2,8,128]{0,4,3,2,1:T(8,128)(2,1)S(1)} copy(bf16[256,2,2,8,128]{4,3,1,2,0:T(8,128)(2,1)} %get-tuple-element.3) | data formatting | bytes 4194304 | tf_op jit(solution)/shard_map/transpose | solution.py:52
  67.9 5.3 %multiply_convert_fusion.1 = bf16[4096,896]{1,0:T(8,128)(2,1)} fusion(bf16[256,4096]{0,1:T(8,128)(2,1)S(1)} %bitcast.31, bf16[256,1792]{1,0:T(8,128)(2,1)S(1)} %copy-done.5), kind=kOutput, calls=%fused_computation.1 | convolution fusion | flops 1886388224 | bytes 9895936 | tf_op jit(solution)/shard_map/dot_general | solution.py:67
  73.3 2.4 %collective-permute-start = (bf16[1024,896]{1,0:T(8,128)(2,1)}, bf16[1024,896]{1,0:T(8,128)(2,1)S(1)}, u32[]{:S(2)}, u32[]{:S(2)}) collective-permute-start(bf16[1024,896]{1,0:T(8,128)(2,1)} %all-gather.6.cloned.1.call-done), channel_id=1, source_target_pairs={{0,16},{16,0},{1,17},{17,1},{2,18},{18,2},{3,19},{19,3},{4,20},{20... | collective-permute-start | bytes 5505032 | tf_op jit(solution)/shard_map/ppermute | solution.py:56
  75.7 38.4 %collective-permute-done = bf16[1024,896]{1,0:T(8,128)(2,1)S(1)} collective-permute-done((bf16[1024,896]{1,0:T(8,128)(2,1)}, bf16[1024,896]{1,0:T(8,128)(2,1)S(1)}, u32[]{:S(2)}, u32[]{:S(2)}) %collective-permute-start) | collective-permute-done | bytes 1835040 | tf_op jit(solution)/shard_map/ppermute | solution.py:56
  114.1 3.6 %pad_maximum_fusion = bf16[2048,896]{1,0:T(8,128)(2,1)} fusion(bf16[1024,896]{1,0:T(8,128)(2,1)S(1)} %collective-permute-done, bf16[1024,896]{1,0:T(8,128)(2,1)} %all-gather.6.cloned.1.call-done), kind=kLoop, calls=%fused_computation.6 | loop fusion | flops 7340032 | bytes 7340032 | tf_op jit(solution)/shard_map/concatenate | solution.py:56
  118.9 1.8 slice.45
  121.9 38.8 %collective-permute-done.2 = bf16[1024,896]{1,0:T(8,128)(2,1)S(1)} collective-permute-done((bf16[1024,896]{1,0:T(8,128)(2,1)S(1)}, bf16[1024,896]{1,0:T(8,128)(2,1)S(1)}, u32[]{:S(2)}, u32[]{:S(2)}) %collective-permute-start.2) | collective-permute-done | bytes 1835040 | tf_op jit(solution)/shard_map/ppermute | solution.py:72
  160.6 1.7 add_convert_fusion
  162.4 7.5 %fusion.7 = f32[4096,256]{1,0:T(8,128)} fusion(bf16[4096,896]{1,0:T(8,128)(2,1)} %all-gather.8.cloned.1.call-done, bf16[256,1792]{1,0:T(8,128)(2,1)S(1)} %copy-done.5), kind=kOutput, calls=%fused_computation.21 | convolution fusion | flops 1879048192 | bytes 11993088 | tf_op jit(solution)/shard_map/dot_general | solution.py:86
  169.9 5.6 %copy.29 = f32[256,2,2,8,128]{4,3,1,2,0:T(8,128)} copy(f32[256,2,2,8,128]{0,4,3,2,1:T(8,128)} %bitcast.35) | data formatting | bytes 8388608 | tf_op jit(solution)/shard_map/reshape | solution.py:92
  175.5 7.5 %fusion.4 = f32[4096,256]{1,0:T(8,128)} fusion(bf16[4096,896]{1,0:T(8,128)(2,1)} %all-gather.12.cloned.1.call-done, bf16[256,1792]{1,0:T(8,128)(2,1)S(1)} %copy-done.5), kind=kOutput, calls=%fused_computation.18 | convolution fusion | flops 1879048192 | bytes 11993088 | tf_op jit(solution)/shard_map/dot_general | solution.py:89
  183.0 5.6 %copy.30 = f32[256,2,8,2,128]{4,2,1,3,0:T(8,128)} copy(f32[256,2,8,2,128]{0,4,3,2,1:T(8,128)} %bitcast.36) | data formatting | bytes 8388608 | tf_op jit(solution)/shard_map/reshape | solution.py:94
  188.6 4.6 %bitcast_add_fusion = bf16[256,8,2,2,128]{4,1,3,2,0:T(8,128)(2,1)S(1)} fusion(f32[256,2,8,2,128]{4,2,1,3,0:T(8,128)} %copy.30, f32[256,2,2,8,128]{4,3,1,2,0:T(8,128)} %copy.29), kind=kLoop, calls=%fused_computation.4 | loop fusion | flops 2097152 | bytes 10485760 | tf_op jit(solution)/shard_map/add | solution.py:92
  193.8 2.0 copy.31
  195.8 4.6 %all-to-all-start = ((bf16[256,8,512]{2,0,1:T(8,128)(2,1)}), bf16[256,8,512]{2,0,1:T(8,128)(2,1)}, u32[]{:S(2)}, u32[]{:S(2)}) async-start(bf16[256,8,512]{2,0,1:T(8,128)(2,1)} %copy.31), calls=%async_computation | async-start | bytes 4194304 | tf_op jit(solution)/shard_map/all_to_all | solution.py:99
  200.4 7.1 %convolution_convert_fusion.1 = bf16[256,896]{1,0:T(8,128)(2,1)} fusion(bf16[256,4096]{0,1:T(8,128)(2,1)} %bitcast.32, bf16[4096,896]{1,0:T(8,128)(2,1)} %all-gather.8.cloned.1.call-done), kind=kOutput, calls=%fused_computation.12 | convolution fusion | flops 1879277568 | bytes 9895936 | tf_op jit(solution)/shard_map/dot_general | solution.py:102
  207.5 3.1 %convolution_convert_fusion = bf16[256,896]{1,0:T(8,128)(2,1)} fusion(bf16[256,4096]{0,1:T(8,128)(2,1)S(1)} %bitcast.30, bf16[4096,896]{1,0:T(8,128)(2,1)S(1)} %bitcast.28), kind=kOutput, calls=%fused_computation.11 | convolution fusion | flops 1879277568 | bytes 9895936 | tf_op jit(solution)/shard_map/dot_general | solution.py:103
  211.7 1.5 collective-permute-start.3
  213.2 2.1 pad_maximum_fusion.1
  215.3 9.1 %all-to-all-done = bf16[256,8,512]{2,0,1:T(8,128)(2,1)} async-done(((bf16[256,8,512]{2,0,1:T(8,128)(2,1)}), bf16[256,8,512]{2,0,1:T(8,128)(2,1)}, u32[]{:S(2)}, u32[]{:S(2)}) %all-to-all-start) | async-done | bytes 2097184 | tf_op jit(solution)/shard_map/all_to_all | solution.py:99
  224.5 2.7 %reduce_sum.30 = bf16[256,512]{1,0:T(8,128)(2,1)} reduce(bf16[256,8,512]{2,0,1:T(8,128)(2,1)} %all-to-all-done, bf16[]{:T(256)} %constant.8.clone.1), dimensions={1}, to_apply=%region_0.1 | reduce | flops 917504 | bytes 2359298 | tf_op jit(solution)/shard_map/reduce_sum | solution.py:14
  227.8 1.7 pad_maximum_fusion.3
  (62 shorter events, 10.2 us)
Async XLA Ops:
  8.0 65.3 %all-gather.6.cloned.1.call-start = ((), (), s32[]{:S(2)}) async-start(), calls=%async_computation.5 | async-start | bytes 2064384 | tf_op jit(solution)/shard_map/all_gather | solution.py:55
  9.8 107.9 %all-gather.10.cloned.1.call-start = ((), (), s32[]{:S(2)}) async-start(), calls=%async_computation.7 | async-start | bytes 4128768 | tf_op jit(solution)/shard_map/all_gather | solution.py:60
  9.9 8.9 %collective-permute-start.1 = (bf16[128,896]{1,0:T(8,128)(2,1)S(1)}, bf16[128,896]{1,0:T(8,128)(2,1)S(1)}, u32[]{:S(2)}, u32[]{:S(2)}) collective-permute-start(bf16[128,896]{1,0:T(8,128)(2,1)S(1)} %get-tuple-element.6), channel_id=1, source_target_pairs={{0,16},{16,0},{1,17},{17,1},{2,18},{18,2},{3,19},{19,3},{4,20},{20... | collective-permute-start | bytes 688136 | tf_op jit(solution)/shard_map/ppermute | solution.py:59
  19.7 98.7 %reduce-scatter.9.cloned.1.call-start = ((), (), s32[]{:S(2)}) async-start(), calls=%async_computation.11 | async-start | bytes 11010048 | tf_op jit(solution)/shard_map/reduce_scatter | solution.py:81
  56.4 3.1 %copy-start.5 = (bf16[256,1792]{1,0:T(8,128)(2,1)S(1)}, bf16[256,1792]{1,0:T(8,128)(2,1)}, u32[]{:S(2)}) copy-start(bf16[256,1792]{1,0:T(8,128)(2,1)} %param.5) | copy-start | bytes 2752516
  59.5 5.3 %copy-start = (bf16[256,2,8,2,128]{0,4,3,2,1:T(8,128)(2,1)}, bf16[256,2,8,2,128]{0,4,3,2,1:T(8,128)(2,1)S(1)}, u32[]{:S(2)}) copy-start(bf16[256,2,8,2,128]{0,4,3,2,1:T(8,128)(2,1)S(1)} %copy.36) | copy-start | bytes 6291460
  64.8 54.1 %reduce-scatter.5.cloned.1.call-start = ((), (), s32[]{:S(2)}) async-start(), calls=%async_computation.9 | async-start | bytes 11010048 | tf_op jit(solution)/shard_map/reduce_scatter | solution.py:76
  67.9 5.3 %copy-start.2 = (bf16[256,2,2,8,128]{0,4,3,2,1:T(8,128)(2,1)}, bf16[256,2,2,8,128]{0,4,3,2,1:T(8,128)(2,1)S(1)}, u32[]{:S(2)}) copy-start(bf16[256,2,2,8,128]{0,4,3,2,1:T(8,128)(2,1)S(1)} %copy.35) | copy-start | bytes 6291460
  73.2 89.2 %all-gather.8.cloned.1.call-start = ((), (), s32[]{:S(2)}) async-start(), calls=%async_computation.6 | async-start | bytes 11010048 | tf_op jit(solution)/shard_map/all_gather | solution.py:57
  73.3 40.8 %collective-permute-start = (bf16[1024,896]{1,0:T(8,128)(2,1)}, bf16[1024,896]{1,0:T(8,128)(2,1)S(1)}, u32[]{:S(2)}, u32[]{:S(2)}) collective-permute-start(bf16[1024,896]{1,0:T(8,128)(2,1)} %all-gather.6.cloned.1.call-done), channel_id=1, source_target_pairs={{0,16},{16,0},{1,17},{17,1},{2,18},{18,2},{3,19},{19,3},{4,20},{20... | collective-permute-start | bytes 5505032 | tf_op jit(solution)/shard_map/ppermute | solution.py:56
  117.7 57.9 %all-gather.12.cloned.1.call-start = ((), (), s32[]{:S(2)}) async-start(), calls=%async_computation.8 | async-start | bytes 11010048 | tf_op jit(solution)/shard_map/all_gather | solution.py:61
  118.3 92.4 %reduce-scatter.11.cloned.1.call-start = ((), (), s32[]{:S(2)}) async-start(), calls=%async_computation.12 | async-start | bytes 4128768 | tf_op jit(solution)/shard_map/reduce_scatter | solution.py:82
  118.8 109.0 %reduce-scatter.7.cloned.1.call-start = ((), (), s32[]{:S(2)}) async-start(), calls=%async_computation.10 | async-start | bytes 2064384 | tf_op jit(solution)/shard_map/reduce_scatter | solution.py:79
  118.9 41.7 %copy-start.3 = (bf16[2048,896]{1,0:T(8,128)(2,1)S(1)}, bf16[2048,896]{1,0:T(8,128)(2,1)}, u32[]{:S(2)}) copy-start(bf16[2048,896]{1,0:T(8,128)(2,1)} %reduce-scatter.5.cloned.1.call-done) | copy-start | bytes 11010052
  120.7 39.9 %collective-permute-start.2 = (bf16[1024,896]{1,0:T(8,128)(2,1)S(1)}, bf16[1024,896]{1,0:T(8,128)(2,1)S(1)}, u32[]{:S(2)}, u32[]{:S(2)}) collective-permute-start(bf16[1024,896]{1,0:T(8,128)(2,1)S(1)} %slice.45), channel_id=1, source_target_pairs={{0,16},{16,0},{1,17},{17,1},{2,18},{18,2},{3,19},{19,3},{4,20},{20... | collective-permute-start | bytes 5505032 | tf_op jit(solution)/shard_map/ppermute | solution.py:72
  195.8 11.7 %slice-start = ((s8[7340032]{0:T(1024)(128)(4,1)}), s8[3145728]{0:T(1024)(128)(4,1)S(1)}, s32[]{:S(2)}) async-start(s8[7340032]{0:T(1024)(128)(4,1)} %bitcast.27), calls=%async_computation.13 | async-start | bytes 6291456
  195.8 28.7 %all-to-all-start = ((bf16[256,8,512]{2,0,1:T(8,128)(2,1)}), bf16[256,8,512]{2,0,1:T(8,128)(2,1)}, u32[]{:S(2)}, u32[]{:S(2)}) async-start(bf16[256,8,512]{2,0,1:T(8,128)(2,1)} %copy.31), calls=%async_computation | async-start | bytes 4194304 | tf_op jit(solution)/shard_map/all_to_all | solution.py:99
  200.4 7.1 %slice-start.1 = ((s8[7340032]{0:T(1024)(128)(4,1)}), s8[4194304]{0:T(1024)(128)(4,1)S(1)}, s32[]{:S(2)}) async-start(s8[7340032]{0:T(1024)(128)(4,1)} %bitcast.27), calls=%async_computation.14 | async-start | bytes 8388608
  200.4 7.1 %copy-start.1 = (bf16[256,2,8,2,128]{0,4,3,2,1:T(8,128)(2,1)S(1)}, bf16[256,2,8,2,128]{0,4,3,2,1:T(8,128)(2,1)}, u32[]{:S(2)}) copy-start(bf16[256,2,8,2,128]{0,4,3,2,1:T(8,128)(2,1)} %copy-done) | copy-start | bytes 6291460
  210.7 17.0 %copy-start.4 = (bf16[256,896]{1,0:T(8,128)(2,1)S(1)}, bf16[256,896]{1,0:T(8,128)(2,1)}, u32[]{:S(2)}) copy-start(bf16[256,896]{1,0:T(8,128)(2,1)} %reduce-scatter.11.cloned.1.call-done) | copy-start | bytes 1376260
  211.7 16.0 %collective-permute-start.3 = (bf16[128,896]{1,0:T(8,128)(2,1)S(1)}, bf16[128,896]{1,0:T(8,128)(2,1)S(1)}, u32[]{:S(2)}, u32[]{:S(2)}) collective-permute-start(bf16[128,896]{1,0:T(8,128)(2,1)S(1)} %slice.47), channel_id=1, source_target_pairs={{0,16},{16,0},{1,17},{17,1},{2,18},{18,2},{3,19},{19,3},{4,20},{20... | collective-permute-start | bytes 688136 | tf_op jit(solution)/shard_map/ppermute | solution.py:72
Sparse Core Ops, SparseCore 0:
  11.2 42.8 all-gather.5
  56.4 47.0 all-gather.9
  117.8 20.3 all-gather.7
  139.8 24.9 all-gather.11
Sparse Core Ops, SparseCore 1:
  64.9 18.8 reduce-scatter.8
  86.2 22.8 reduce-scatter.4
  121.3 45.4 reduce-scatter.10
  169.4 41.6 reduce-scatter.6

commit v7 on v5

--- a/solution.py
+++ b/solution.py
@@ -12,6 +12,21 @@
 
 def sum_to_bf16(received, axis):
     return jnp.sum(received.astype(jnp.float32), axis=axis).astype(jnp.bfloat16)
+
+
+def ring_gather(x, axis, n):
+    fwd = [(i, (i + 1) % n) for i in range(n)]
+    bwd = [(i, (i - 1) % n) for i in range(n)]
+    from_minus, from_plus = [], []
+    m, p = x, x
+    for _ in range(n // 2 - 1):
+        m = lax.ppermute(m, axis, fwd)
+        p = lax.ppermute(p, axis, bwd)
+        from_minus.append(m)
+        from_plus.append(p)
+    h = x.shape[0] // 2
+    far = jnp.concatenate([lax.ppermute(m[:h], axis, fwd), lax.ppermute(p[h:], axis, bwd)], axis=0)
+    return jnp.concatenate([x, *from_plus, far, *from_minus[::-1]], axis=0)
 
 
 def shards(hidden, down_weight, cotangent, scores, prompt_ids):
@@ -45,14 +60,15 @@
     d_all = weighted.shape[1]
     own_first = lax.axis_index("yhi") == 0
     weighted_5 = weighted.reshape(tokens_here, n_z, n_yhi, n_core, rows_w)
-    weighted_p = (
-        jnp.where(own_first, weighted_5, jnp.flip(weighted_5, axis=2))
-        .transpose(0, 3, 1, 2, 4)
-        .reshape(tokens_here, d_all)
+    weighted_rel = jnp.where(own_first, weighted_5, jnp.flip(weighted_5, axis=2))
+    weighted_p = weighted_rel.transpose(0, 3, 1, 2, 4).reshape(tokens_here, d_all)
+    my_z = lax.axis_index("z")
+    weighted_g = (
+        jnp.roll(weighted_rel, -my_z, axis=1).transpose(0, 3, 1, 2, 4).reshape(tokens_here, d_all)
     )
     swap = [(0, 1), (1, 0)]
     gathered = jnp.concatenate([down_weight, lax.ppermute(down_weight, "yhi", swap)], axis=0)
-    gathered = lax.all_gather(gathered, "z", axis=0, tiled=True)
+    gathered = ring_gather(gathered, "z", n_z)
     gathered = lax.all_gather(gathered, "core", axis=0, tiled=True)
 
     scale = 1.0 / math.sqrt(tokens_here * n_sample)
@@ -75,11 +91,12 @@
     partial_value = partial_value.reshape(tokens_here, n_core, n_z, n_yhi, rows_w).transpose(
         0, 2, 3, 1, 4
     )
+    partial_value = jnp.roll(partial_value, my_z, axis=1)
     partial_value = jnp.where(own_first, partial_value, jnp.flip(partial_value, axis=2)).reshape(
         tokens_here, n_tensor, d_all // n_tensor
     )
     layer_out = sum_to_bf16(lax.all_to_all(partial_value, "tensor", 1, 1, tiled=True), 1)
-    hidden_grad = jnp.dot(weighted_p, gathered, preferred_element_type=jnp.float32).astype(
+    hidden_grad = jnp.dot(weighted_g, gathered, preferred_element_type=jnp.float32).astype(
         jnp.bfloat16
     )
     return (layer_out, hidden_grad, weight_grad)

time: 225 us -> 289 us (1.28)
  waiting for transfers between devices: 113 us -> 152 us
  local copies, waits for them, and re-layouts: 17.4 us -> 33.8 us
  starting transfers between devices: 11.9 us -> 19.4 us
    ppermute x0 -> x8, waiting for transfers between devices: none -> 60 us  [the longest x3 53.9 us: ring_gather(): m = lax.ppermute(m, axis, fwd)]
    all_gather x1 -> x0, waiting for transfers between devices: 40.2 us -> none  [shards(): gathered = lax.all_gather(gathered, 'z', axis=0, tiled=True)]
    reduce_scatter x1, waiting for transfers between devices: 29 us -> 53.9 us  [shards(): lax.psum_scatter(grad_part, 'z', scatter_dimension=0, tiled=True)]
    unnamed x17 -> x21, local copies, waits for them, and re-layouts: 3.09 us -> 13 us
    ppermute x0 -> x8, starting transfers between devices: none -> 8.44 us  [the longest x3 3.98 us: ring_gather(): m = lax.ppermute(m, axis, fwd)]
    transpose x1 -> x2, local copies, waits for them, and re-layouts: 3.01 us -> 7.27 us  [the longest x1 4.26 us: shards(): weighted_rel.transpose(0, 3, 1, 2, 4).reshape(tokens_here, d_all)]
    ppermute x1, waiting for transfers between devices: 10.8 us -> 7.29 us  [shards(): lax.ppermute(down_weight, 'yhi', swap)]
  transfers between devices with their start and end apart: 7 -> 14, of which waited for: 4 -> 8; matrix products, arithmetic and copies ran while one was open for 25% -> 17% of each run, Pallas kernels for 0% -> 0%
where the time goes in v7:
time: 289 us; the launch traced here: 286 us
  waiting for transfers between devices  152 us (53%)
  local copies, waits for them, and re-layouts  33.8 us (12%)
  matrix products  28.3 us (10%)
  blocking collectives  20.2 us (7%)
  starting transfers between devices  19.4 us (7%)
  other arithmetic  17.7 us (6%)
  between operations  14.6 us (5%)
    reduce_scatter x1, waiting for transfers between devices, shards(): lax.psum_scatter(grad_part, 'z', scatter_dimension=0, tiled=True)  53.9 us
    ppermute x3, waiting for transfers between devices, ring_gather(): m = lax.ppermute(m, axis, fwd)  53.9 us
    all_gather x1, waiting for transfers between devices, shards(): gathered = lax.all_gather(gathered, 'core', axis=0, tiled=True)  30.2 us
    unnamed x1, blocking collectives  20.2 us
    unnamed x21, local copies, waits for them, and re-layouts  13 us
    dot_general x1, matrix products, shards(): lax.dot_general(hidden, gathered, (((1,), (1,)), ((), ())), preferred_ele...  10.5 us
    dot_general x1, matrix products, shards(): lax.dot_general(weighted_p, hidden, (((0,), (0,)), ((), ())), preferred_e...  9.39 us
    dot_general x1, matrix products, shards(): jnp.dot(weighted_g, gathered, preferred_element_type=jnp.float32)  8.39 us
  transfers between devices with their start and end apart: 14, of which 8 were waited for; matrix products, arithmetic and copies ran while one was open for 17% of the time, Pallas kernels for 0%

profile of v7, /device:TPU:32, one launch (start us, length us, event | category | flops | bytes accessed | tf_op | source)
XLA Modules:
  0.0 286.1 jit_solution(12872564503551582761)
XLA Ops:
  7.3 1.3 dynamic-slice
  10.1 20.2 %all-reduce = s32[256]{0:T(256)S(1)} all-reduce(s32[256]{0:T(256)S(1)} %add_dynamic-update-slice_fusion), channel_id=2, replica_groups=mesh['z'=8,'yhi'=2,'core'=2,'tensor'=8] {'z','yhi','core'}, use_global_device_ids=true, to_apply=%add | all-reduce | flops 256 | bytes 2048
  30.4 3.3 %copy.26 = bf16[256,4096]{0,1:T(8,128)(2,1)S(1)} copy(bf16[256,4096]{1,0:T(8,128)(2,1)} %param.9) | data formatting | bytes 4194304 | tf_op args[2]
  34.6 1.8 multiply_convert_fusion.1
  36.4 3.5 %copy.28 = bf16[256,8,2,2,128]{4,1,3,2,0:T(8,128)(2,1)S(1)} copy(bf16[256,8,2,2,128]{0,4,3,2,1:T(8,128)(2,1)} %bitcast.20) | data formatting | bytes 4194304 | tf_op jit(solution)/shard_map/reshape | solution.py:62
  39.9 1.9 fusion.10
  41.8 4.3 %copy.30 = bf16[256,2,8,2,128]{0,4,3,2,1:T(8,128)(2,1)} copy(bf16[256,2,8,2,128]{4,2,1,3,0:T(8,128)(2,1)} %fusion.10) | data formatting | bytes 4194304 | tf_op jit(solution)/shard_map/transpose | solution.py:64
  46.1 9.4 %multiply_convert_fusion = bf16[4096,1792]{1,0:T(8,128)(2,1)} fusion(bf16[256,4096]{0,1:T(8,128)(2,1)} %bitcast.23, bf16[256,1792]{1,0:T(8,128)(2,1)S(1)} %copy-done), kind=kOutput, calls=%fused_computation | convolution fusion | flops 3772776448 | bytes 17694720 | tf_op jit(solution)/shard_map/dot_general | solution.py:76
  56.5 2.4 collective-permute-start
  59.7 7.3 %collective-permute-done = bf16[128,1792]{1,0:T(8,128)(2,1)S(1)} collective-permute-done((bf16[128,1792]{1,0:T(8,128)(2,1)S(1)}, bf16[128,1792]{1,0:T(8,128)(2,1)S(1)}, u32[]{:S(2)}, u32[]{:S(2)}) %collective-permute-start) | collective-permute-done | bytes 458784 | tf_op jit(solution)/shard_map/ppermute | solution.py:70
  69.8 18.0 %collective-permute-done.4 = bf16[256,1792]{1,0:T(8,128)(2,1)S(1)} collective-permute-done((bf16[256,1792]{1,0:T(8,128)(2,1)S(1)}, bf16[256,1792]{1,0:T(8,128)(2,1)S(1)}, u32[]{:S(2)}, u32[]{:S(2)}) %collective-permute-start.4) | collective-permute-done | bytes 917536 | tf_op jit(solution)/shard_map/ppermute | solution.py:23
  87.8 1.5 collective-permute-start.5
  89.9 18.5 %collective-permute-done.5 = bf16[256,1792]{1,0:T(8,128)(2,1)S(1)} collective-permute-done((bf16[256,1792]{1,0:T(8,128)(2,1)S(1)}, bf16[256,1792]{1,0:T(8,128)(2,1)S(1)}, u32[]{:S(2)}, u32[]{:S(2)}) %collective-permute-start.5) | collective-permute-done | bytes 917536 | tf_op jit(solution)/shard_map/ppermute | solution.py:23
  108.3 1.5 collective-permute-start.6
  111.4 17.4 %collective-permute-done.6 = bf16[256,1792]{1,0:T(8,128)(2,1)S(1)} collective-permute-done((bf16[256,1792]{1,0:T(8,128)(2,1)S(1)}, bf16[256,1792]{1,0:T(8,128)(2,1)S(1)}, u32[]{:S(2)}, u32[]{:S(2)}) %collective-permute-start.6) | collective-permute-done | bytes 917536 | tf_op jit(solution)/shard_map/ppermute | solution.py:23
  128.8 1.6 collective-permute-start.7
  133.2 4.2 %collective-permute-done.7 = bf16[128,1792]{1,0:T(8,128)(2,1)S(1)} collective-permute-done((bf16[128,1792]{1,0:T(8,128)(2,1)S(1)}, bf16[128,1792]{1,0:T(8,128)(2,1)S(1)}, u32[]{:S(2)}, u32[]{:S(2)}) %collective-permute-start.7) | collective-permute-done | bytes 458784 | tf_op jit(solution)/shard_map/ppermute | solution.py:28
  138.2 1.9 collective-permute-done.8
  144.7 30.2 %all-gather.3.cloned.1.call-done = bf16[4096,1792]{1,0:T(8,128)(2,1)} async-done(((bf16[2048,1792]{1,0:T(8,128)(2,1)}), bf16[4096,1792]{1,0:T(8,128)(2,1)}) %all-gather.3.cloned.1.call-update) | async-done | bytes 14680080 | tf_op jit(solution)/shard_map/all_gather | solution.py:72
  175.0 10.5 %convolution_convert_fusion = bf16[4096,256]{1,0:T(8,128)(2,1)} fusion(bf16[4096,1792]{1,0:T(8,128)(2,1)} %all-gather.3.cloned.1.call-done, bf16[256,1792]{1,0:T(8,128)(2,1)S(1)} %copy-done), kind=kOutput, calls=%fused_computation.1 | convolution fusion | flops 3759144960 | bytes 17694720 | tf_op jit(solution)/shard_map/dot_general | solution.py:88
  185.5 4.6 %copy.24 = bf16[256,2,8,2,128]{4,2,1,3,0:T(8,128)(2,1)} copy(bf16[256,2,8,2,128]{0,4,3,2,1:T(8,128)(2,1)} %bitcast.24) | data formatting | bytes 4194304 | tf_op jit(solution)/shard_map/reshape | solution.py:91
  190.1 4.0 %fusion.2 = bf16[256,8,2,2,128]{4,1,3,2,0:T(8,128)(2,1)S(1)} fusion(s32[]{:T(128)S(6)} %select_n.43, bf16[256,8,2,2,128]{4,1,3,2,0:T(8,128)(2,1)} %bitcast.21), kind=kLoop, calls=%fused_computation.12 | loop fusion | flops 4194304 | bytes 4194308 | tf_op jit(solution)/shard_map/jit(_roll_dynamic)/concatenate | solution.py:94
  194.6 2.0 copy.25
  196.6 5.2 %all-to-all-start = ((bf16[256,8,512]{2,0,1:T(8,128)(2,1)}), bf16[256,8,512]{2,0,1:T(8,128)(2,1)}, u32[]{:S(2)}, u32[]{:S(2)}) async-start(bf16[256,8,512]{2,0,1:T(8,128)(2,1)} %copy.25), calls=%async_computation | async-start | bytes 4194304 | tf_op jit(solution)/shard_map/all_to_all | solution.py:98
  202.4 2.8 fusion.1
  205.2 3.0 %copy.29 = bf16[256,2,8,2,128]{0,4,3,2,1:T(8,128)(2,1)S(1)} copy(bf16[256,2,8,2,128]{4,2,1,3,0:T(8,128)(2,1)} %fusion.1) | data formatting | bytes 4194304 | tf_op jit(solution)/shard_map/transpose | solution.py:67
  208.2 53.9 %reduce-scatter.5.cloned.1.call-done = bf16[256,1792]{1,0:T(8,128)(2,1)} async-done(((bf16[2048,1792]{1,0:T(8,128)(2,1)}), bf16[256,1792]{1,0:T(8,128)(2,1)}) %reduce-scatter.5.cloned.1.call-update) | async-done | bytes 917520 | tf_op jit(solution)/shard_map/reduce_scatter | solution.py:82
  262.1 1.0 slice.29
  263.2 3.3 %collective-permute-start.9 = (bf16[128,1792]{1,0:T(8,128)(2,1)S(1)}, bf16[128,1792]{1,0:T(8,128)(2,1)}, u32[]{:S(2)}, u32[]{:S(2)}) collective-permute-start(bf16[128,1792]{1,0:T(8,128)(2,1)S(1)} %slice.29), channel_id=1, source_target_pairs={{0,16},{16,0},{1,17},{17,1},{2,18},{18,2},{3,19},{19,3},{4,20},{20... | collective-permute-start | bytes 1376264 | tf_op jit(solution)/shard_map/ppermute | solution.py:85
  266.5 8.4 %convolution_convert_fusion.1 = bf16[256,1792]{1,0:T(8,128)(2,1)} fusion(bf16[256,4096]{0,1:T(8,128)(2,1)S(1)} %bitcast.19, bf16[4096,1792]{1,0:T(8,128)(2,1)} %all-gather.3.cloned.1.call-done), kind=kOutput, calls=%fused_computation.9 | convolution fusion | flops 3758555136 | bytes 17694720 | tf_op jit(solution)/shard_map/dot_general | solution.py:99
  274.9 2.7 reduce_sum.30
  277.6 2.0 add_convert_fusion
  (55 shorter events, 18.1 us)
Async XLA Ops:
  7.2 38.9 %copy-start = (bf16[256,1792]{1,0:T(8,128)(2,1)S(1)}, bf16[256,1792]{1,0:T(8,128)(2,1)}, u32[]{:S(2)}) copy-start(bf16[256,1792]{1,0:T(8,128)(2,1)} %param.7) | copy-start | bytes 2752516
  7.2 27.1 %copy-start.3 = (s32[4]{0:T(128)S(1)}, s32[4]{0:T(128)}, u32[]{:S(2)}) copy-start(s32[4]{0:T(128)} %param.11) | copy-start | bytes 52
  7.2 27.3 %copy-start.4 = (s32[4]{0:T(128)S(1)}, s32[4]{0:T(128)}, u32[]{:S(2)}) copy-start(s32[4]{0:T(128)} %param.10) | copy-start | bytes 52
  7.2 136.8 %reduce-scatter.3.cloned.1.call-start = ((), (), s32[]{:S(2)}) async-start(), calls=%async_computation.4 | async-start | bytes 22020096 | tf_op jit(solution)/shard_map/reduce_scatter | solution.py:81
  55.4 1.0 copy-start.2
  55.5 119.5 %all-gather.3.cloned.1.call-start = ((), (), s32[]{:S(2)}) async-start(), calls=%async_computation.3 | async-start | bytes 22020096 | tf_op jit(solution)/shard_map/all_gather | solution.py:72
  56.5 10.5 %collective-permute-start = (bf16[128,1792]{1,0:T(8,128)(2,1)S(1)}, bf16[128,1792]{1,0:T(8,128)(2,1)S(1)}, u32[]{:S(2)}, u32[]{:S(2)}) collective-permute-start(bf16[128,1792]{1,0:T(8,128)(2,1)S(1)} %copy-done.2), channel_id=1, source_target_pairs={{0,16},{16,0},{1,17},{17,1},{2,18},{18,2},{3,19},{19,3},{4,20},{20... | collective-permute-start | bytes 1376264 | tf_op jit(solution)/shard_map/ppermute | solution.py:70
  67.8 20.0 %collective-permute-start.4 = (bf16[256,1792]{1,0:T(8,128)(2,1)S(1)}, bf16[256,1792]{1,0:T(8,128)(2,1)S(1)}, u32[]{:S(2)}, u32[]{:S(2)}) collective-permute-start(bf16[256,1792]{1,0:T(8,128)(2,1)S(1)} %get-tuple-element.4), channel_id=1, source_target_pairs={{0,32},{32,64},{64,96},{96,128},{128,160},{160,192},{192,224},{224... | collective-permute-start | bytes 2752520 | tf_op jit(solution)/shard_map/ppermute | solution.py:23
  68.8 20.5 %collective-permute-start.1 = (bf16[256,1792]{1,0:T(8,128)(2,1)S(1)}, bf16[256,1792]{1,0:T(8,128)(2,1)S(1)}, u32[]{:S(2)}, u32[]{:S(2)}) collective-permute-start(bf16[256,1792]{1,0:T(8,128)(2,1)S(1)} %get-tuple-element.4), channel_id=1, source_target_pairs={{0,224},{32,0},{64,32},{96,64},{128,96},{160,128},{192,160},{224,1... | collective-permute-start | bytes 2752520 | tf_op jit(solution)/shard_map/ppermute | solution.py:24
  87.8 20.5 %collective-permute-start.5 = (bf16[256,1792]{1,0:T(8,128)(2,1)S(1)}, bf16[256,1792]{1,0:T(8,128)(2,1)S(1)}, u32[]{:S(2)}, u32[]{:S(2)}) collective-permute-start(bf16[256,1792]{1,0:T(8,128)(2,1)S(1)} %collective-permute-done.4), channel_id=1, source_target_pairs={{0,32},{32,64},{64,96},{96,128},{128,160},{160,192},{192,224},{224... | collective-permute-start | bytes 2752520 | tf_op jit(solution)/shard_map/ppermute | solution.py:23
  89.3 20.5 %collective-permute-start.2 = (bf16[256,1792]{1,0:T(8,128)(2,1)S(1)}, bf16[256,1792]{1,0:T(8,128)(2,1)S(1)}, u32[]{:S(2)}, u32[]{:S(2)}) collective-permute-start(bf16[256,1792]{1,0:T(8,128)(2,1)S(1)} %collective-permute-done.1), channel_id=1, source_target_pairs={{0,224},{32,0},{64,32},{96,64},{128,96},{160,128},{192,160},{224,1... | collective-permute-start | bytes 2752520 | tf_op jit(solution)/shard_map/ppermute | solution.py:24
  108.3 20.4 %collective-permute-start.6 = (bf16[256,1792]{1,0:T(8,128)(2,1)S(1)}, bf16[256,1792]{1,0:T(8,128)(2,1)S(1)}, u32[]{:S(2)}, u32[]{:S(2)}) collective-permute-start(bf16[256,1792]{1,0:T(8,128)(2,1)S(1)} %collective-permute-done.5), channel_id=1, source_target_pairs={{0,32},{32,64},{64,96},{96,128},{128,160},{160,192},{192,224},{224... | collective-permute-start | bytes 2752520 | tf_op jit(solution)/shard_map/ppermute | solution.py:23
  109.8 21.5 %collective-permute-start.3 = (bf16[256,1792]{1,0:T(8,128)(2,1)S(1)}, bf16[256,1792]{1,0:T(8,128)(2,1)S(1)}, u32[]{:S(2)}, u32[]{:S(2)}) collective-permute-start(bf16[256,1792]{1,0:T(8,128)(2,1)S(1)} %collective-permute-done.2), channel_id=1, source_target_pairs={{0,224},{32,0},{64,32},{96,64},{128,96},{160,128},{192,160},{224,1... | collective-permute-start | bytes 2752520 | tf_op jit(solution)/shard_map/ppermute | solution.py:24
  128.8 8.6 %collective-permute-start.7 = (bf16[128,1792]{1,0:T(8,128)(2,1)S(1)}, bf16[128,1792]{1,0:T(8,128)(2,1)S(1)}, u32[]{:S(2)}, u32[]{:S(2)}) collective-permute-start(bf16[128,1792]{1,0:T(8,128)(2,1)S(1)} %slice.24), channel_id=1, source_target_pairs={{0,32},{32,64},{64,96},{96,128},{128,160},{160,192},{192,224},{224... | collective-permute-start | bytes 1376264 | tf_op jit(solution)/shard_map/ppermute | solution.py:28
  131.4 8.7 %collective-permute-start.8 = (bf16[128,1792]{1,0:T(8,128)(2,1)S(1)}, bf16[128,1792]{1,0:T(8,128)(2,1)S(1)}, u32[]{:S(2)}, u32[]{:S(2)}) collective-permute-start(bf16[128,1792]{1,0:T(8,128)(2,1)S(1)} %slice.25), channel_id=1, source_target_pairs={{0,224},{32,0},{64,32},{96,64},{128,96},{160,128},{192,160},{224,1... | collective-permute-start | bytes 1376264 | tf_op jit(solution)/shard_map/ppermute | solution.py:28
  144.0 118.1 %reduce-scatter.5.cloned.1.call-start = ((), (), s32[]{:S(2)}) async-start(), calls=%async_computation.5 | async-start | bytes 8257536 | tf_op jit(solution)/shard_map/reduce_scatter | solution.py:82
  196.6 78.3 %all-to-all-start = ((bf16[256,8,512]{2,0,1:T(8,128)(2,1)}), bf16[256,8,512]{2,0,1:T(8,128)(2,1)}, u32[]{:S(2)}, u32[]{:S(2)}) async-start(bf16[256,8,512]{2,0,1:T(8,128)(2,1)} %copy.25), calls=%async_computation | async-start | bytes 4194304 | tf_op jit(solution)/shard_map/all_to_all | solution.py:98
  263.2 14.4 %collective-permute-start.9 = (bf16[128,1792]{1,0:T(8,128)(2,1)S(1)}, bf16[128,1792]{1,0:T(8,128)(2,1)}, u32[]{:S(2)}, u32[]{:S(2)}) collective-permute-start(bf16[128,1792]{1,0:T(8,128)(2,1)S(1)} %slice.29), channel_id=1, source_target_pairs={{0,16},{16,0},{1,17},{17,1},{2,18},{18,2},{3,19},{19,3},{4,20},{20... | collective-permute-start | bytes 1376264 | tf_op jit(solution)/shard_map/ppermute | solution.py:85
  266.5 13.1 %copy-start.1 = (bf16[256,1792]{1,0:T(8,128)(2,1)S(1)}, bf16[256,1792]{1,0:T(8,128)(2,1)}, u32[]{:S(2)}) copy-start(bf16[256,1792]{1,0:T(8,128)(2,1)} %param.7) | copy-start | bytes 2752516
Sparse Core Ops, SparseCore 0:
  55.6 27.6 reduce-scatter.2
  144.1 30.8 all-gather.2
  177.5 84.5 reduce-scatter.4

commit v8 on v4

--- a/solution.py
+++ b/solution.py
@@ -51,8 +51,11 @@
         .reshape(tokens_here, d_all)
     )
     swap = [(0, 1), (1, 0)]
-    gathered = lax.all_gather(down_weight, "z", axis=0, tiled=True)
-    gathered = jnp.concatenate([gathered, lax.ppermute(gathered, "yhi", swap)], axis=0)
+    gathered_own = lax.all_gather(down_weight, "z", axis=0, tiled=True)
+    gathered_partner = lax.all_gather(
+        lax.ppermute(down_weight, "yhi", swap), "z", axis=0, tiled=True
+    )
+    gathered = jnp.concatenate([gathered_own, gathered_partner], axis=0)
     gathered = lax.all_gather(gathered, "core", axis=0, tiled=True)
 
     scale = 1.0 / math.sqrt(tokens_here * n_sample)
@@ -64,11 +67,11 @@
     ).astype(jnp.bfloat16)
     grad_part = lax.psum_scatter(grad_part, "core", scatter_dimension=0, tiled=True)
     half = grad_part.shape[0] // n_yhi
-    grad_part = (
-        grad_part[:half].astype(jnp.float32)
-        + lax.ppermute(grad_part[half:], "yhi", swap).astype(jnp.float32)
+    theirs = lax.psum_scatter(grad_part[half:], "z", scatter_dimension=0, tiled=True)
+    mine = lax.psum_scatter(grad_part[:half], "z", scatter_dimension=0, tiled=True)
+    weight_grad = (
+        mine.astype(jnp.float32) + lax.ppermute(theirs, "yhi", swap).astype(jnp.float32)
     ).astype(jnp.bfloat16)
-    weight_grad = lax.psum_scatter(grad_part, "z", scatter_dimension=0, tiled=True)
 
     partial_value = lax.dot_general(
         hidden, gathered, (((1,), (1,)), ((), ())), preferred_element_type=jnp.float32

time: 302 us -> 239 us (0.79)
  waiting for transfers between devices: 183 us -> 112 us
  local copies, waits for them, and re-layouts: 19.9 us -> 26.2 us
  other arithmetic: 19.2 us -> 22.8 us
    ppermute x2, waiting for transfers between devices: 157 us -> 10.8 us  [the longest x1 10.8 us: shards(): lax.ppermute(down_weight, 'yhi', swap)]
    all_gather x1 -> x2, waiting for transfers between devices: 8.86 us -> 39.3 us  [the longest x1 39.2 us: shards(): lax.all_gather(lax.ppermute(down_weight, 'yhi', swap), 'z', axis=0, tiled...]
    all_gather x1, waiting for transfers between devices: 0.03 us -> 25.2 us  [shards(): gathered = lax.all_gather(gathered, 'core', axis=0, tiled=True)]
    reduce_scatter x1 -> x2, waiting for transfers between devices: 0.01 us -> 19.5 us  [the longest x1 19.5 us: shards(): lax.psum_scatter(grad_part[:half], 'z', scatter_dimension=0, tiled=True)]
    slice x1, local copies, waits for them, and re-layouts: 2.43 us -> 6.56 us  [shards(): grad_part[:half]]
    unnamed x13 -> x7, local copies, waits for them, and re-layouts: 3.89 us -> 6.23 us
  transfers between devices with their start and end apart: 7 -> 9, of which waited for: 4 -> 5; matrix products, arithmetic and copies ran while one was open for 22% -> 31% of each run, Pallas kernels for 0% -> 0%
where the time goes in v8:
time: 239 us; the launch traced here: 236 us
  waiting for transfers between devices  112 us (47%)
  matrix products  26.3 us (11%)
  local copies, waits for them, and re-layouts  26.2 us (11%)
  other arithmetic  22.8 us (10%)
  blocking collectives  20.8 us (9%)
  between operations  16 us (7%)
  starting transfers between devices  11.7 us (5%)
    all_gather x1, waiting for transfers between devices, shards(): lax.all_gather(lax.ppermute(down_weight, 'yhi', swap), 'z', axis=0, tiled...  39.2 us
    all_gather x1, waiting for transfers between devices, shards(): gathered = lax.all_gather(gathered, 'core', axis=0, tiled=True)  25.2 us
    unnamed x1, blocking collectives  20.8 us
    reduce_scatter x1, waiting for transfers between devices, shards(): lax.psum_scatter(grad_part[:half], 'z', scatter_dimension=0, tiled=True)  19.5 us
    all_to_all x1, waiting for transfers between devices, shards(): lax.all_to_all(partial_value, 'tensor', 1, 1, tiled=True)  16.4 us
    ppermute x1, waiting for transfers between devices, shards(): lax.ppermute(down_weight, 'yhi', swap)  10.8 us
    dot_general x1, matrix products, shards(): lax.dot_general(hidden, gathered, (((1,), (1,)), ((), ())), preferred_ele...  10.7 us
    dot_general x1, matrix products, shards(): jnp.dot(weighted_p, gathered, preferred_element_type=jnp.float32)  8.31 us
  transfers between devices with their start and end apart: 9, of which 5 were waited for; matrix products, arithmetic and copies ran while one was open for 31% of the time, Pallas kernels for 0%

profile of v8, /device:TPU:32, one launch (start us, length us, event | category | flops | bytes accessed | tf_op | source)
XLA Modules:
  0.0 236.2 jit_solution(4594835262944763769)
XLA Ops:
  8.1 0.7 all-gather.5.cloned.1.call-update
  8.8 3.3 %collective-permute-start = (bf16[128,1792]{1,0:T(8,128)(2,1)}, bf16[128,1792]{1,0:T(8,128)(2,1)S(1)}, u32[]{:S(2)}, u32[]{:S(2)}) collective-permute-start(bf16[128,1792]{1,0:T(8,128)(2,1)} %param.6), channel_id=1, source_target_pairs={{0,16},{16,0},{1,17},{17,1},{2,18},{18,2},{3,19},{19,3},{4,20},{20... | collective-permute-start | bytes 1376264 | tf_op jit(solution)/shard_map/ppermute | solution.py:56
  12.1 10.8 %collective-permute-done = bf16[128,1792]{1,0:T(8,128)(2,1)S(1)} collective-permute-done((bf16[128,1792]{1,0:T(8,128)(2,1)}, bf16[128,1792]{1,0:T(8,128)(2,1)S(1)}, u32[]{:S(2)}, u32[]{:S(2)}) %collective-permute-start) | collective-permute-done | bytes 458784 | tf_op jit(solution)/shard_map/ppermute | solution.py:56
  22.9 0.8 copy-done.1
  23.7 1.3 dynamic-slice
  25.6 0.8 add_dynamic-update-slice_fusion
  26.5 20.8 %all-reduce = s32[256]{0:T(256)S(1)} all-reduce(s32[256]{0:T(256)S(1)} %add_dynamic-update-slice_fusion), channel_id=2, replica_groups=mesh['z'=8,'yhi'=2,'core'=2,'tensor'=8] {'z','yhi','core'}, use_global_device_ids=true, to_apply=%add | all-reduce | flops 256 | bytes 2048
  48.0 0.8 select_reduce_fusion
  48.9 0.7 exponential_multiply_fusion
  49.7 4.2 %copy.24 = bf16[256,4096]{0,1:T(8,128)(2,1)} copy(bf16[256,4096]{1,0:T(8,128)(2,1)} %param.7) | data formatting | bytes 4194304 | tf_op args[2]
  53.9 2.0 multiply_convert_fusion.1
  55.9 3.2 %copy.26 = bf16[256,8,2,2,128]{4,1,3,2,0:T(8,128)(2,1)} copy(bf16[256,8,2,2,128]{0,4,3,2,1:T(8,128)(2,1)S(1)} %bitcast.18) | data formatting | bytes 4194304 | tf_op jit(solution)/shard_map/reshape | solution.py:47
  59.1 4.1 %fusion = bf16[256,2,2,8,128]{4,3,1,2,0:T(8,128)(2,1)} fusion(bf16[256,8,2,2,128]{4,1,3,2,0:T(8,128)(2,1)} %copy.26, pred[]{:T(512)S(6)} %eq.31), kind=kLoop, calls=%fused_computation.7 | loop fusion | flops 1048576 | bytes 4194305 | tf_op jit(solution)/shard_map/transpose | solution.py:50
  63.1 3.0 %copy.27 = bf16[256,2,2,8,128]{0,4,3,2,1:T(8,128)(2,1)S(1)} copy(bf16[256,2,2,8,128]{4,3,1,2,0:T(8,128)(2,1)} %fusion) | data formatting | bytes 4194304 | tf_op jit(solution)/shard_map/transpose | solution.py:50
  66.2 7.3 %multiply_convert_fusion = bf16[4096,1792]{1,0:T(8,128)(2,1)} fusion(bf16[256,4096]{0,1:T(8,128)(2,1)S(1)} %bitcast.16, bf16[256,1792]{1,0:T(8,128)(2,1)S(1)} %copy-done), kind=kOutput, calls=%fused_computation | convolution fusion | flops 3772776448 | bytes 17694720 | tf_op jit(solution)/shard_map/dot_general | solution.py:63
  73.5 39.2 %all-gather.7.cloned.1.call-done = bf16[1024,1792]{1,0:T(8,128)(2,1)} async-done(((bf16[128,1792]{1,0:T(8,128)(2,1)}), bf16[1024,1792]{1,0:T(8,128)(2,1)}) %all-gather.7.cloned.1.call-update) | async-done | bytes 3670032 | tf_op jit(solution)/shard_map/all_gather | solution.py:55
  112.8 6.6 %pad_maximum_fusion = bf16[2048,1792]{1,0:T(8,128)(2,1)} fusion(bf16[1024,1792]{1,0:T(8,128)(2,1)} %all-gather.7.cloned.1.call-done, bf16[1024,1792]{1,0:T(8,128)(2,1)} %all-gather.5.cloned.1.call-done), kind=kLoop, calls=%fused_computation.1 | loop fusion | flops 14680064 | bytes 14680064 | tf_op jit(solution)/shard_map/concatenate | solution.py:58
  119.5 6.6 %fusion.2 = (bf16[1024,1792]{1,0:T(8,128)(2,1)}, bf16[1024,1792]{1,0:T(8,128)(2,1)}) fusion(bf16[2048,1792]{1,0:T(8,128)(2,1)} %reduce-scatter.4.cloned.1.call-done), kind=kLoop, calls=%fused_computation.19 | loop fusion | bytes 14680064 | tf_op jit(solution)/shard_map/slice | solution.py:71
  126.1 0.2 reduce-scatter.6.cloned.1.call-start
  126.3 0.3 reduce-scatter.6.cloned.1.call-update
  126.7 25.2 %all-gather.9.cloned.1.call-done = bf16[4096,1792]{1,0:T(8,128)(2,1)} async-done(((bf16[2048,1792]{1,0:T(8,128)(2,1)}), bf16[4096,1792]{1,0:T(8,128)(2,1)}) %all-gather.9.cloned.1.call-update) | async-done | bytes 14680080 | tf_op jit(solution)/shard_map/all_gather | solution.py:59
  151.9 10.7 %convolution_convert_fusion = bf16[4096,256]{1,0:T(8,128)(2,1)} fusion(bf16[4096,1792]{1,0:T(8,128)(2,1)} %all-gather.9.cloned.1.call-done, bf16[256,1792]{1,0:T(8,128)(2,1)S(1)} %copy-done), kind=kOutput, calls=%fused_computation.2 | convolution fusion | flops 3759144960 | bytes 17694720 | tf_op jit(solution)/shard_map/dot_general | solution.py:76
  162.6 4.7 %copy.22 = bf16[256,2,2,8,128]{4,3,1,2,0:T(8,128)(2,1)} copy(bf16[256,2,2,8,128]{0,4,3,2,1:T(8,128)(2,1)} %bitcast.21) | data formatting | bytes 4194304 | tf_op jit(solution)/shard_map/reshape | solution.py:79
  167.3 2.8 %reverse_select_fusion.1 = bf16[256,8,2,2,128]{4,1,3,2,0:T(8,128)(2,1)S(1)} fusion(bf16[256,8,2,2,128]{4,1,3,2,0:T(8,128)(2,1)} %bitcast.19, pred[]{:T(512)S(6)} %eq.31), kind=kLoop, calls=%fused_computation.5 | loop fusion | flops 1048576 | bytes 4194305 | tf_op jit(solution)/shard_map/jit(_where)/select_n | solution.py:82
  170.1 2.1 copy.23
  172.2 5.2 %all-to-all-start = ((bf16[256,8,512]{2,0,1:T(8,128)(2,1)}), bf16[256,8,512]{2,0,1:T(8,128)(2,1)}, u32[]{:S(2)}, u32[]{:S(2)}) async-start(bf16[256,8,512]{2,0,1:T(8,128)(2,1)} %copy.23), calls=%async_computation | async-start | bytes 4194304 | tf_op jit(solution)/shard_map/all_to_all | solution.py:85
  177.4 2.8 %collective-permute-start.1 = (bf16[128,1792]{1,0:T(8,128)(2,1)}, bf16[128,1792]{1,0:T(8,128)(2,1)S(1)}, u32[]{:S(2)}, u32[]{:S(2)}) collective-permute-start(bf16[128,1792]{1,0:T(8,128)(2,1)} %reduce-scatter.8.cloned.1.call-done), channel_id=1, source_target_pairs={{0,16},{16,0},{1,17},{17,1},{2,18},{18,2},{3,19},{19,3},{4,20},{20... | collective-permute-start | bytes 1376264 | tf_op jit(solution)/shard_map/ppermute | solution.py:73
  180.2 8.3 %convolution_convert_fusion.1 = bf16[256,1792]{1,0:T(8,128)(2,1)} fusion(bf16[256,4096]{0,1:T(8,128)(2,1)S(1)} %bitcast.17, bf16[4096,1792]{1,0:T(8,128)(2,1)} %all-gather.9.cloned.1.call-done), kind=kOutput, calls=%fused_computation.6 | convolution fusion | flops 3758555136 | bytes 17694720 | tf_op jit(solution)/shard_map/dot_general | solution.py:86
  188.5 16.4 %all-to-all-done = bf16[256,8,512]{2,0,1:T(8,128)(2,1)} async-done(((bf16[256,8,512]{2,0,1:T(8,128)(2,1)}), bf16[256,8,512]{2,0,1:T(8,128)(2,1)}, u32[]{:S(2)}, u32[]{:S(2)}) %all-to-all-start) | async-done | bytes 2097184 | tf_op jit(solution)/shard_map/all_to_all | solution.py:85
  204.9 2.7 %reduce_sum.30 = bf16[256,512]{1,0:T(8,128)(2,1)} reduce(bf16[256,8,512]{2,0,1:T(8,128)(2,1)} %all-to-all-done, bf16[]{:T(256)} %constant.8.clone.1), dimensions={1}, to_apply=%region_0.1 | reduce | flops 917504 | bytes 2359298 | tf_op jit(solution)/shard_map/reduce_sum | solution.py:14
  207.6 19.5 %reduce-scatter.6.cloned.1.call-done = bf16[128,1792]{1,0:T(8,128)(2,1)} async-done(((bf16[1024,1792]{1,0:T(8,128)(2,1)}), bf16[128,1792]{1,0:T(8,128)(2,1)}) %reduce-scatter.6.cloned.1.call-update) | async-done | bytes 458768 | tf_op jit(solution)/shard_map/reduce_scatter | solution.py:71
  227.1 1.9 add_convert_fusion
  (27 shorter events, 1.2 us)
Async XLA Ops:
  8.0 58.2 %copy-start = (bf16[256,1792]{1,0:T(8,128)(2,1)S(1)}, bf16[256,1792]{1,0:T(8,128)(2,1)}, u32[]{:S(2)}) copy-start(bf16[256,1792]{1,0:T(8,128)(2,1)} %param.5) | copy-start | bytes 2752516
  8.0 65.5 %all-gather.5.cloned.1.call-start = ((), (), s32[]{:S(2)}) async-start(), calls=%async_computation.4 | async-start | bytes 4128768 | tf_op jit(solution)/shard_map/all_gather | solution.py:54
  8.7 104.0 %all-gather.7.cloned.1.call-start = ((), (), s32[]{:S(2)}) async-start(), calls=%async_computation.5 | async-start | bytes 4128768 | tf_op jit(solution)/shard_map/all_gather | solution.py:55
  8.8 14.1 %collective-permute-start = (bf16[128,1792]{1,0:T(8,128)(2,1)}, bf16[128,1792]{1,0:T(8,128)(2,1)S(1)}, u32[]{:S(2)}, u32[]{:S(2)}) collective-permute-start(bf16[128,1792]{1,0:T(8,128)(2,1)} %param.6), channel_id=1, source_target_pairs={{0,16},{16,0},{1,17},{17,1},{2,18},{18,2},{3,19},{19,3},{4,20},{20... | collective-permute-start | bytes 1376264 | tf_op jit(solution)/shard_map/ppermute | solution.py:56
  22.9 0.8 copy-start.1
  23.6 95.9 %reduce-scatter.4.cloned.1.call-start = ((), (), s32[]{:S(2)}) async-start(), calls=%async_computation.7 | async-start | bytes 22020096 | tf_op jit(solution)/shard_map/reduce_scatter | solution.py:68
  73.5 78.4 %all-gather.9.cloned.1.call-start = ((), (), s32[]{:S(2)}) async-start(), calls=%async_computation.6 | async-start | bytes 22020096 | tf_op jit(solution)/shard_map/all_gather | solution.py:59
  119.4 57.9 %reduce-scatter.8.cloned.1.call-start = ((), (), s32[]{:S(2)}) async-start(), calls=%async_computation.9 | async-start | bytes 4128768 | tf_op jit(solution)/shard_map/reduce_scatter | solution.py:70
  126.1 101.0 %reduce-scatter.6.cloned.1.call-start = ((), (), s32[]{:S(2)}) async-start(), calls=%async_computation.8 | async-start | bytes 4128768 | tf_op jit(solution)/shard_map/reduce_scatter | solution.py:71
  172.2 32.8 %all-to-all-start = ((bf16[256,8,512]{2,0,1:T(8,128)(2,1)}), bf16[256,8,512]{2,0,1:T(8,128)(2,1)}, u32[]{:S(2)}, u32[]{:S(2)}) async-start(bf16[256,8,512]{2,0,1:T(8,128)(2,1)} %copy.23), calls=%async_computation | async-start | bytes 4194304 | tf_op jit(solution)/shard_map/all_to_all | solution.py:85
  177.4 49.8 %collective-permute-start.1 = (bf16[128,1792]{1,0:T(8,128)(2,1)}, bf16[128,1792]{1,0:T(8,128)(2,1)S(1)}, u32[]{:S(2)}, u32[]{:S(2)}) collective-permute-start(bf16[128,1792]{1,0:T(8,128)(2,1)} %reduce-scatter.8.cloned.1.call-done), channel_id=1, source_target_pairs={{0,16},{16,0},{1,17},{17,1},{2,18},{18,2},{3,19},{19,3},{4,20},{20... | collective-permute-start | bytes 1376264 | tf_op jit(solution)/shard_map/ppermute | solution.py:73
Sparse Core Ops, SparseCore 0:
  10.6 51.3 all-gather.4
  64.3 48.4 all-gather.6
  126.2 48.9 reduce-scatter.7
  177.7 49.4 reduce-scatter.5
Sparse Core Ops, SparseCore 1:
  73.5 27.5 reduce-scatter.3
  119.5 32.3 all-gather.8

commit v9 on v5

--- a/solution.py
+++ b/solution.py
@@ -43,35 +43,46 @@
 
     rows_w = down_weight.shape[0]
     d_all = weighted.shape[1]
+    d_half = d_all // n_core
     own_first = lax.axis_index("yhi") == 0
+    my_core = lax.axis_index("core")
+    swap = [(0, 1), (1, 0)]
     weighted_5 = weighted.reshape(tokens_here, n_z, n_yhi, n_core, rows_w)
-    weighted_p = (
-        jnp.where(own_first, weighted_5, jnp.flip(weighted_5, axis=2))
-        .transpose(0, 3, 1, 2, 4)
-        .reshape(tokens_here, d_all)
-    )
-    swap = [(0, 1), (1, 0)]
+    weighted_rel = jnp.where(own_first, weighted_5, jnp.flip(weighted_5, axis=2))
+    weighted_mine = lax.dynamic_index_in_dim(weighted_rel, my_core, axis=3, keepdims=False)
+    weighted_mine = weighted_mine.reshape(tokens_here, d_half)
+    weighted_theirs = lax.dynamic_index_in_dim(weighted_rel, 1 - my_core, axis=3, keepdims=False)
+    weighted_recv = lax.ppermute(weighted_theirs.reshape(tokens_here, d_half), "core", swap)
+    hidden_recv = lax.ppermute(hidden, "core", swap)
+
     gathered = jnp.concatenate([down_weight, lax.ppermute(down_weight, "yhi", swap)], axis=0)
     gathered = lax.all_gather(gathered, "z", axis=0, tiled=True)
-    gathered = lax.all_gather(gathered, "core", axis=0, tiled=True)
 
     scale = 1.0 / math.sqrt(tokens_here * n_sample)
     grad_part = (
         lax.dot_general(
-            weighted_p, hidden, (((0,), (0,)), ((), ())), preferred_element_type=jnp.float32
+            jnp.concatenate([weighted_mine, weighted_recv], axis=0),
+            jnp.concatenate([hidden, hidden_recv], axis=0),
+            (((0,), (0,)), ((), ())),
+            preferred_element_type=jnp.float32,
         )
         * scale
     ).astype(jnp.bfloat16)
-    grad_part = lax.psum_scatter(grad_part, "core", scatter_dimension=0, tiled=True)
     grad_part = lax.psum_scatter(grad_part, "z", scatter_dimension=0, tiled=True)
     weight_grad = (
         grad_part[:rows_w].astype(jnp.float32)
         + lax.ppermute(grad_part[rows_w:], "yhi", swap).astype(jnp.float32)
     ).astype(jnp.bfloat16)
 
-    partial_value = lax.dot_general(
-        hidden, gathered, (((1,), (1,)), ((), ())), preferred_element_type=jnp.float32
-    ).astype(jnp.bfloat16)
+    def value_of(rows):
+        return lax.dot_general(
+            rows, gathered, (((1,), (1,)), ((), ())), preferred_element_type=jnp.float32
+        ).astype(jnp.bfloat16)
+
+    value_mine = value_of(hidden)
+    value_recv = lax.ppermute(value_of(hidden_recv), "core", swap)
+    partial_value = jnp.stack([value_mine, value_recv], axis=1)
+    partial_value = jnp.where(my_core == 0, partial_value, jnp.flip(partial_value, axis=1))
     partial_value = partial_value.reshape(tokens_here, n_core, n_z, n_yhi, rows_w).transpose(
         0, 2, 3, 1, 4
     )
@@ -79,9 +90,11 @@
         tokens_here, n_tensor, d_all // n_tensor
     )
     layer_out = sum_to_bf16(lax.all_to_all(partial_value, "tensor", 1, 1, tiled=True), 1)
-    hidden_grad = jnp.dot(weighted_p, gathered, preferred_element_type=jnp.float32).astype(
-        jnp.bfloat16
-    )
+    grad_for_other = jnp.dot(weighted_recv, gathered, preferred_element_type=jnp.float32)
+    hidden_grad = (
+        jnp.dot(weighted_mine, gathered, preferred_element_type=jnp.float32)
+        + lax.ppermute(grad_for_other, "core", swap)
+    ).astype(jnp.bfloat16)
     return (layer_out, hidden_grad, weight_grad)
 
 

time: 225 us -> 222 us (0.987)
  other arithmetic: 16.2 us -> 13.9 us
    all_gather x1 -> x0, waiting for transfers between devices: 32 us -> none  [shards(): gathered = lax.all_gather(gathered, 'core', axis=0, tiled=True)]
    reduce_scatter x1, waiting for transfers between devices: 29 us -> 59.5 us  [shards(): lax.psum_scatter(grad_part, 'z', scatter_dimension=0, tiled=True)]
    transpose x1 -> x0, other arithmetic: 4.12 us -> none  [shards(): weighted_p = jnp.where(own_first, weighted_5, jnp.flip(weighted_5, axis=2...]
    ppermute x1, waiting for transfers between devices: 0.01 us -> 3.35 us  [shards(): lax.ppermute(grad_part[rows_w:], 'yhi', swap).astype(jnp.float32)]
    select_n x0 -> x2, other arithmetic: none -> 3.31 us  [the longest x1 2.82 us: shards(): jnp.where(own_first, weighted_5, jnp.flip(weighted_5, axis=2))]
    ppermute x0 -> x4, waiting for transfers between devices: none -> 3.02 us  [the longest x1 3.02 us: shards(): hidden_recv = lax.ppermute(hidden, 'core', swap)]
    transpose x1 -> x0, local copies, waits for them, and re-layouts: 3.01 us -> none  [shards(): weighted_p = jnp.where(own_first, weighted_5, jnp.flip(weighted_5, axis=2...]
    dynamic_slice x0 -> x3, local copies, waits for them, and re-layouts: none -> 2.74 us  [the longest x1 1.59 us: shards(): lax.dynamic_index_in_dim(weighted_rel, 1 - my_core, axis=3, keepdims=False)]
  transfers between devices with their start and end apart: 7 -> 9, of which waited for: 4 -> 5; matrix products, arithmetic and copies ran while one was open for 25% -> 24% of each run, Pallas kernels for 0% -> 0%
where the time goes in v9:
time: 222 us; the launch traced here: 219 us
  waiting for transfers between devices  115 us (52%)
  matrix products  26.4 us (12%)
  blocking collectives  20.4 us (9%)
  local copies, waits for them, and re-layouts  16.6 us (7%)
  between operations  14.9 us (7%)
  other arithmetic  13.9 us (6%)
  starting transfers between devices  12.6 us (6%)
    reduce_scatter x1, waiting for transfers between devices, shards(): lax.psum_scatter(grad_part, 'z', scatter_dimension=0, tiled=True)  59.5 us
    all_gather x1, waiting for transfers between devices, shards(): gathered = lax.all_gather(gathered, 'z', axis=0, tiled=True)  38 us
    unnamed x1, blocking collectives  20.4 us
    ppermute x1, waiting for transfers between devices, shards(): lax.ppermute(down_weight, 'yhi', swap)  10.8 us
    dot_general x2, matrix products, value_of(): lax.dot_general(rows, gathered, (((1,), (1,)), ((), ())), preferred_eleme...  8.89 us
    dot_general x1, matrix products, shards(): lax.dot_general(jnp.concatenate([weighted_mine, weighted_recv], axis=0),...  7.52 us
    dot_general x1, matrix products, shards(): jnp.dot(weighted_mine, gathered, preferred_element_type=jnp.float32)  6.61 us
    all_to_all x1, starting transfers between devices, shards(): lax.all_to_all(partial_value, 'tensor', 1, 1, tiled=True)  5.13 us
  transfers between devices with their start and end apart: 9, of which 5 were waited for; matrix products, arithmetic and copies ran while one was open for 24% of the time, Pallas kernels for 0%

profile of v9, /device:TPU:32, one launch (start us, length us, event | category | flops | bytes accessed | tf_op | source)
XLA Modules:
  0.0 219.5 jit_solution(11949393025093331972)
XLA Ops:
  7.3 3.3 %collective-permute-start = (bf16[128,1792]{1,0:T(8,128)(2,1)}, bf16[128,1792]{1,0:T(8,128)(2,1)S(1)}, u32[]{:S(2)}, u32[]{:S(2)}) collective-permute-start(bf16[128,1792]{1,0:T(8,128)(2,1)} %param.6), channel_id=1, source_target_pairs={{0,16},{16,0},{1,17},{17,1},{2,18},{18,2},{3,19},{19,3},{4,20},{20... | collective-permute-start | bytes 1376264 | tf_op jit(solution)/shard_map/ppermute | solution.py:58
  10.5 10.8 %collective-permute-done = bf16[128,1792]{1,0:T(8,128)(2,1)S(1)} collective-permute-done((bf16[128,1792]{1,0:T(8,128)(2,1)}, bf16[128,1792]{1,0:T(8,128)(2,1)S(1)}, u32[]{:S(2)}, u32[]{:S(2)}) %collective-permute-start) | collective-permute-done | bytes 458784 | tf_op jit(solution)/shard_map/ppermute | solution.py:58
  21.3 2.0 pad_maximum_fusion.1
  23.4 0.6 dynamic-slice
  24.8 20.4 %all-reduce = s32[256]{0:T(256)S(1)} all-reduce(s32[256]{0:T(256)S(1)} %add_dynamic-update-slice_fusion), channel_id=2, replica_groups=mesh['z'=8,'yhi'=2,'core'=2,'tensor'=8] {'z','yhi','core'}, use_global_device_ids=true, to_apply=%add | all-reduce | flops 256 | bytes 2048
  46.3 2.5 %copy.26 = bf16[256,4096]{0,1:T(8,128)(2,1)} copy(bf16[256,4096]{1,0:T(8,128)(2,1)S(1)} %copy-done.1) | data formatting | bytes 4194304 | tf_op args[2]
  48.9 2.0 multiply_convert_fusion.1
  50.9 3.2 %copy.28 = bf16[256,8,2,2,128]{4,1,3,2,0:T(8,128)(2,1)} copy(bf16[256,8,2,2,128]{0,4,3,2,1:T(8,128)(2,1)S(1)} %bitcast.22) | data formatting | bytes 4194304 | tf_op jit(solution)/shard_map/reshape | solution.py:50
  54.0 2.8 %reverse_select_fusion = bf16[256,8,2,2,128]{4,1,3,2,0:T(8,128)(2,1)S(1)} fusion(bf16[256,8,2,2,128]{4,1,3,2,0:T(8,128)(2,1)} %copy.28, pred[]{:T(512)S(6)} %eq.34), kind=kLoop, calls=%fused_computation.2 | loop fusion | flops 1048576 | bytes 4194305 | tf_op jit(solution)/shard_map/jit(_where)/select_n | solution.py:51
  56.9 0.4 constant_dynamic-slice_fusion.1
  57.2 1.6 copy.30
  58.8 0.5 collective-permute-start.1
  59.3 0.8 copy.29
  60.1 3.0 %collective-permute-done.1 = bf16[256,1792]{1,0:T(8,128)(2,1)} collective-permute-done((bf16[256,1792]{1,0:T(8,128)(2,1)}, bf16[256,1792]{1,0:T(8,128)(2,1)}, u32[]{:S(2)}, u32[]{:S(2)}) %collective-permute-start.1) | collective-permute-done | bytes 917536 | tf_op jit(solution)/shard_map/ppermute | solution.py:56
  63.1 7.5 %multiply_convert_fusion = bf16[2048,1792]{1,0:T(8,128)(2,1)} fusion(bf16[256,2048]{0,1:T(8,128)(2,1)S(1)} %collective-permute-done.3, bf16[256,2048]{0,1:T(8,128)(2,1)S(1)} %bitcast.26, bf16[256,1792]{1,0:T(8,128)(2,1)} %collective-permute-done.1, bf16[256,1792]{1,0:T(8,128)(2,1)} %param.5), kind=kOutput, calls=%fused_computation | convolution fusion | flops 3773300736 | bytes 11272192 | tf_op jit(solution)/shard_map/dot_general | solution.py:63
  70.7 38.0 %all-gather.3.cloned.1.call-done = bf16[2048,1792]{1,0:T(8,128)(2,1)} async-done(((bf16[256,1792]{1,0:T(8,128)(2,1)}), bf16[2048,1792]{1,0:T(8,128)(2,1)}) %all-gather.3.cloned.1.call-update) | async-done | bytes 7340048 | tf_op jit(solution)/shard_map/all_gather | solution.py:59
  108.7 5.5 %fusion.2 = bf16[256,2048]{0,1:T(8,128)(2,1)S(1)} fusion(bf16[2048,1792]{1,0:T(8,128)(2,1)} %all-gather.3.cloned.1.call-done, bf16[256,1792]{1,0:T(8,128)(2,1)} %collective-permute-done.1), kind=kOutput, calls=%fused_computation.10 | convolution fusion | flops 1879572480 | bytes 9306112 | tf_op jit(solution)/shard_map/dot_general | solution.py:78
  114.3 3.3 %fusion.11 = f32[256,1792]{1,0:T(8,128)} fusion(bf16[256,2048]{0,1:T(8,128)(2,1)S(1)} %collective-permute-done.3, bf16[2048,1792]{1,0:T(8,128)(2,1)S(1)} %copy-done), kind=kOutput, calls=%fused_computation.33 | convolution fusion | flops 1879048192 | bytes 10223616 | tf_op jit(solution)/shard_map/dot_general | solution.py:93
  117.7 0.5 collective-permute-start.4
  118.2 3.4 %fusion.1 = bf16[256,1,2048]{0,2,1:T(8,128)(2,1)S(1)} fusion(bf16[2048,1792]{1,0:T(8,128)(2,1)S(1)} %copy-done, bf16[256,1792]{1,0:T(8,128)(2,1)} %param.5), kind=kOutput, calls=%fused_computation.9 | convolution fusion | flops 1879572480 | bytes 9306112 | tf_op jit(solution)/shard_map/dot_general | solution.py:78
  121.8 0.5 reverse_select_fusion.2
  122.2 3.2 %copy.24 = bf16[256,2,8,2,128]{4,2,1,3,0:T(8,128)(2,1)} copy(bf16[256,2,8,2,128]{0,4,3,2,1:T(8,128)(2,1)S(1)} %bitcast.23) | data formatting | bytes 4194304 | tf_op jit(solution)/shard_map/reshape | solution.py:86
  125.4 2.8 %reverse_select_fusion.1 = bf16[256,8,2,2,128]{4,1,3,2,0:T(8,128)(2,1)S(1)} fusion(bf16[256,8,2,2,128]{4,1,3,2,0:T(8,128)(2,1)} %bitcast.24, pred[]{:T(512)S(6)} %eq.34), kind=kLoop, calls=%fused_computation.3 | loop fusion | flops 1048576 | bytes 4194305 | tf_op jit(solution)/shard_map/jit(_where)/select_n | solution.py:89
  128.2 2.0 copy.25
  130.2 5.1 %all-to-all-start = ((bf16[256,8,512]{2,0,1:T(8,128)(2,1)}), bf16[256,8,512]{2,0,1:T(8,128)(2,1)S(1)}, u32[]{:S(2)}, u32[]{:S(2)}) async-start(bf16[256,8,512]{2,0,1:T(8,128)(2,1)} %copy.25), calls=%async_computation | async-start | bytes 4194304 | tf_op jit(solution)/shard_map/all_to_all | solution.py:92
  135.3 59.5 %reduce-scatter.2.cloned.1.call-done = bf16[256,1792]{1,0:T(8,128)(2,1)} async-done(((bf16[2048,1792]{1,0:T(8,128)(2,1)}), bf16[256,1792]{1,0:T(8,128)(2,1)}) %reduce-scatter.2.cloned.1.call-update) | async-done | bytes 917520 | tf_op jit(solution)/shard_map/reduce_scatter | solution.py:71
  194.9 1.8 slice.19
  196.7 3.0 %collective-permute-start.5 = (bf16[128,1792]{1,0:T(8,128)(2,1)}, bf16[128,1792]{1,0:T(8,128)(2,1)}, u32[]{:S(2)}, u32[]{:S(2)}) collective-permute-start(bf16[128,1792]{1,0:T(8,128)(2,1)} %slice.19), channel_id=1, source_target_pairs={{0,16},{16,0},{1,17},{17,1},{2,18},{18,2},{3,19},{19,3},{4,20},{20... | collective-permute-start | bytes 1376264 | tf_op jit(solution)/shard_map/ppermute | solution.py:74
  199.7 6.6 %fusion = bf16[256,1792]{1,0:T(8,128)(2,1)} fusion(f32[256,1792]{1,0:T(8,128)} %collective-permute-done.4, bf16[256,2048]{0,1:T(8,128)(2,1)S(1)} %bitcast.27, bf16[2048,1792]{1,0:T(8,128)(2,1)} %all-gather.3.cloned.1.call-done), kind=kOutput, calls=%fused_computation.8 | convolution fusion | flops 1879965696 | bytes 11141120 | tf_op jit(solution)/shard_map/dot_general | solution.py:95
  206.3 1.0 reduce_sum.30
  207.4 3.3 %collective-permute-done.5 = bf16[128,1792]{1,0:T(8,128)(2,1)} collective-permute-done((bf16[128,1792]{1,0:T(8,128)(2,1)}, bf16[128,1792]{1,0:T(8,128)(2,1)}, u32[]{:S(2)}, u32[]{:S(2)}) %collective-permute-start.5) | collective-permute-done | bytes 458784 | tf_op jit(solution)/shard_map/ppermute | solution.py:74
  210.7 1.9 add_convert_fusion
  (37 shorter events, 1.7 us)
Async XLA Ops:
  7.2 16.2 %copy-start.5 = (u32[256]{0:T(256)S(1)}, u32[256]{0:T(256)}, u32[]{:S(2)}) copy-start(u32[256]{0:T(256)} %constant.44) | copy-start | bytes 3076
  7.2 17.5 %copy-start.4 = (s32[4]{0:T(128)S(1)}, s32[4]{0:T(128)}, u32[]{:S(2)}) copy-start(s32[4]{0:T(128)} %param.8) | copy-start | bytes 52
  7.2 17.5 %copy-start.3 = (s32[4]{0:T(128)S(1)}, s32[4]{0:T(128)}, u32[]{:S(2)}) copy-start(s32[4]{0:T(128)} %param.9) | copy-start | bytes 52
  7.2 39.1 %copy-start.1 = (bf16[256,4096]{1,0:T(8,128)(2,1)S(1)}, bf16[256,4096]{1,0:T(8,128)(2,1)}, u32[]{:S(2)}) copy-start(bf16[256,4096]{1,0:T(8,128)(2,1)} %param.7) | copy-start | bytes 6291460
  7.2 101.5 %all-gather.3.cloned.1.call-start = ((), (), s32[]{:S(2)}) async-start(), calls=%async_computation.2 | async-start | bytes 8257536 | tf_op jit(solution)/shard_map/all_gather | solution.py:59
  7.3 14.1 %collective-permute-start = (bf16[128,1792]{1,0:T(8,128)(2,1)}, bf16[128,1792]{1,0:T(8,128)(2,1)S(1)}, u32[]{:S(2)}, u32[]{:S(2)}) collective-permute-start(bf16[128,1792]{1,0:T(8,128)(2,1)} %param.6), channel_id=1, source_target_pairs={{0,16},{16,0},{1,17},{17,1},{2,18},{18,2},{3,19},{19,3},{4,20},{20... | collective-permute-start | bytes 1376264 | tf_op jit(solution)/shard_map/ppermute | solution.py:58
  23.3 171.5 %reduce-scatter.2.cloned.1.call-start = ((), (), s32[]{:S(2)}) async-start(), calls=%async_computation.3 | async-start | bytes 8257536 | tf_op jit(solution)/shard_map/reduce_scatter | solution.py:71
  58.8 4.3 %collective-permute-start.3 = (bf16[256,2048]{0,1:T(8,128)(2,1)}, bf16[256,2048]{0,1:T(8,128)(2,1)S(1)}, u32[]{:S(2)}, u32[]{:S(2)}) collective-permute-start(bf16[256,2048]{0,1:T(8,128)(2,1)} %bitcast.10), channel_id=1, source_target_pairs={{0,8},{8,0},{1,9},{9,1},{2,10},{10,2},{3,11},{11,3},{4,12},{12,4},... | collective-permute-start | bytes 3145736 | tf_op jit(solution)/shard_map/ppermute | solution.py:55
  58.8 4.3 %collective-permute-start.1 = (bf16[256,1792]{1,0:T(8,128)(2,1)}, bf16[256,1792]{1,0:T(8,128)(2,1)}, u32[]{:S(2)}, u32[]{:S(2)}) collective-permute-start(bf16[256,1792]{1,0:T(8,128)(2,1)} %param.5), channel_id=1, source_target_pairs={{0,8},{8,0},{1,9},{9,1},{2,10},{10,2},{3,11},{11,3},{4,12},{12,4},... | collective-permute-start | bytes 2752520 | tf_op jit(solution)/shard_map/ppermute | solution.py:56
  108.7 5.6 %copy-start = (bf16[2048,1792]{1,0:T(8,128)(2,1)S(1)}, bf16[2048,1792]{1,0:T(8,128)(2,1)}, u32[]{:S(2)}) copy-start(bf16[2048,1792]{1,0:T(8,128)(2,1)} %all-gather.3.cloned.1.call-done) | copy-start | bytes 22020100
  114.2 7.3 %collective-permute-start.2 = (bf16[256,2048]{0,1:T(8,128)(2,1)S(1)}, bf16[256,2048]{0,1:T(8,128)(2,1)S(1)}, u32[]{:S(2)}, u32[]{:S(2)}) collective-permute-start(bf16[256,2048]{0,1:T(8,128)(2,1)S(1)} %fusion.2), channel_id=1, source_target_pairs={{0,8},{8,0},{1,9},{9,1},{2,10},{10,2},{3,11},{11,3},{4,12},{12,4},... | collective-permute-start | bytes 3145736 | tf_op jit(solution)/shard_map/ppermute | solution.py:83
  117.7 82.0 %collective-permute-start.4 = (f32[256,1792]{1,0:T(8,128)}, f32[256,1792]{1,0:T(8,128)}, u32[]{:S(2)}, u32[]{:S(2)}) collective-permute-start(f32[256,1792]{1,0:T(8,128)} %fusion.11), channel_id=1, source_target_pairs={{0,8},{8,0},{1,9},{9,1},{2,10},{10,2},{3,11},{11,3},{4,12},{12,4},... | collective-permute-start | bytes 5505032 | tf_op jit(solution)/shard_map/ppermute | solution.py:96
  130.2 76.1 %all-to-all-start = ((bf16[256,8,512]{2,0,1:T(8,128)(2,1)}), bf16[256,8,512]{2,0,1:T(8,128)(2,1)S(1)}, u32[]{:S(2)}, u32[]{:S(2)}) async-start(bf16[256,8,512]{2,0,1:T(8,128)(2,1)} %copy.25), calls=%async_computation | async-start | bytes 4194304 | tf_op jit(solution)/shard_map/all_to_all | solution.py:92
  196.7 14.0 %collective-permute-start.5 = (bf16[128,1792]{1,0:T(8,128)(2,1)}, bf16[128,1792]{1,0:T(8,128)(2,1)}, u32[]{:S(2)}, u32[]{:S(2)}) collective-permute-start(bf16[128,1792]{1,0:T(8,128)(2,1)} %slice.19), channel_id=1, source_target_pairs={{0,16},{16,0},{1,17},{17,1},{2,18},{18,2},{3,19},{19,3},{4,20},{20... | collective-permute-start | bytes 1376264 | tf_op jit(solution)/shard_map/ppermute | solution.py:74
  206.3 4.4 %copy-start.2 = (bf16[256,1792]{1,0:T(8,128)(2,1)S(1)}, bf16[256,1792]{1,0:T(8,128)(2,1)}, u32[]{:S(2)}) copy-start(bf16[256,1792]{1,0:T(8,128)(2,1)} %reduce-scatter.2.cloned.1.call-done) | copy-start | bytes 2752516
Sparse Core Ops, SparseCore 0:
  23.5 85.1 all-gather.2
  111.2 83.5 reduce-scatter.1

commit v10 on v9

--- a/solution.py
+++ b/solution.py
@@ -68,10 +68,13 @@
         )
         * scale
     ).astype(jnp.bfloat16)
-    grad_part = lax.psum_scatter(grad_part, "z", scatter_dimension=0, tiled=True)
+    grad_part = grad_part.reshape(n_z, -1, grad_part.shape[1])
+    grad_part = jnp.sum(
+        lax.all_to_all(grad_part, "z", 0, 0, tiled=True).astype(jnp.float32), axis=0
+    )
     weight_grad = (
-        grad_part[:rows_w].astype(jnp.float32)
-        + lax.ppermute(grad_part[rows_w:], "yhi", swap).astype(jnp.float32)
+        grad_part[:rows_w]
+        + lax.ppermute(grad_part[rows_w:].astype(jnp.bfloat16), "yhi", swap).astype(jnp.float32)
     ).astype(jnp.bfloat16)
 
     def value_of(rows):

time: 222 us -> 336 us (1.51)
  waiting for transfers between devices: 115 us -> 222 us
  other arithmetic: 13.9 us -> 20.3 us
  starting transfers between devices: 12.6 us -> 18.5 us
    all_gather x1, waiting for transfers between devices: 38 us -> 168 us  [shards(): gathered = lax.all_gather(gathered, 'z', axis=0, tiled=True)]
    reduce_scatter x1 -> x0, waiting for transfers between devices: 59.5 us -> none  [shards(): lax.psum_scatter(grad_part, 'z', scatter_dimension=0, tiled=True)]
    ppermute x1, waiting for transfers between devices: 3.35 us -> 28.4 us  [shards(): lax.ppermute(grad_part[rows_w:].astype(jnp.bfloat16), 'yhi', swap)]
    all_to_all x0 -> x1, waiting for transfers between devices: none -> 22.3 us  [shards(): lax.all_to_all(grad_part, 'z', 0, 0, tiled=True).astype(jnp.float32)]
    ppermute x1, waiting for transfers between devices: 10.8 us -> 0.01 us  [shards(): lax.ppermute(down_weight, 'yhi', swap)]
    all_to_all x0 -> x1, starting transfers between devices: none -> 5.86 us  [shards(): lax.all_to_all(grad_part, 'z', 0, 0, tiled=True).astype(jnp.float32)]
    reduce_sum x0 -> x1, other arithmetic: none -> 4.45 us  [shards(): jnp.sum(lax.all_to_all(grad_part, 'z', 0, 0, tiled=True).astype(jnp.float...]
  transfers between devices with their start and end apart: 9 -> 9, of which waited for: 5 -> 4; matrix products, arithmetic and copies ran while one was open for 24% -> 16% of each run, Pallas kernels for 0% -> 0%
where the time goes in v10:
time: 336 us
  waiting for transfers between devices  222 us (66%)
  matrix products  23.1 us (7%)
  blocking collectives  21.7 us (6%)
  other arithmetic  20.3 us (6%)
  starting transfers between devices  18.5 us (6%)
  local copies, waits for them, and re-layouts  15.5 us (5%)
  between operations  14.9 us (4%)
    all_gather x1, waiting for transfers between devices, shards(): gathered = lax.all_gather(gathered, 'z', axis=0, tiled=True)  168 us
    ppermute x1, waiting for transfers between devices, shards(): lax.ppermute(grad_part[rows_w:].astype(jnp.bfloat16), 'yhi', swap)  28.4 us
    all_to_all x1, waiting for transfers between devices, shards(): lax.all_to_all(grad_part, 'z', 0, 0, tiled=True).astype(jnp.float32)  22.3 us
    unnamed x1, blocking collectives  21.7 us
    dot_general x2, matrix products, value_of(): lax.dot_general(rows, gathered, (((1,), (1,)), ((), ())), preferred_eleme...  7.72 us
    dot_general x1, matrix products, shards(): lax.dot_general(jnp.concatenate([weighted_mine, weighted_recv], axis=0),...  7.48 us
  transfers between devices with their start and end apart: 9, of which 4 were waited for; matrix products, arithmetic and copies ran while one was open for 16% of the time, Pallas kernels for 0%

profile of v10, /device:TPU:32, one launch (start us, length us, event | category | flops | bytes accessed | tf_op | source)
XLA Modules:
  0.0 335.6 jit_solution(15251914635403936242)
XLA Ops:
  7.2 3.3 collective-permute-start
  10.5 1.3 dynamic-slice
  12.4 0.8 add_dynamic-update-slice_fusion
  13.3 21.7 %all-reduce = s32[256]{0:T(256)S(1)} all-reduce(s32[256]{0:T(256)S(1)} %add_dynamic-update-slice_fusion), channel_id=2, replica_groups=mesh['z'=8,'yhi'=2,'core'=2,'tensor'=8] {'z','yhi','core'}, use_global_device_ids=true, to_apply=%add | all-reduce | flops 256 | bytes 2048
  35.6 0.8 select_reduce_fusion
  36.5 2.0 pad_maximum_fusion.1
  38.7 2.5 copy.26
  41.2 2.0 multiply_convert_fusion.1
  43.2 3.1 copy.28
  46.4 2.8 reverse_select_fusion
  49.6 1.6 copy.30
  51.2 0.5 collective-permute-start.1
  51.7 0.8 copy.29
  52.5 3.0 collective-permute-done.1
  55.5 7.5 %multiply_convert_fusion = bf16[2048,1792]{1,0:T(8,128)(2,1)} fusion(bf16[256,2048]{0,1:T(8,128)(2,1)S(1)} %collective-permute-done.3, bf16[256,2048]{0,1:T(8,128)(2,1)S(1)} %bitcast.30, bf16[256,1792]{1,0:T(8,128)(2,1)} %collective-permute-done.1, bf16[256,1792]{1,0:T(8,128)(2,1)} %param.5), kind=kOutput, calls=%fused_computation.1 | convolution fusion | flops 3773300736 | bytes 11272192 | tf_op jit(solution)/shard_map/dot_general | solution.py:63
  63.0 5.9 %all-to-all-start.1 = ((bf16[8,256,1792]{2,1,0:T(8,128)(2,1)}), bf16[8,256,1792]{2,1,0:T(8,128)(2,1)}, u32[]{:S(2)}, u32[]{:S(2)}) async-start(bf16[8,256,1792]{2,1,0:T(8,128)(2,1)} %bitcast.29), calls=%async_computation.1 | async-start | bytes 14680064 | tf_op jit(solution)/shard_map/all_to_all | solution.py:73
  68.9 167.9 %all-gather.3.cloned.1.call-done = bf16[2048,1792]{1,0:T(8,128)(2,1)} async-done(((bf16[256,1792]{1,0:T(8,128)(2,1)}), bf16[2048,1792]{1,0:T(8,128)(2,1)}) %all-gather.3.cloned.1.call-update) | async-done | bytes 7340048 | tf_op jit(solution)/shard_map/all_gather | solution.py:59
  236.8 5.5 %fusion.2 = bf16[256,2048]{0,1:T(8,128)(2,1)S(1)} fusion(bf16[2048,1792]{1,0:T(8,128)(2,1)} %all-gather.3.cloned.1.call-done, bf16[256,1792]{1,0:T(8,128)(2,1)} %collective-permute-done.1), kind=kOutput, calls=%fused_computation.11 | convolution fusion | flops 1879572480 | bytes 9306112 | tf_op jit(solution)/shard_map/dot_general | solution.py:81
  242.4 3.4 %fusion.12 = f32[256,1792]{1,0:T(8,128)} fusion(bf16[256,2048]{0,1:T(8,128)(2,1)S(1)} %collective-permute-done.3, bf16[2048,1792]{1,0:T(8,128)(2,1)S(1)} %copy-done), kind=kOutput, calls=%fused_computation.36 | convolution fusion | flops 1879048192 | bytes 10223616 | tf_op jit(solution)/shard_map/dot_general | solution.py:96
  245.8 0.5 collective-permute-start.4
  246.3 2.2 fusion.1
  249.2 3.2 copy.24
  252.4 2.8 reverse_select_fusion.1
  255.1 2.0 copy.25
  257.2 22.3 %all-to-all-done.1 = bf16[8,256,1792]{2,1,0:T(8,128)(2,1)} async-done(((bf16[8,256,1792]{2,1,0:T(8,128)(2,1)}), bf16[8,256,1792]{2,1,0:T(8,128)(2,1)}, u32[]{:S(2)}, u32[]{:S(2)}) %all-to-all-start.1) | async-done | bytes 7340064 | tf_op jit(solution)/shard_map/all_to_all | solution.py:73
  279.5 5.4 %all-to-all-start = ((bf16[256,8,512]{2,0,1:T(8,128)(2,1)}), bf16[256,8,512]{2,0,1:T(8,128)(2,1)}, u32[]{:S(2)}, u32[]{:S(2)}) async-start(bf16[256,8,512]{2,0,1:T(8,128)(2,1)} %copy.25), calls=%async_computation | async-start | bytes 4194304 | tf_op jit(solution)/shard_map/all_to_all | solution.py:95
  284.9 4.5 %convert_reduce_fusion = f32[256,1792]{1,0:T(8,128)S(1)} fusion(bf16[8,256,1792]{2,1,0:T(8,128)(2,1)} %all-to-all-done.1), kind=kLoop, calls=%fused_computation | loop fusion | flops 6881280 | bytes 9175040 | tf_op jit(solution)/shard_map/reduce_sum | solution.py:72
  289.5 2.8 collective-permute-start.5
  292.3 28.4 %collective-permute-done.5 = bf16[128,1792]{1,0:T(8,128)(2,1)S(1)} collective-permute-done((bf16[128,1792]{1,0:T(8,128)(2,1)S(1)}, bf16[128,1792]{1,0:T(8,128)(2,1)S(1)}, u32[]{:S(2)}, u32[]{:S(2)}) %collective-permute-start.5) | collective-permute-done | bytes 458784 | tf_op jit(solution)/shard_map/ppermute | solution.py:77
  320.6 0.9 fusion.9
  321.5 4.5 %fusion = bf16[256,1792]{1,0:T(8,128)(2,1)} fusion(f32[256,1792]{1,0:T(8,128)} %collective-permute-done.4, bf16[256,2048]{0,1:T(8,128)(2,1)S(1)} %bitcast.31, bf16[2048,1792]{1,0:T(8,128)(2,1)S(1)} %bitcast.24), kind=kOutput, calls=%fused_computation.9 | convolution fusion | flops 1879965696 | bytes 11141120 | tf_op jit(solution)/shard_map/dot_general | solution.py:98
  326.0 2.7 reduce_sum.39
  (42 shorter events, 2.2 us)
Async XLA Ops:
  7.2 31.4 %copy-start.4 = (s32[4]{0:T(128)S(1)}, s32[4]{0:T(128)}, u32[]{:S(2)}) copy-start(s32[4]{0:T(128)} %param.8) | copy-start | bytes 52
  7.2 31.5 %copy-start.3 = (bf16[256,4096]{1,0:T(8,128)(2,1)S(1)}, bf16[256,4096]{1,0:T(8,128)(2,1)}, u32[]{:S(2)}) copy-start(bf16[256,4096]{1,0:T(8,128)(2,1)} %param.7) | copy-start | bytes 6291460
  7.2 229.6 %all-gather.3.cloned.1.call-start = ((), (), s32[]{:S(2)}) async-start(), calls=%async_computation.2 | async-start | bytes 8257536 | tf_op jit(solution)/shard_map/all_gather | solution.py:59
  7.2 29.3 %collective-permute-start = (bf16[128,1792]{1,0:T(8,128)(2,1)}, bf16[128,1792]{1,0:T(8,128)(2,1)S(1)}, u32[]{:S(2)}, u32[]{:S(2)}) collective-permute-start(bf16[128,1792]{1,0:T(8,128)(2,1)} %param.6), channel_id=1, source_target_pairs={{0,16},{16,0},{1,17},{17,1},{2,18},{18,2},{3,19},{19,3},{4,20},{20... | collective-permute-start | bytes 1376264 | tf_op jit(solution)/shard_map/ppermute | solution.py:58
  51.2 4.3 %collective-permute-start.3 = (bf16[256,2048]{0,1:T(8,128)(2,1)}, bf16[256,2048]{0,1:T(8,128)(2,1)S(1)}, u32[]{:S(2)}, u32[]{:S(2)}) collective-permute-start(bf16[256,2048]{0,1:T(8,128)(2,1)} %bitcast.32), channel_id=1, source_target_pairs={{0,8},{8,0},{1,9},{9,1},{2,10},{10,2},{3,11},{11,3},{4,12},{12,4},... | collective-permute-start | bytes 3145736 | tf_op jit(solution)/shard_map/ppermute | solution.py:55
  51.2 4.3 %collective-permute-start.1 = (bf16[256,1792]{1,0:T(8,128)(2,1)}, bf16[256,1792]{1,0:T(8,128)(2,1)}, u32[]{:S(2)}, u32[]{:S(2)}) collective-permute-start(bf16[256,1792]{1,0:T(8,128)(2,1)} %param.5), channel_id=1, source_target_pairs={{0,8},{8,0},{1,9},{9,1},{2,10},{10,2},{3,11},{11,3},{4,12},{12,4},... | collective-permute-start | bytes 2752520 | tf_op jit(solution)/shard_map/ppermute | solution.py:56
  52.5 10.5 %copy-start.1 = (bf16[256,8,2,1,128]{0,4,2,1,3:T(8,128)(2,1)}, bf16[256,8,2,1,128]{0,4,2,1,3:T(8,128)(2,1)S(1)}, u32[]{:S(2)}) copy-start(bf16[256,8,2,1,128]{0,4,2,1,3:T(8,128)(2,1)S(1)} %copy.29) | copy-start | bytes 3145732
  63.0 216.5 %all-to-all-start.1 = ((bf16[8,256,1792]{2,1,0:T(8,128)(2,1)}), bf16[8,256,1792]{2,1,0:T(8,128)(2,1)}, u32[]{:S(2)}, u32[]{:S(2)}) async-start(bf16[8,256,1792]{2,1,0:T(8,128)(2,1)} %bitcast.29), calls=%async_computation.1 | async-start | bytes 14680064 | tf_op jit(solution)/shard_map/all_to_all | solution.py:73
  236.8 5.6 %copy-start = (bf16[2048,1792]{1,0:T(8,128)(2,1)S(1)}, bf16[2048,1792]{1,0:T(8,128)(2,1)}, u32[]{:S(2)}) copy-start(bf16[2048,1792]{1,0:T(8,128)(2,1)} %all-gather.3.cloned.1.call-done) | copy-start | bytes 22020100
  242.3 4.0 %copy-start.5 = (bf16[256,1792]{1,0:T(8,128)(2,1)S(1)}, bf16[256,1792]{1,0:T(8,128)(2,1)}, u32[]{:S(2)}) copy-start(bf16[256,1792]{1,0:T(8,128)(2,1)} %param.5) | copy-start | bytes 2752516
  242.3 6.2 %collective-permute-start.2 = (bf16[256,2048]{0,1:T(8,128)(2,1)S(1)}, bf16[256,2048]{0,1:T(8,128)(2,1)S(1)}, u32[]{:S(2)}, u32[]{:S(2)}) collective-permute-start(bf16[256,2048]{0,1:T(8,128)(2,1)S(1)} %fusion.2), channel_id=1, source_target_pairs={{0,8},{8,0},{1,9},{9,1},{2,10},{10,2},{3,11},{11,3},{4,12},{12,4},... | collective-permute-start | bytes 3145736 | tf_op jit(solution)/shard_map/ppermute | solution.py:86
  245.8 75.7 %collective-permute-start.4 = (f32[256,1792]{1,0:T(8,128)}, f32[256,1792]{1,0:T(8,128)}, u32[]{:S(2)}, u32[]{:S(2)}) collective-permute-start(f32[256,1792]{1,0:T(8,128)} %fusion.12), channel_id=1, source_target_pairs={{0,8},{8,0},{1,9},{9,1},{2,10},{10,2},{3,11},{11,3},{4,12},{12,4},... | collective-permute-start | bytes 5505032 | tf_op jit(solution)/shard_map/ppermute | solution.py:99
  279.5 42.0 %slice-start = ((s8[7340032]{0:T(1024)(128)(4,1)}), s8[3145728]{0:T(1024)(128)(4,1)S(1)}, s32[]{:S(2)}) async-start(s8[7340032]{0:T(1024)(128)(4,1)} %bitcast.23), calls=%async_computation.3 | async-start | bytes 6291456
  279.5 46.6 %all-to-all-start = ((bf16[256,8,512]{2,0,1:T(8,128)(2,1)}), bf16[256,8,512]{2,0,1:T(8,128)(2,1)}, u32[]{:S(2)}, u32[]{:S(2)}) async-start(bf16[256,8,512]{2,0,1:T(8,128)(2,1)} %copy.25), calls=%async_computation | async-start | bytes 4194304 | tf_op jit(solution)/shard_map/all_to_all | solution.py:95
  284.9 36.6 %slice-start.1 = ((s8[7340032]{0:T(1024)(128)(4,1)}), s8[4194304]{0:T(1024)(128)(4,1)S(1)}, s32[]{:S(2)}) async-start(s8[7340032]{0:T(1024)(128)(4,1)} %bitcast.23), calls=%async_computation.4 | async-start | bytes 8388608
  289.4 32.1 %copy-start.2 = (bf16[256,8,2,1,128]{0,4,2,1,3:T(8,128)(2,1)S(1)}, bf16[256,8,2,1,128]{0,4,2,1,3:T(8,128)(2,1)}, u32[]{:S(2)}) copy-start(bf16[256,8,2,1,128]{0,4,2,1,3:T(8,128)(2,1)} %copy-done.1) | copy-start | bytes 3145732
  289.5 31.2 %collective-permute-start.5 = (bf16[128,1792]{1,0:T(8,128)(2,1)S(1)}, bf16[128,1792]{1,0:T(8,128)(2,1)S(1)}, u32[]{:S(2)}, u32[]{:S(2)}) collective-permute-start(bf16[128,1792]{1,0:T(8,128)(2,1)S(1)} %slice.28), channel_id=1, source_target_pairs={{0,16},{16,0},{1,17},{17,1},{2,18},{18,2},{3,19},{19,3},{4,20},{20... | collective-permute-start | bytes 1376264 | tf_op jit(solution)/shard_map/ppermute | solution.py:77
Sparse Core Ops, SparseCore 0:
  38.6 198.0 all-gather.2

commit v11 on v9

--- a/solution.py
+++ b/solution.py
@@ -59,20 +59,25 @@
     gathered = lax.all_gather(gathered, "z", axis=0, tiled=True)
 
     scale = 1.0 / math.sqrt(tokens_here * n_sample)
+    yhi_major = jnp.concatenate([weighted_mine, weighted_recv], axis=0)
+    yhi_major = (
+        yhi_major.reshape(-1, n_z, n_yhi, rows_w).transpose(0, 2, 1, 3).reshape(-1, d_half)
+    )
     grad_part = (
         lax.dot_general(
-            jnp.concatenate([weighted_mine, weighted_recv], axis=0),
+            yhi_major,
             jnp.concatenate([hidden, hidden_recv], axis=0),
             (((0,), (0,)), ((), ())),
             preferred_element_type=jnp.float32,
         )
         * scale
     ).astype(jnp.bfloat16)
-    grad_part = lax.psum_scatter(grad_part, "z", scatter_dimension=0, tiled=True)
-    weight_grad = (
-        grad_part[:rows_w].astype(jnp.float32)
-        + lax.ppermute(grad_part[rows_w:], "yhi", swap).astype(jnp.float32)
+    half = grad_part.shape[0] // n_yhi
+    grad_part = (
+        grad_part[:half].astype(jnp.float32)
+        + lax.ppermute(grad_part[half:], "yhi", swap).astype(jnp.float32)
     ).astype(jnp.bfloat16)
+    weight_grad = lax.psum_scatter(grad_part, "z", scatter_dimension=0, tiled=True)
 
     def value_of(rows):
         return lax.dot_general(

time: 222 us -> 222 us (level)
  local copies, waits for them, and re-layouts: 16.6 us -> 19.7 us
  waiting for transfers between devices: 115 us -> 112 us
  other arithmetic: 13.9 us -> 16.3 us
    ppermute x1, waiting for transfers between devices: 3.35 us -> 80.6 us  [shards(): lax.ppermute(grad_part[half:], 'yhi', swap).astype(jnp.float32)]
    reduce_scatter x1, waiting for transfers between devices: 59.5 us -> 0.01 us  [shards(): lax.psum_scatter(grad_part, 'z', scatter_dimension=0, tiled=True)]
    all_gather x1, waiting for transfers between devices: 38 us -> 0.02 us  [shards(): gathered = lax.all_gather(gathered, 'z', axis=0, tiled=True)]
    all_to_all x1, waiting for transfers between devices: 0.01 us -> 18.6 us  [shards(): lax.all_to_all(partial_value, 'tensor', 1, 1, tiled=True)]
    ppermute x1, waiting for transfers between devices: 3.02 us -> 0.01 us  [shards(): hidden_recv = lax.ppermute(hidden, 'core', swap)]
    transpose x0 -> x1, local copies, waits for them, and re-layouts: none -> 2.82 us  [shards(): yhi_major.reshape(-1, n_z, n_yhi, rows_w).transpose(0, 2, 1, 3)]
  transfers between devices with their start and end apart: 9 -> 9, of which waited for: 5 -> 4; matrix products, arithmetic and copies ran while one was open for 24% -> 27% of each run, Pallas kernels for 0% -> 0%
where the time goes in v11:
time: 222 us; the launch traced here: 219 us
  waiting for transfers between devices  112 us (50%)
  matrix products  24.2 us (11%)
  blocking collectives  20.4 us (9%)
  local copies, waits for them, and re-layouts  19.7 us (9%)
  other arithmetic  16.3 us (7%)
  between operations  14.9 us (7%)
  starting transfers between devices  11.4 us (5%)
    ppermute x1, waiting for transfers between devices, shards(): lax.ppermute(grad_part[half:], 'yhi', swap).astype(jnp.float32)  80.6 us
    unnamed x1, blocking collectives  20.4 us
    all_to_all x1, waiting for transfers between devices, shards(): lax.all_to_all(partial_value, 'tensor', 1, 1, tiled=True)  18.6 us
    ppermute x1, waiting for transfers between devices, shards(): lax.ppermute(down_weight, 'yhi', swap)  10.8 us
    dot_general x2, matrix products, value_of(): lax.dot_general(rows, gathered, (((1,), (1,)), ((), ())), preferred_eleme...  7.72 us
    dot_general x1, matrix products, shards(): jnp.dot(weighted_mine, gathered, preferred_element_type=jnp.float32)  7.02 us
    dot_general x1, matrix products, shards(): lax.dot_general(yhi_major, jnp.concatenate([hidden, hidden_recv], axis=0)...  6.12 us
  transfers between devices with their start and end apart: 9, of which 4 were waited for; matrix products, arithmetic and copies ran while one was open for 27% of the time, Pallas kernels for 0%

profile of v11, /device:TPU:32, one launch (start us, length us, event | category | flops | bytes accessed | tf_op | source)
XLA Modules:
  0.0 219.1 jit_solution(4507022765664985431)
XLA Ops:
  7.3 3.3 %collective-permute-start = (bf16[128,1792]{1,0:T(8,128)(2,1)}, bf16[128,1792]{1,0:T(8,128)(2,1)S(1)}, u32[]{:S(2)}, u32[]{:S(2)}) collective-permute-start(bf16[128,1792]{1,0:T(8,128)(2,1)} %param.6), channel_id=1, source_target_pairs={{0,16},{16,0},{1,17},{17,1},{2,18},{18,2},{3,19},{19,3},{4,20},{20... | collective-permute-start | bytes 1376264 | tf_op jit(solution)/shard_map/ppermute | solution.py:58
  10.5 10.8 %collective-permute-done = bf16[128,1792]{1,0:T(8,128)(2,1)S(1)} collective-permute-done((bf16[128,1792]{1,0:T(8,128)(2,1)}, bf16[128,1792]{1,0:T(8,128)(2,1)S(1)}, u32[]{:S(2)}, u32[]{:S(2)}) %collective-permute-start) | collective-permute-done | bytes 458784 | tf_op jit(solution)/shard_map/ppermute | solution.py:58
  21.3 2.0 pad_maximum_fusion.1
  23.4 0.6 dynamic-slice
  24.8 20.4 %all-reduce = s32[256]{0:T(256)S(1)} all-reduce(s32[256]{0:T(256)S(1)} %add_dynamic-update-slice_fusion), channel_id=2, replica_groups=mesh['z'=8,'yhi'=2,'core'=2,'tensor'=8] {'z','yhi','core'}, use_global_device_ids=true, to_apply=%add | all-reduce | flops 256 | bytes 2048
  46.3 2.5 %copy.30 = bf16[256,4096]{0,1:T(8,128)(2,1)} copy(bf16[256,4096]{1,0:T(8,128)(2,1)S(1)} %copy-done.3) | data formatting | bytes 4194304 | tf_op args[2]
  48.8 2.0 multiply_convert_fusion.1
  50.9 3.1 %copy.32 = bf16[256,8,2,2,128]{4,1,3,2,0:T(8,128)(2,1)} copy(bf16[256,8,2,2,128]{0,4,3,2,1:T(8,128)(2,1)S(1)} %bitcast.29) | data formatting | bytes 4194304 | tf_op jit(solution)/shard_map/reshape | solution.py:50
  54.0 2.8 %reverse_select_fusion = bf16[256,8,2,2,128]{4,1,3,2,0:T(8,128)(2,1)S(1)} fusion(bf16[256,8,2,2,128]{4,1,3,2,0:T(8,128)(2,1)} %copy.32, pred[]{:T(512)S(6)} %eq.34), kind=kLoop, calls=%fused_computation.3 | loop fusion | flops 1048576 | bytes 4194305 | tf_op jit(solution)/shard_map/jit(_where)/select_n | solution.py:51
  57.2 0.8 copy.34
  58.1 0.5 collective-permute-start.1
  58.6 2.1 collective-permute-done.3
  60.7 1.8 copy.35
  62.6 1.4 maximum_bitcast_fusion
  64.0 2.8 %copy.36 = bf16[512,2,8,128]{0,3,2,1:T(8,128)(2,1)} copy(bf16[512,2,8,128]{3,2,1,0:T(8,128)(2,1)S(1)} %maximum_bitcast_fusion) | data formatting | bytes 4194304 | tf_op jit(solution)/shard_map/transpose | solution.py:64
  66.8 6.1 %multiply_convert_fusion = bf16[2048,1792]{1,0:T(8,128)(2,1)S(1)} fusion(bf16[512,2048]{0,1:T(8,128)(2,1)} %bitcast.35, bf16[256,1792]{1,0:T(8,128)(2,1)} %collective-permute-done.1, bf16[256,1792]{1,0:T(8,128)(2,1)} %param.5), kind=kOutput, calls=%fused_computation | convolution fusion | flops 3769106432 | bytes 11272192 | tf_op jit(solution)/shard_map/dot_general | solution.py:67
  73.2 2.6 %collective-permute-start.5 = (bf16[1024,1792]{1,0:T(8,128)(2,1)S(1)}, bf16[1024,1792]{1,0:T(8,128)(2,1)S(1)}, u32[]{:S(2)}, u32[]{:S(2)}) collective-permute-start(bf16[1024,1792]{1,0:T(8,128)(2,1)S(1)} %slice.19), channel_id=1, source_target_pairs={{0,16},{16,0},{1,17},{17,1},{2,18},{18,2},{3,19},{19,3},{4,20},{20... | collective-permute-start | bytes 11010056 | tf_op jit(solution)/shard_map/ppermute | solution.py:78
  75.8 80.6 %collective-permute-done.5 = bf16[1024,1792]{1,0:T(8,128)(2,1)S(1)} collective-permute-done((bf16[1024,1792]{1,0:T(8,128)(2,1)S(1)}, bf16[1024,1792]{1,0:T(8,128)(2,1)S(1)}, u32[]{:S(2)}, u32[]{:S(2)}) %collective-permute-start.5) | collective-permute-done | bytes 3670048 | tf_op jit(solution)/shard_map/ppermute | solution.py:78
  156.3 2.8 %add_convert_fusion = bf16[1024,1792]{1,0:T(8,128)(2,1)} fusion(bf16[1024,1792]{1,0:T(8,128)(2,1)S(1)} %collective-permute-done.5, bf16[2048,1792]{1,0:T(8,128)(2,1)S(1)} %multiply_convert_fusion), kind=kLoop, calls=%fused_computation.1 | loop fusion | flops 7340032 | bytes 11010048 | tf_op jit(solution)/shard_map/convert_element_type | solution.py:79
  159.2 5.5 %fusion.2 = bf16[256,2048]{0,1:T(8,128)(2,1)S(1)} fusion(bf16[2048,1792]{1,0:T(8,128)(2,1)} %all-gather.3.cloned.1.call-done, bf16[256,1792]{1,0:T(8,128)(2,1)} %collective-permute-done.1), kind=kOutput, calls=%fused_computation.11 | convolution fusion | flops 1879572480 | bytes 9306112 | tf_op jit(solution)/shard_map/dot_general | solution.py:83
  165.0 3.4 %fusion.8 = f32[256,1792]{1,0:T(8,128)} fusion(bf16[256,2048]{0,1:T(8,128)(2,1)S(1)} %copy-done.2, bf16[2048,1792]{1,0:T(8,128)(2,1)S(1)} %copy-done), kind=kOutput, calls=%fused_computation.31 | convolution fusion | flops 1879048192 | bytes 10223616 | tf_op jit(solution)/shard_map/dot_general | solution.py:98
  168.3 0.4 collective-permute-start.4
  168.7 2.2 %fusion.1 = bf16[256,1,2048]{0,2,1:T(8,128)(2,1)S(1)} fusion(bf16[2048,1792]{1,0:T(8,128)(2,1)S(1)} %copy-done, bf16[256,1792]{1,0:T(8,128)(2,1)S(1)} %copy-done.6), kind=kOutput, calls=%fused_computation.10 | convolution fusion | flops 1879572480 | bytes 9306112 | tf_op jit(solution)/shard_map/dot_general | solution.py:83
  171.1 0.5 reverse_select_fusion.2
  171.6 3.2 %copy.28 = bf16[256,2,8,2,128]{4,2,1,3,0:T(8,128)(2,1)} copy(bf16[256,2,8,2,128]{0,4,3,2,1:T(8,128)(2,1)S(1)} %bitcast.30) | data formatting | bytes 4194304 | tf_op jit(solution)/shard_map/reshape | solution.py:91
  174.8 2.8 %reverse_select_fusion.1 = bf16[256,8,2,2,128]{4,1,3,2,0:T(8,128)(2,1)S(1)} fusion(bf16[256,8,2,2,128]{4,1,3,2,0:T(8,128)(2,1)} %bitcast.31, pred[]{:T(512)S(6)} %eq.34), kind=kLoop, calls=%fused_computation.4 | loop fusion | flops 1048576 | bytes 4194305 | tf_op jit(solution)/shard_map/jit(_where)/select_n | solution.py:94
  177.6 2.0 copy.29
  179.6 4.4 %all-to-all-start = ((bf16[256,8,512]{2,0,1:T(8,128)(2,1)}), bf16[256,8,512]{2,0,1:T(8,128)(2,1)S(1)}, u32[]{:S(2)}, u32[]{:S(2)}) async-start(bf16[256,8,512]{2,0,1:T(8,128)(2,1)} %copy.29), calls=%async_computation | async-start | bytes 4194304 | tf_op jit(solution)/shard_map/all_to_all | solution.py:97
  184.0 1.6 copy.33
  185.6 7.0 %fusion = bf16[256,1792]{1,0:T(8,128)(2,1)} fusion(f32[256,1792]{1,0:T(8,128)} %collective-permute-done.4, bf16[256,2048]{0,1:T(8,128)(2,1)} %bitcast.34, bf16[2048,1792]{1,0:T(8,128)(2,1)} %all-gather.3.cloned.1.call-done), kind=kOutput, calls=%fused_computation.9 | convolution fusion | flops 1879965696 | bytes 11141120 | tf_op jit(solution)/shard_map/dot_general | solution.py:100
  192.6 18.6 %all-to-all-done = bf16[256,8,512]{2,0,1:T(8,128)(2,1)S(1)} async-done(((bf16[256,8,512]{2,0,1:T(8,128)(2,1)}), bf16[256,8,512]{2,0,1:T(8,128)(2,1)S(1)}, u32[]{:S(2)}, u32[]{:S(2)}) %all-to-all-start) | async-done | bytes 2097184 | tf_op jit(solution)/shard_map/all_to_all | solution.py:97
  211.2 1.0 reduce_sum.30
  (44 shorter events, 2.5 us)
Async XLA Ops:
  7.2 16.2 %copy-start.7 = (u32[256]{0:T(256)S(1)}, u32[256]{0:T(256)}, u32[]{:S(2)}) copy-start(u32[256]{0:T(256)} %constant.44) | copy-start | bytes 3076
  7.2 17.5 %copy-start.4 = (s32[4]{0:T(128)S(1)}, s32[4]{0:T(128)}, u32[]{:S(2)}) copy-start(s32[4]{0:T(128)} %param.9) | copy-start | bytes 52
  7.2 17.5 %copy-start.5 = (s32[4]{0:T(128)S(1)}, s32[4]{0:T(128)}, u32[]{:S(2)}) copy-start(s32[4]{0:T(128)} %param.8) | copy-start | bytes 52
  7.2 39.1 %copy-start.3 = (bf16[256,4096]{1,0:T(8,128)(2,1)S(1)}, bf16[256,4096]{1,0:T(8,128)(2,1)}, u32[]{:S(2)}) copy-start(bf16[256,4096]{1,0:T(8,128)(2,1)} %param.7) | copy-start | bytes 6291460
  7.2 152.0 %all-gather.3.cloned.1.call-start = ((), (), s32[]{:S(2)}) async-start(), calls=%async_computation.2 | async-start | bytes 8257536 | tf_op jit(solution)/shard_map/all_gather | solution.py:59
  7.3 14.1 %collective-permute-start = (bf16[128,1792]{1,0:T(8,128)(2,1)}, bf16[128,1792]{1,0:T(8,128)(2,1)S(1)}, u32[]{:S(2)}, u32[]{:S(2)}) collective-permute-start(bf16[128,1792]{1,0:T(8,128)(2,1)} %param.6), channel_id=1, source_target_pairs={{0,16},{16,0},{1,17},{17,1},{2,18},{18,2},{3,19},{19,3},{4,20},{20... | collective-permute-start | bytes 1376264 | tf_op jit(solution)/shard_map/ppermute | solution.py:58
  23.3 188.9 %reduce-scatter.2.cloned.1.call-start = ((), (), s32[]{:S(2)}) async-start(), calls=%async_computation.3 | async-start | bytes 4128768 | tf_op jit(solution)/shard_map/reduce_scatter | solution.py:80
  58.0 2.7 %collective-permute-start.3 = (bf16[256,2048]{0,1:T(8,128)(2,1)S(1)}, bf16[256,2048]{0,1:T(8,128)(2,1)S(1)}, u32[]{:S(2)}, u32[]{:S(2)}) collective-permute-start(bf16[256,2048]{0,1:T(8,128)(2,1)S(1)} %bitcast.36), channel_id=1, source_target_pairs={{0,8},{8,0},{1,9},{9,1},{2,10},{10,2},{3,11},{11,3},{4,12},{12,4},... | collective-permute-start | bytes 3145736 | tf_op jit(solution)/shard_map/ppermute | solution.py:55
  58.1 8.7 %collective-permute-start.1 = (bf16[256,1792]{1,0:T(8,128)(2,1)}, bf16[256,1792]{1,0:T(8,128)(2,1)}, u32[]{:S(2)}, u32[]{:S(2)}) collective-permute-start(bf16[256,1792]{1,0:T(8,128)(2,1)} %param.5), channel_id=1, source_target_pairs={{0,8},{8,0},{1,9},{9,1},{2,10},{10,2},{3,11},{11,3},{4,12},{12,4},... | collective-permute-start | bytes 2752520 | tf_op jit(solution)/shard_map/ppermute | solution.py:56
  60.7 1.8 copy-start.1
  73.2 83.2 %collective-permute-start.5 = (bf16[1024,1792]{1,0:T(8,128)(2,1)S(1)}, bf16[1024,1792]{1,0:T(8,128)(2,1)S(1)}, u32[]{:S(2)}, u32[]{:S(2)}) collective-permute-start(bf16[1024,1792]{1,0:T(8,128)(2,1)S(1)} %slice.19), channel_id=1, source_target_pairs={{0,16},{16,0},{1,17},{17,1},{2,18},{18,2},{3,19},{19,3},{4,20},{20... | collective-permute-start | bytes 11010056 | tf_op jit(solution)/shard_map/ppermute | solution.py:78
  159.2 5.7 %copy-start.2 = (bf16[256,2048]{0,1:T(8,128)(2,1)S(1)}, bf16[256,2048]{0,1:T(8,128)(2,1)}, u32[]{:S(2)}) copy-start(bf16[256,2048]{0,1:T(8,128)(2,1)} %copy-done.1) | copy-start | bytes 3145732
  159.2 5.7 %copy-start = (bf16[2048,1792]{1,0:T(8,128)(2,1)S(1)}, bf16[2048,1792]{1,0:T(8,128)(2,1)}, u32[]{:S(2)}) copy-start(bf16[2048,1792]{1,0:T(8,128)(2,1)} %all-gather.3.cloned.1.call-done) | copy-start | bytes 22020100
  164.8 4.0 %copy-start.6 = (bf16[256,1792]{1,0:T(8,128)(2,1)S(1)}, bf16[256,1792]{1,0:T(8,128)(2,1)}, u32[]{:S(2)}) copy-start(bf16[256,1792]{1,0:T(8,128)(2,1)} %param.5) | copy-start | bytes 2752516
  164.8 6.2 %collective-permute-start.2 = (bf16[256,2048]{0,1:T(8,128)(2,1)S(1)}, bf16[256,2048]{0,1:T(8,128)(2,1)S(1)}, u32[]{:S(2)}, u32[]{:S(2)}) collective-permute-start(bf16[256,2048]{0,1:T(8,128)(2,1)S(1)} %fusion.2), channel_id=1, source_target_pairs={{0,8},{8,0},{1,9},{9,1},{2,10},{10,2},{3,11},{11,3},{4,12},{12,4},... | collective-permute-start | bytes 3145736 | tf_op jit(solution)/shard_map/ppermute | solution.py:88
  168.3 17.3 %collective-permute-start.4 = (f32[256,1792]{1,0:T(8,128)}, f32[256,1792]{1,0:T(8,128)}, u32[]{:S(2)}, u32[]{:S(2)}) collective-permute-start(f32[256,1792]{1,0:T(8,128)} %fusion.8), channel_id=1, source_target_pairs={{0,8},{8,0},{1,9},{9,1},{2,10},{10,2},{3,11},{11,3},{4,12},{12,4},... | collective-permute-start | bytes 5505032 | tf_op jit(solution)/shard_map/ppermute | solution.py:101
  179.6 31.6 %all-to-all-start = ((bf16[256,8,512]{2,0,1:T(8,128)(2,1)}), bf16[256,8,512]{2,0,1:T(8,128)(2,1)S(1)}, u32[]{:S(2)}, u32[]{:S(2)}) async-start(bf16[256,8,512]{2,0,1:T(8,128)(2,1)} %copy.29), calls=%async_computation | async-start | bytes 4194304 | tf_op jit(solution)/shard_map/all_to_all | solution.py:97
Sparse Core Ops, SparseCore 0:
  23.5 85.1 all-gather.2
  159.3 46.2 reduce-scatter.1
